TPU v7x, 128 devices: a whole 4x4x4 slice. The times are simulated.
128 devices in a mesh: group: 2 (over core), member: 64 (over x, z, y).
Axes of the slice: x: 4, y: 4, z: 4, core: 2. Of those that a mesh axis runs over, the one named last changes fastest.
Arguments:
- features: bfloat16 [262144, 256], P(('group', 'member')), may hold values from -6 to 6
- local_home: int32 [8192], P(('group', 'member')), may hold values from 0 to 15
- local_near: int32 [8192], P(('group', 'member')), may hold values from 0 to 15
- local_tiles: bfloat16 [8192, 128, 128], P(('group', 'member')), may hold values from -0.125 to 0.125
- remote_home: int32 [8192], P(('group', 'member')), may hold values from 0 to 15
- remote_far: int32 [8192], P(('group', 'member')), may hold values from 0 to 2047, as said below
- remote_tiles: bfloat16 [8192, 128, 128], P(('group', 'member')), may hold values from -0.125 to 0.125
- weight: bfloat16 [512, 256], replicated, may hold values from -0.25 to 0.25
- cotangent: bfloat16 [262144, 256], P(('group', 'member')), may hold values from -6 to 6
Outputs:
- output: bfloat16 [262144, 256], P(('group', 'member'))
- grad_weight: float32 [512, 256], replicated
- grad_features: float32 [262144, 256], P(('group', 'member'))
Inputs may be any that keep to these rules, and one draw needn't show every extreme that they name: `remote_far`: the remote pairs of one owner name partner blocks on 64 different owners other than itself, one block from each owner; one owner, drawn from the seed, holds a partner block of every other owner's remote pairs.
All inputs are finite; a program needn't handle non-finite values.
Results may differ from a plain program's by a relative error of at most 0.0057.
Values may be sent and summed in bfloat16 or wider, within the bound.
No kernel may reach another device: no remote copies, remote signals or barrier semaphores. Data moves between devices by JAX's collectives and lax.ppermute only.
A program may use at most 192 MiB of HBM per device.

v0:
```python
import math

import jax
import jax.numpy as jnp
from jax import lax
from jax.sharding import PartitionSpec as P

F = 256
BLOCK = 128
BLK_DEV = 16


def spread(index_list, count, dtype):
    return (index_list[:, None] == jnp.arange(count, dtype=jnp.int32)[None, :]).astype(dtype)


def carry_blocks(buffer):
    return lax.all_to_all(buffer, ("group", "member"), split_axis=0, concat_axis=0, tiled=True)


def return_blocks(buffer):
    return lax.all_to_all(buffer, ("group", "member"), split_axis=0, concat_axis=0, tiled=True)


def body(
    features,
    local_home,
    local_near,
    local_tiles,
    remote_home,
    remote_far,
    remote_tiles,
    weight,
    cotangent,
):
    device_count = lax.axis_size(("group", "member"))
    row_count = features.shape[0]
    own_blocks = row_count // BLOCK
    target_dev = remote_far // BLK_DEV
    wanted = remote_far % BLK_DEV
    request = jnp.full((device_count,), -1, jnp.int32).at[target_dev].set(wanted)
    asked = lax.all_to_all(request, ("group", "member"), split_axis=0, concat_axis=0, tiled=True)
    picked = jnp.clip(asked, 0, own_blocks - 1)
    back_hot = spread(asked, own_blocks, jnp.bfloat16)
    segment_ids = jnp.concatenate([local_home, local_near, remote_home])

    def apply_graph(blocks_in):
        outgoing = blocks_in[picked]
        arrived = carry_blocks(outgoing)
        to_far = jnp.einsum(
            "pba,pbf->paf", remote_tiles, blocks_in[remote_home], preferred_element_type=jnp.float32
        ).astype(jnp.bfloat16)
        send_back = jnp.zeros((device_count, BLOCK, F), jnp.bfloat16).at[target_dev].set(to_far)
        returned = return_blocks(send_back)
        to_home = jnp.einsum(
            "pab,pbf->paf", local_tiles, blocks_in[local_near], preferred_element_type=jnp.float32
        )
        to_near = jnp.einsum(
            "pba,pbf->paf", local_tiles, blocks_in[local_home], preferred_element_type=jnp.float32
        )
        far_vals = arrived[target_dev]
        to_home_r = jnp.einsum(
            "pab,pbf->paf", remote_tiles, far_vals, preferred_element_type=jnp.float32
        )
        products = jnp.concatenate([to_home, to_near, to_home_r], axis=0)
        total = jax.ops.segment_sum(products, segment_ids, num_segments=own_blocks)
        total = total + jnp.einsum(
            "sk,saf->kaf", back_hot, returned, preferred_element_type=jnp.float32
        )
        return total.reshape(row_count, F)

    aggregate = apply_graph(features.reshape(own_blocks, BLOCK, F)).astype(jnp.bfloat16)
    joined = jnp.concatenate([features, aggregate], axis=1)
    pre_act = jnp.dot(joined, weight, preferred_element_type=jnp.float32)
    sigmoid_z = jax.nn.sigmoid(pre_act)
    output = (pre_act * sigmoid_z).astype(jnp.bfloat16)
    grad_pre = (
        cotangent.astype(jnp.float32) * sigmoid_z * (1.0 + pre_act * (1.0 - sigmoid_z))
    ).astype(jnp.bfloat16)
    partial_grad = jnp.einsum("ra,rf->af", joined, grad_pre, preferred_element_type=jnp.float32)
    grad_scale = 1.0 / math.sqrt(row_count * device_count)
    grad_weight = lax.psum(partial_grad, ("group", "member")) * grad_scale
    grad_joined = jnp.einsum("rf,af->ra", grad_pre, weight, preferred_element_type=jnp.float32)
    grad_agg = grad_joined[:, F:].astype(jnp.bfloat16).reshape(own_blocks, BLOCK, F)
    grad_features = grad_joined[:, :F] + apply_graph(grad_agg)
    return (output, grad_weight, grad_features)


def solution(mesh):
    in_specs = (
        P(("group", "member"), None),
        P(("group", "member")),
        P(("group", "member")),
        P(("group", "member"), None, None),
        P(("group", "member")),
        P(("group", "member")),
        P(("group", "member"), None, None),
        P(),
        P(("group", "member"), None),
    )
    out_specs = (P(("group", "member"), None), P(), P(("group", "member"), None))
    return jax.shard_map(body, mesh=mesh, in_specs=in_specs, out_specs=out_specs, check_vma=False)
```

profile of v0, /device:TPU:41, one launch (start us, length us, event | category | flops | bytes accessed | tf_op | source)
XLA Modules:
  0.0 953.0 jit_solution(5109169967945188336)
XLA Ops:
  9.5 10.5 %all-to-all-start = ((s32[128,1,1]{2,1,0:T(1,128)}), s32[128,1,1]{2,1,0:T(1,128)S(1)}, u32[]{:S(2)}, u32[]{:S(2)}) async-start(s32[128,1,1]{2,1,0:T(1,128)} %copy.50), calls=%async_computation | async-start | bytes 131072 | tf_op jit(solution)/shard_map/all_to_all | solution.py:42
  20.7 4.0 gather_fusion
  24.6 6.1 convert_bitcast_fusion.1
  30.8 6.4 copy.52
  37.1 4.3 broadcast.61.clone
  41.4 12.1 %scatter_fusion = bf16[128,128,256]{2,1,0:T(8,128)(2,1)} fusion(bf16[128,128,256]{2,1,0:T(8,128)(2,1)} %broadcast.61.clone, s32[64]{0:T(128)S(1)} %get-tuple-element.8, bf16[64,128,256]{2,1,0:T(8,128)(2,1)} %copy.52), kind=kCustom, calls=%fused_computation.11 | custom fusion | bytes 12583168 | tf_op jit(solution)/shard_map/scatter | solution.py:53
  53.6 10.1 %all-to-all-start.1 = ((bf16[128,128,256]{2,1,0:T(8,128)(2,1)}), bf16[128,128,256]{2,1,0:T(8,128)(2,1)}, u32[]{:S(2)}, u32[]{:S(2)}) async-start(bf16[128,128,256]{2,1,0:T(8,128)(2,1)} %scatter_fusion), calls=%async_computation.1 | async-start | bytes 16777216 | tf_op jit(solution)/shard_map/all_to_all | solution.py:22
  63.7 4.6 clamp_reduce_fusion
  68.4 6.5 gather_fusion.3
  74.9 104.7 %all-to-all-done.1 = bf16[128,128,256]{2,1,0:T(8,128)(2,1)} async-done(((bf16[128,128,256]{2,1,0:T(8,128)(2,1)}), bf16[128,128,256]{2,1,0:T(8,128)(2,1)}, u32[]{:S(2)}, u32[]{:S(2)}) %all-to-all-start.1) | async-done | bytes 8388640 | tf_op jit(solution)/shard_map/all_to_all | solution.py:22
  179.6 10.9 %all-to-all-start.2 = ((bf16[128,128,256]{2,1,0:T(8,128)(2,1)}), bf16[128,128,256]{2,1,0:T(8,128)(2,1)}, u32[]{:S(2)}, u32[]{:S(2)}) async-start(bf16[128,128,256]{2,1,0:T(8,128)(2,1)} %gather_fusion.3), calls=%async_computation.2 | async-start | bytes 16777216 | tf_op jit(solution)/shard_map/all_to_all | solution.py:18
  190.5 2.9 gather_fusion.2
  193.4 2.8 gather_fusion.1
  196.3 6.9 convolution_bitcast_fusion.4
  203.2 4.5 convolution_bitcast_fusion.5
  207.7 7.9 fusion.2
  215.6 2.5 copy.57
  218.1 87.4 %all-to-all-done.2 = bf16[128,128,256]{2,1,0:T(8,128)(2,1)} async-done(((bf16[128,128,256]{2,1,0:T(8,128)(2,1)}), bf16[128,128,256]{2,1,0:T(8,128)(2,1)}, u32[]{:S(2)}, u32[]{:S(2)}) %all-to-all-start.2) | async-done | bytes 8388640 | tf_op jit(solution)/shard_map/all_to_all | solution.py:18
  305.5 6.1 gather_fusion.4
  311.7 4.2 convolution_bitcast_fusion.3
  315.8 15.8 %pad_maximum_fusion = f32[192,128,256]{1,2,0:T(8,128)} fusion(f32[64,128,256]{1,2,0:T(8,128)S(1)} %convolution_bitcast_fusion.3, f32[64,128,256]{1,2,0:T(8,128)} %convolution_bitcast_fusion.4, f32[64,128,256]{1,2,0:T(8,128)} %convolution_bitcast_fusion.5), kind=kLoop, calls=%fused_computation.15 | loop fusion | flops 12582912 | bytes 50331648 | tf_op jit(solution)/shard_map/concatenate | solution.py:65
  331.6 24.6 %copy.58 = f32[192,128,256]{2,1,0:T(8,128)} copy(f32[192,128,256]{1,2,0:T(8,128)} %pad_maximum_fusion) | data formatting | bytes 50331648 | tf_op jit(solution)/shard_map/concatenate | solution.py:65
  356.2 55.2 %scatter_fusion.1 = f32[16,128,256]{2,1,0:T(8,128)} fusion(f32[16,128,256]{2,1,0:T(8,128)} %copy.57, s32[192]{0:T(256)S(1)} %pad_add_fusion, f32[192,128,256]{2,1,0:T(8,128)} %copy.58), kind=kCustom, calls=%fused_computation.12 | custom fusion | flops 6291456 | bytes 75498240 | tf_op jit(solution)/shard_map/scatter-add | solution.py:66
  413.2 3.9 multiply_convert_fusion
  418.0 2.0 copy-done.2
  420.2 2.8 gather_fusion.5
  423.0 6.1 convert_bitcast_fusion
  429.1 6.4 copy.60
  435.5 4.3 broadcast.61
  439.8 12.0 %scatter_fusion.2 = bf16[128,128,256]{2,1,0:T(8,128)(2,1)} fusion(bf16[128,128,256]{2,1,0:T(8,128)(2,1)} %broadcast.61, s32[64]{0:T(128)S(1)} %get-tuple-element.8, bf16[64,128,256]{2,1,0:T(8,128)(2,1)} %copy.60), kind=kCustom, calls=%fused_computation.13 | custom fusion | bytes 12583168 | tf_op jit(solution)/shard_map/scatter | solution.py:53
  451.8 10.6 %all-to-all-start.3 = ((bf16[128,128,256]{2,1,0:T(8,128)(2,1)}), bf16[128,128,256]{2,1,0:T(8,128)(2,1)}, u32[]{:S(2)}, u32[]{:S(2)}) async-start(bf16[128,128,256]{2,1,0:T(8,128)(2,1)} %scatter_fusion.2), calls=%async_computation.3 | async-start | bytes 16777216 | tf_op jit(solution)/shard_map/all_to_all | solution.py:22
  462.4 6.5 gather_fusion.8
  468.9 109.4 %all-to-all-done.3 = bf16[128,128,256]{2,1,0:T(8,128)(2,1)} async-done(((bf16[128,128,256]{2,1,0:T(8,128)(2,1)}), bf16[128,128,256]{2,1,0:T(8,128)(2,1)}, u32[]{:S(2)}, u32[]{:S(2)}) %all-to-all-start.3) | async-done | bytes 8388640 | tf_op jit(solution)/shard_map/all_to_all | solution.py:22
  578.2 10.6 %all-to-all-start.4 = ((bf16[128,128,256]{2,1,0:T(8,128)(2,1)}), bf16[128,128,256]{2,1,0:T(8,128)(2,1)}, u32[]{:S(2)}, u32[]{:S(2)}) async-start(bf16[128,128,256]{2,1,0:T(8,128)(2,1)} %gather_fusion.8), calls=%async_computation.4 | async-start | bytes 16777216 | tf_op jit(solution)/shard_map/all_to_all | solution.py:18
  589.1 2.9 gather_fusion.7
  592.0 2.8 gather_fusion.6
  594.7 3.4 fusion.4
  598.2 6.9 convolution_bitcast_fusion.1
  605.0 4.5 convolution_bitcast_fusion.2
  609.6 214.2 %all-reduce.2.cloned.1.call-done = f32[512,256]{1,0:T(8,128)} async-done(((f32[512,256]{1,0:T(8,128)}), f32[512,256]{1,0:T(8,128)}) %all-reduce.2.cloned.1.call-update) | async-done | bytes 524304 | tf_op jit(solution)/shard_map/psum | solution.py:82
  825.6 7.9 fusion
  833.5 2.5 copy.65
  836.0 6.1 gather_fusion.9
  842.2 4.2 convolution_bitcast_fusion
  846.3 15.8 %pad_maximum_fusion.1 = f32[192,128,256]{1,2,0:T(8,128)} fusion(f32[64,128,256]{1,2,0:T(8,128)S(1)} %convolution_bitcast_fusion, f32[64,128,256]{1,2,0:T(8,128)} %convolution_bitcast_fusion.1, f32[64,128,256]{1,2,0:T(8,128)} %convolution_bitcast_fusion.2), kind=kLoop, calls=%fused_computation.16 | loop fusion | flops 12582912 | bytes 50331648 | tf_op jit(solution)/shard_map/concatenate | solution.py:65
  862.1 24.6 %copy.66 = f32[192,128,256]{2,1,0:T(8,128)} copy(f32[192,128,256]{1,2,0:T(8,128)} %pad_maximum_fusion.1) | data formatting | bytes 50331648 | tf_op jit(solution)/shard_map/concatenate | solution.py:65
  886.7 55.2 %scatter_fusion.3 = f32[16,128,256]{2,1,0:T(8,128)} fusion(f32[16,128,256]{2,1,0:T(8,128)} %copy.65, s32[192]{0:T(256)S(1)} %pad_add_fusion, f32[192,128,256]{2,1,0:T(8,128)} %copy.66), kind=kCustom, calls=%fused_computation.14 | custom fusion | flops 6291456 | bytes 75498240 | tf_op jit(solution)/shard_map/scatter-add | solution.py:66
  941.9 3.8 slice_add_fusion
  (42 shorter events, 8.2 us)
Async XLA Ops:
  7.2 189.1 %copy-start = (bf16[64,128,128]{2,1,0:T(8,128)(2,1)S(1)}, bf16[64,128,128]{2,1,0:T(8,128)(2,1)}, u32[]{:S(2)}) copy-start(bf16[64,128,128]{2,1,0:T(8,128)(2,1)} %param.12) | copy-start | bytes 6291460
  9.5 44.0 %all-to-all-start = ((s32[128,1,1]{2,1,0:T(1,128)}), s32[128,1,1]{2,1,0:T(1,128)S(1)}, u32[]{:S(2)}, u32[]{:S(2)}) async-start(s32[128,1,1]{2,1,0:T(1,128)} %copy.50), calls=%async_computation | async-start | bytes 131072 | tf_op jit(solution)/shard_map/all_to_all | solution.py:42
  53.6 14.8 %copy-start.1 = (bf16[2048,256]{1,0:T(8,128)(2,1)S(1)}, bf16[2048,256]{1,0:T(8,128)(2,1)}, u32[]{:S(2)}) copy-start(bf16[2048,256]{1,0:T(8,128)(2,1)} %param.9) | copy-start | bytes 3145732
  53.6 126.0 %all-to-all-start.1 = ((bf16[128,128,256]{2,1,0:T(8,128)(2,1)}), bf16[128,128,256]{2,1,0:T(8,128)(2,1)}, u32[]{:S(2)}, u32[]{:S(2)}) async-start(bf16[128,128,256]{2,1,0:T(8,128)(2,1)} %scatter_fusion), calls=%async_computation.1 | async-start | bytes 16777216 | tf_op jit(solution)/shard_map/all_to_all | solution.py:22
  74.9 115.6 %copy-start.10 = (s32[64]{0:T(128)S(1)}, s32[64]{0:T(128)}, u32[]{:S(2)}) copy-start(s32[64]{0:T(128)} %param.10) | copy-start | bytes 772
  179.6 126.0 %all-to-all-start.2 = ((bf16[128,128,256]{2,1,0:T(8,128)(2,1)}), bf16[128,128,256]{2,1,0:T(8,128)(2,1)}, u32[]{:S(2)}, u32[]{:S(2)}) async-start(bf16[128,128,256]{2,1,0:T(8,128)(2,1)} %gather_fusion.3), calls=%async_computation.2 | async-start | bytes 16777216 | tf_op jit(solution)/shard_map/all_to_all | solution.py:18
  190.5 2.9 copy-start.9
  193.4 2.8 copy-start.8
  196.3 6.9 copy-start.4
  356.2 56.9 %copy-start.7 = (bf16[512,256]{1,0:T(8,128)(2,1)S(1)}, bf16[512,256]{1,0:T(8,128)(2,1)}, u32[]{:S(2)}) copy-start(bf16[512,256]{1,0:T(8,128)(2,1)} %param.16) | copy-start | bytes 786436
  413.2 3.9 copy-start.6
  417.1 1.0 copy-start.5
  418.0 2.0 copy-start.2
  451.8 126.5 %all-to-all-start.3 = ((bf16[128,128,256]{2,1,0:T(8,128)(2,1)}), bf16[128,128,256]{2,1,0:T(8,128)(2,1)}, u32[]{:S(2)}, u32[]{:S(2)}) async-start(bf16[128,128,256]{2,1,0:T(8,128)(2,1)} %scatter_fusion.2), calls=%async_computation.3 | async-start | bytes 16777216 | tf_op jit(solution)/shard_map/all_to_all | solution.py:22
  578.2 257.8 %all-to-all-start.4 = ((bf16[128,128,256]{2,1,0:T(8,128)(2,1)}), bf16[128,128,256]{2,1,0:T(8,128)(2,1)}, u32[]{:S(2)}, u32[]{:S(2)}) async-start(bf16[128,128,256]{2,1,0:T(8,128)(2,1)} %gather_fusion.8), calls=%async_computation.4 | async-start | bytes 16777216 | tf_op jit(solution)/shard_map/all_to_all | solution.py:18
  588.8 234.9 %all-reduce.2.cloned.1.call-start = ((), (), s32[]{:S(2)}) async-start(), calls=%async_computation.5 | async-start | bytes 1048576 | tf_op jit(solution)/shard_map/psum | solution.py:82
  598.2 6.9 copy-start.3
Sparse Core Ops, SparseCore 0:
  598.3 225.3 all-reduce.1
where the time goes:
time: 966 us; the launch traced here: 953 us
  waiting for transfers between devices  516 us (53%)
  other arithmetic  156 us (16%)
  local copies, waits for them, and re-layouts  147 us (15%)
  matrix products  67.2 us (7%)
  starting transfers between devices  52.9 us (5%)
  between operations  14.7 us (2%)
    psum x1, waiting for transfers between devices, body(): grad_weight = lax.psum(partial_grad, ('group', 'member')) * grad_scale  214 us
    all_to_all x2, waiting for transfers between devices, return_blocks(): lax.all_to_all(buffer, ('group', 'member'), split_axis=0, concat_axis=0,...  214 us
    scatter-add x2, other arithmetic, apply_graph(): total = jax.ops.segment_sum(products, segment_ids, num_segments=own_blocks)  110 us
    all_to_all x2, waiting for transfers between devices, carry_blocks(): lax.all_to_all(buffer, ('group', 'member'), split_axis=0, concat_axis=0,...  87.4 us
    concatenate x2, local copies, waits for them, and re-layouts, apply_graph(): products = jnp.concatenate([to_home, to_near, to_home_r], axis=0)  49.3 us
    concatenate x2, other arithmetic, apply_graph(): products = jnp.concatenate([to_home, to_near, to_home_r], axis=0)  31.5 us
    scatter x2, local copies, waits for them, and re-layouts, apply_graph(): jnp.zeros((device_count, BLOCK, F), jnp.bfloat16).at[target_dev].set(to_far)  24.1 us
    all_to_all x2, starting transfers between devices, carry_blocks(): lax.all_to_all(buffer, ('group', 'member'), split_axis=0, concat_axis=0,...  21.5 us
  transfers between devices with their start and end apart: 6, of which 4 were waited for; matrix products, arithmetic and copies ran while one was open for 12% of the time, Pallas kernels for 0%

commit v1 on v0

v1 whole, which is shorter than its diff:
```python
import math

import jax
import jax.numpy as jnp
from jax import lax
from jax.experimental import pallas as pl
from jax.experimental.pallas import tpu as pltpu
from jax.sharding import PartitionSpec as P

F = 256
BLOCK = 128
BLK_DEV = 16
AXES = ("group", "member")
VMEM_LIMIT = 56 * 1024 * 1024


def _smem():
    return pl.BlockSpec(memory_space=pltpu.SMEM)


def _vmem():
    return pl.BlockSpec(memory_space=pltpu.VMEM)


def _dot_t(a, v):
    return lax.dot_general(a, v, (((0,), (0,)), ((), ())), preferred_element_type=jnp.float32)


def _send_kernel(picked_ref, rhome_ref, tdev_ref, x_ref, rt_ref, send_ref):
    slots = send_ref.shape[0]
    pairs = rt_ref.shape[0]

    def fill(t, c):
        send_ref[t, 0] = x_ref[picked_ref[t]]
        send_ref[t, 1] = jnp.zeros((BLOCK, F), send_ref.dtype)
        return c

    lax.fori_loop(0, slots, fill, 0)

    def term(p, c):
        r = _dot_t(rt_ref[p], x_ref[rhome_ref[p]])
        send_ref[tdev_ref[p], 1] = r.astype(send_ref.dtype)
        return c

    lax.fori_loop(0, pairs, term, 0)


def build_send(picked, rhome, tdev, x, rtiles):
    slots = picked.shape[0]
    return pl.pallas_call(
        _send_kernel,
        out_shape=jax.ShapeDtypeStruct((slots, 2, BLOCK, F), jnp.bfloat16),
        in_specs=[_smem(), _smem(), _smem(), _vmem(), _vmem()],
        out_specs=_vmem(),
        compiler_params=pltpu.CompilerParams(vmem_limit_bytes=VMEM_LIMIT),
    )(picked, rhome, tdev, x, rtiles)


def _gather_kernel(lhome_ref, lnear_ref, rhome_ref, tdev_ref, picked_ref, valid_ref,
                   x_ref, lt_ref, rt_ref, recv_ref, init_ref, out_ref):
    out_ref[...] = init_ref[...]
    n_local = lt_ref.shape[0]
    n_remote = rt_ref.shape[0]
    slots = recv_ref.shape[0]

    def local(p, c):
        h = lhome_ref[p]
        n = lnear_ref[p]
        a = lt_ref[p]
        out_ref[h] += jnp.dot(a, x_ref[n], preferred_element_type=jnp.float32)
        out_ref[n] += _dot_t(a, x_ref[h])
        return c

    lax.fori_loop(0, n_local, local, 0)

    def remote(p, c):
        h = rhome_ref[p]
        out_ref[h] += jnp.dot(rt_ref[p], recv_ref[tdev_ref[p], 0], preferred_element_type=jnp.float32)
        return c

    lax.fori_loop(0, n_remote, remote, 0)

    def back(s, c):
        @pl.when(valid_ref[s] > 0)
        def _():
            k = picked_ref[s]
            out_ref[k] += recv_ref[s, 1].astype(jnp.float32)
        return c

    lax.fori_loop(0, slots, back, 0)


def gather_sum(lhome, lnear, rhome, tdev, picked, valid, x, ltiles, rtiles, recv, init):
    return pl.pallas_call(
        _gather_kernel,
        out_shape=jax.ShapeDtypeStruct(init.shape, jnp.float32),
        in_specs=[_smem()] * 6 + [_vmem()] * 5,
        out_specs=_vmem(),
        compiler_params=pltpu.CompilerParams(vmem_limit_bytes=VMEM_LIMIT),
    )(lhome, lnear, rhome, tdev, picked, valid, x, ltiles, rtiles, recv, init)


def body(
    features,
    local_home,
    local_near,
    local_tiles,
    remote_home,
    remote_far,
    remote_tiles,
    weight,
    cotangent,
):
    device_count = lax.axis_size(AXES)
    row_count = features.shape[0]
    own_blocks = row_count // BLOCK
    lhome = jnp.clip(local_home, 0, own_blocks - 1)
    lnear = jnp.clip(local_near, 0, own_blocks - 1)
    rhome = jnp.clip(remote_home, 0, own_blocks - 1)
    target_dev = jnp.clip(remote_far // BLK_DEV, 0, device_count - 1)
    wanted = remote_far % BLK_DEV
    request = jnp.full((device_count,), -1, jnp.int32).at[target_dev].set(wanted)
    asked = lax.all_to_all(request, AXES, split_axis=0, concat_axis=0, tiled=True)
    picked = jnp.clip(asked, 0, own_blocks - 1)
    valid = (asked >= 0).astype(jnp.int32)

    def apply_graph(blocks_in, init):
        send = build_send(picked, rhome, target_dev, blocks_in, remote_tiles)
        recv = lax.all_to_all(send, AXES, split_axis=0, concat_axis=0, tiled=True)
        total = gather_sum(lhome, lnear, rhome, target_dev, picked, valid,
                           blocks_in, local_tiles, remote_tiles, recv, init)
        return total.reshape(row_count, F)

    zeros = jnp.zeros((own_blocks, BLOCK, F), jnp.float32)
    aggregate = apply_graph(features.reshape(own_blocks, BLOCK, F), zeros).astype(jnp.bfloat16)
    joined = jnp.concatenate([features, aggregate], axis=1)
    pre_act = jnp.dot(joined, weight, preferred_element_type=jnp.float32)
    sigmoid_z = jax.nn.sigmoid(pre_act)
    output = (pre_act * sigmoid_z).astype(jnp.bfloat16)
    grad_pre = (
        cotangent.astype(jnp.float32) * sigmoid_z * (1.0 + pre_act * (1.0 - sigmoid_z))
    ).astype(jnp.bfloat16)
    partial_grad = jnp.einsum("ra,rf->af", joined, grad_pre, preferred_element_type=jnp.float32)
    rows = partial_grad.shape[0]
    chunk = rows // device_count
    pieces = lax.all_to_all(
        partial_grad.reshape(device_count, chunk, F), AXES, split_axis=0, concat_axis=0, tiled=True
    )
    mine = pieces.sum(axis=0)
    spread_out = jnp.broadcast_to(mine[None], (device_count, chunk, F))
    gathered = lax.all_to_all(spread_out, AXES, split_axis=0, concat_axis=0, tiled=True)
    grad_scale = 1.0 / math.sqrt(row_count * device_count)
    grad_weight = gathered.reshape(rows, F) * grad_scale
    grad_joined = jnp.einsum("rf,af->ra", grad_pre, weight, preferred_element_type=jnp.float32)
    grad_agg = grad_joined[:, F:].astype(jnp.bfloat16).reshape(own_blocks, BLOCK, F)
    init_b = grad_joined[:, :F].reshape(own_blocks, BLOCK, F)
    grad_features = apply_graph(grad_agg, init_b)
    return (output, grad_weight, grad_features)


def solution(mesh):
    in_specs = (
        P(AXES, None),
        P(AXES),
        P(AXES),
        P(AXES, None, None),
        P(AXES),
        P(AXES),
        P(AXES, None, None),
        P(),
        P(AXES, None),
    )
    out_specs = (P(AXES, None), P(), P(AXES, None))
    return jax.shard_map(body, mesh=mesh, in_specs=in_specs, out_specs=out_specs, check_vma=False)
```

time: 966 us -> 738 us (0.76); the launches traced: 953 us -> 738 us
  other arithmetic: 156 us -> 10.3 us
  local copies, waits for them, and re-layouts: 147 us -> 11.6 us
  Pallas kernels: 0 us -> 112 us
  matrix products: 67.2 us -> 3.78 us
  waiting for transfers between devices: 516 us -> 549 us
  starting transfers between devices: 52.9 us -> 35.5 us
  blocking collectives: 0 us -> 15.1 us
  between operations: 14.7 us -> 0.76 us
    all_to_all x5 -> x4, waiting for transfers between devices: 301 us -> 549 us  [the longest x2 542 us: apply_graph(): recv = lax.all_to_all(send, AXES, split_axis=0, concat_axis=0, tiled=True)]
    psum x1 -> x0, waiting for transfers between devices: 214 us -> none  [body(): grad_weight = lax.psum(partial_grad, ('group', 'member')) * grad_scale]
    pallas_call x0 -> x4, Pallas kernels: none -> 112 us  [the longest x2 68.8 us: gather_sum(): pl.pallas_call(_gather_kernel, out_shape=jax.ShapeDtypeStruct(init.shape,...]
    scatter-add x2 -> x0, other arithmetic: 110 us -> none  [apply_graph(): total = jax.ops.segment_sum(products, segment_ids, num_segments=own_blocks)]
    dot_general x10 -> x0, matrix products: 59.1 us -> none  [the longest x2 15.8 us: apply_graph(): jnp.einsum('sk,saf->kaf', back_hot, returned, preferred_element_type=jnp....]
    concatenate x2 -> x0, local copies, waits for them, and re-layouts: 49.3 us -> none  [apply_graph(): products = jnp.concatenate([to_home, to_near, to_home_r], axis=0)]
    gather x10 -> x0, local copies, waits for them, and re-layouts: 43.3 us -> none  [the longest x2 13 us: apply_graph(): outgoing = blocks_in[picked]]
    concatenate x3 -> x0, other arithmetic: 31.6 us -> none  [the longest x2 31.5 us: apply_graph(): products = jnp.concatenate([to_home, to_near, to_home_r], axis=0)]
  transfers between devices with their start and end apart: 6 -> 4, of which waited for: 4 -> 3; matrix products, arithmetic and copies ran while one was open for 12% -> 1% of each run, Pallas kernels for 0% -> 3%
where the time goes in v1:
time: 738 us
  waiting for transfers between devices  549 us (74%)
  Pallas kernels  112 us (15%)
  starting transfers between devices  35.5 us (5%)
  blocking collectives  15.1 us (2%)
  local copies, waits for them, and re-layouts  11.6 us (2%)
  other arithmetic  10.3 us (1%)
    all_to_all x2, waiting for transfers between devices, apply_graph(): recv = lax.all_to_all(send, AXES, split_axis=0, concat_axis=0, tiled=True)  542 us
    pallas_call x2, Pallas kernels, gather_sum(): pl.pallas_call(_gather_kernel, out_shape=jax.ShapeDtypeStruct(init.shape,...  68.8 us
    pallas_call x2, Pallas kernels, build_send(): pl.pallas_call(_send_kernel, out_shape=jax.ShapeDtypeStruct((slots, 2, BL...  43.5 us
    all_to_all x2, starting transfers between devices, apply_graph(): recv = lax.all_to_all(send, AXES, split_axis=0, concat_axis=0, tiled=True)  17.9 us
    all_to_all x1, blocking collectives, body(): lax.all_to_all(partial_grad.reshape(device_count, chunk, F), AXES, split_...  15.1 us
  transfers between devices with their start and end apart: 4, of which 3 were waited for; matrix products, arithmetic and copies ran while one was open for 1% of the time, Pallas kernels for 3%

profile of v1, /device:TPU:41, one launch (start us, length us, event | category | flops | bytes accessed | tf_op | source)
XLA Modules:
  0.0 737.8 jit_solution(14925214439483005437)
XLA Ops:
  0.6 0.0 copy-start
  0.6 1.2 compare_select_fusion
  1.9 0.8 scatter_custom_fusion
  2.7 0.7 copy.13
  3.4 10.5 %all-to-all-start = ((s32[128,1,1]{2,1,0:T(1,128)}), s32[128,1,1]{2,1,0:T(1,128)S(1)}, u32[]{:S(2)}, u32[]{:S(2)}) async-start(s32[128,1,1]{2,1,0:T(1,128)} %copy.13), calls=%async_computation | async-start | bytes 131072 | tf_op jit(solution)/shard_map/all_to_all | solution.py:123
  13.9 1.2 broadcast_clamp_fusion.rhome_ref
  15.1 6.3 all-to-all-done
  21.3 5.2 fusion.2
  26.5 21.7 %shard_map.112 = bf16[128,2,128,256]{3,2,1,0:T(8,128)(2,1)} custom-call(s32[128]{0:T(128)} %get-tuple-element.4.picked_ref, s32[64]{0:T(128)} %broadcast_clamp_fusion.rhome_ref, s32[64]{0:T(128)} %get-tuple-element.6.tdev_ref, bf16[16,128,256]{2,1,0:T(8,128)(2,1)} %bitcast.14, bf16[64,128,128]{2,1,0:T(8,128)(2,1)} %rt_ref.7), custom_call_target="tpu_custom_call" | custom-call | tf_op jit(solution)/shard_map/pallas_call | solution.py:50
  48.3 0.0 copy-start.4
  48.3 0.0 copy-start.5
  48.3 7.7 %all-to-all-start.1 = ((bf16[128,2,128,256]{3,2,1,0:T(8,128)(2,1)}), bf16[128,2,128,256]{3,2,1,0:T(8,128)(2,1)}, u32[]{:S(2)}, u32[]{:S(2)}) async-start(bf16[128,2,128,256]{3,2,1,0:T(8,128)(2,1)} %shard_map.112), calls=%async_computation.1 | async-start | bytes 33554432 | tf_op jit(solution)/shard_map/all_to_all | solution.py:129
  56.0 0.0 copy-done.4
  56.0 0.0 copy-done.5
  56.0 0.6 broadcast_clamp_fusion.1
  56.6 272.9 %all-to-all-done.1.recv_ref = bf16[128,2,128,256]{3,2,1,0:T(8,128)(2,1)} async-done(((bf16[128,2,128,256]{3,2,1,0:T(8,128)(2,1)}), bf16[128,2,128,256]{3,2,1,0:T(8,128)(2,1)}, u32[]{:S(2)}, u32[]{:S(2)}) %all-to-all-start.1) | async-done | bytes 16777248 | tf_op jit(solution)/shard_map/all_to_all | solution.py:129
  329.5 1.5 broadcast_in_dim.17.init_ref
  331.0 34.4 %shard_map.113 = f32[16,128,256]{2,1,0:T(8,128)} custom-call(s32[64]{0:T(128)} %get-tuple-element.11.lhome_ref, s32[64]{0:T(128)} %get-tuple-element.10.lnear_ref, s32[64]{0:T(128)} %broadcast_clamp_fusion.rhome_ref, s32[64]{0:T(128)} %get-tuple-element.6.tdev_ref, s32[128]{0:T(128)} %get-tuple-element.4.picked_ref, s32[128]{0:T(128)} %get-tuple-element.3.valid_ref, ...), custom_call_target="tpu_custom_call" | custom-call | tf_op jit(solution)/shard_map/pallas_call | solution.py:94
  365.4 0.0 copy-start.3
  365.4 0.0 copy-start.6
  365.4 1.9 convert_element_type.23
  367.3 0.0 copy-done
  367.3 0.0 copy-done.3
  367.3 0.3 copy-done.6
  367.6 2.3 multiply_convert_fusion
  369.9 0.7 fusion
  370.6 0.1 reshape.37
  370.8 15.1 %all_to_all.29 = f32[128,4,256]{2,1,0:T(4,128)S(1)} all-to-all(f32[128,4,256]{2,1,0:T(4,128)S(1)} %reshape.37), channel_id=1, replica_groups=mesh['group'=2,'member'=64] {'group','member'}, dimensions={0} | all-to-all | bytes 1048576 | tf_op jit(solution)/shard_map/all_to_all | solution.py:146
  385.9 0.1 reduce_sum.9
  386.0 0.9 broadcast_in_dim.18
  386.9 7.1 all-to-all-start.3
  394.0 0.7 fusion.9
  394.8 0.0 copy-start.2
  394.8 2.1 copy-done.2
  396.8 1.1 slice.12
  398.0 21.7 %shard_map.114 = bf16[128,2,128,256]{3,2,1,0:T(8,128)(2,1)} custom-call(s32[128]{0:T(128)} %get-tuple-element.4.picked_ref, s32[64]{0:T(128)} %broadcast_clamp_fusion.rhome_ref, s32[64]{0:T(128)} %get-tuple-element.6.tdev_ref, bf16[16,128,256]{2,1,0:T(8,128)(2,1)} %bitcast.11, bf16[64,128,128]{2,1,0:T(8,128)(2,1)} %rt_ref.7), custom_call_target="tpu_custom_call" | custom-call | tf_op jit(solution)/shard_map/pallas_call | solution.py:50
  419.7 0.0 all-to-all-done.3
  419.7 10.2 %all-to-all-start.4 = ((bf16[128,2,128,256]{3,2,1,0:T(8,128)(2,1)}), bf16[128,2,128,256]{3,2,1,0:T(8,128)(2,1)}, u32[]{:S(2)}, u32[]{:S(2)}) async-start(bf16[128,2,128,256]{3,2,1,0:T(8,128)(2,1)} %shard_map.114), calls=%async_computation.4 | async-start | bytes 33554432 | tf_op jit(solution)/shard_map/all_to_all | solution.py:129
  429.9 3.0 slice.10
  433.0 0.1 broadcast_multiply_fusion
  433.1 1.0 mul.27
  434.1 269.4 %all-to-all-done.4.recv_ref = bf16[128,2,128,256]{3,2,1,0:T(8,128)(2,1)} async-done(((bf16[128,2,128,256]{3,2,1,0:T(8,128)(2,1)}), bf16[128,2,128,256]{3,2,1,0:T(8,128)(2,1)}, u32[]{:S(2)}, u32[]{:S(2)}) %all-to-all-start.4) | async-done | bytes 16777248 | tf_op jit(solution)/shard_map/all_to_all | solution.py:129
  703.4 0.0 copy-start.1
  703.4 34.4 %shard_map.115 = f32[16,128,256]{2,1,0:T(8,128)} custom-call(s32[64]{0:T(128)} %get-tuple-element.11.lhome_ref, s32[64]{0:T(128)} %get-tuple-element.10.lnear_ref, s32[64]{0:T(128)} %broadcast_clamp_fusion.rhome_ref, s32[64]{0:T(128)} %get-tuple-element.6.tdev_ref, s32[128]{0:T(128)} %get-tuple-element.4.picked_ref, s32[128]{0:T(128)} %get-tuple-element.3.valid_ref, ...), custom_call_target="tpu_custom_call" | custom-call | tf_op jit(solution)/shard_map/pallas_call | solution.py:94
  737.8 0.0 copy-done.1
Async XLA Ops:
  0.6 366.6 %copy-start = (bf16[512,256]{1,0:T(8,128)(2,1)S(1)}, bf16[512,256]{1,0:T(8,128)(2,1)}, u32[]{:S(2)}) copy-start(bf16[512,256]{1,0:T(8,128)(2,1)} %param.16) | copy-start | bytes 786436
  3.4 17.9 %all-to-all-start = ((s32[128,1,1]{2,1,0:T(1,128)}), s32[128,1,1]{2,1,0:T(1,128)S(1)}, u32[]{:S(2)}, u32[]{:S(2)}) async-start(s32[128,1,1]{2,1,0:T(1,128)} %copy.13), calls=%async_computation | async-start | bytes 131072 | tf_op jit(solution)/shard_map/all_to_all | solution.py:123
  48.3 7.7 %copy-start.4 = (s32[64]{0:T(128)S(1)}, s32[64]{0:T(128)}, u32[]{:S(2)}) copy-start(s32[64]{0:T(128)} %param.11) | copy-start | bytes 772
  48.3 7.7 %copy-start.5 = (s32[64]{0:T(128)S(1)}, s32[64]{0:T(128)}, u32[]{:S(2)}) copy-start(s32[64]{0:T(128)} %param.10) | copy-start | bytes 772
  48.3 281.2 %all-to-all-start.1 = ((bf16[128,2,128,256]{3,2,1,0:T(8,128)(2,1)}), bf16[128,2,128,256]{3,2,1,0:T(8,128)(2,1)}, u32[]{:S(2)}, u32[]{:S(2)}) async-start(bf16[128,2,128,256]{3,2,1,0:T(8,128)(2,1)} %shard_map.112), calls=%async_computation.1 | async-start | bytes 33554432 | tf_op jit(solution)/shard_map/all_to_all | solution.py:129
  365.4 1.9 copy-start.3
  365.4 2.2 copy-start.6
  386.9 32.8 %all-to-all-start.3 = ((f32[128,4,256]{2,1,0:T(4,128)}), f32[128,4,256]{2,1,0:T(4,128)S(1)}, u32[]{:S(2)}, u32[]{:S(2)}) async-start(f32[128,4,256]{2,1,0:T(4,128)} %broadcast_in_dim.18), calls=%async_computation.3 | async-start | bytes 1048576 | tf_op jit(solution)/shard_map/all_to_all | solution.py:151
  394.8 2.1 copy-start.2
  419.7 283.7 %all-to-all-start.4 = ((bf16[128,2,128,256]{3,2,1,0:T(8,128)(2,1)}), bf16[128,2,128,256]{3,2,1,0:T(8,128)(2,1)}, u32[]{:S(2)}, u32[]{:S(2)}) async-start(bf16[128,2,128,256]{3,2,1,0:T(8,128)(2,1)} %shard_map.114), calls=%async_computation.4 | async-start | bytes 33554432 | tf_op jit(solution)/shard_map/all_to_all | solution.py:129
  703.4 34.4 %copy-start.1 = (bf16[512,256]{1,0:T(8,128)(2,1)S(1)}, bf16[512,256]{1,0:T(8,128)(2,1)}, u32[]{:S(2)}) copy-start(bf16[512,256]{1,0:T(8,128)(2,1)} %param.16) | copy-start | bytes 786436

commit v2 on v1

v2 whole, which is shorter than its diff:
```python
import math

import jax
import jax.numpy as jnp
from jax import lax
from jax.experimental import pallas as pl
from jax.experimental.pallas import tpu as pltpu
from jax.sharding import PartitionSpec as P

F = 256
BLOCK = 128
BLK_DEV = 16
AXES = ("group", "member")
VMEM_LIMIT = 56 * 1024 * 1024


def _smem():
    return pl.BlockSpec(memory_space=pltpu.SMEM)


def _vmem():
    return pl.BlockSpec(memory_space=pltpu.VMEM)


def _dot_t(a, v):
    return lax.dot_general(a, v, (((0,), (0,)), ((), ())), preferred_element_type=jnp.float32)


def _lists(dest, n_dest):
    order = jnp.argsort(dest, stable=True).astype(jnp.int32)
    counts = jnp.sum(dest[:, None] == jnp.arange(n_dest, dtype=jnp.int32)[None, :], axis=0)
    starts = jnp.concatenate([jnp.zeros((1,), jnp.int32), jnp.cumsum(counts).astype(jnp.int32)])
    return order, starts


def _local_kernel(hs_ref, ho_ref, ns_ref, no_ref, lh_ref, ln_ref, x_ref, lt_ref, init_ref, out_ref):
    blocks = out_ref.shape[0]

    def per_block(k, c):
        acc = init_ref[k]

        def home_term(i, a):
            p = ho_ref[i]
            return a + jnp.dot(lt_ref[p], x_ref[ln_ref[p]], preferred_element_type=jnp.float32)

        acc = lax.fori_loop(hs_ref[k], hs_ref[k + 1], home_term, acc)

        def near_term(i, a):
            p = no_ref[i]
            return a + _dot_t(lt_ref[p], x_ref[lh_ref[p]])

        acc = lax.fori_loop(ns_ref[k], ns_ref[k + 1], near_term, acc)
        out_ref[k] = acc
        return c

    lax.fori_loop(0, blocks, per_block, 0)


def local_sum(hs, ho, ns, no, lh, ln, x, ltiles, init):
    pairs = ltiles.shape[0]
    cost = pl.CostEstimate(
        flops=2 * 2 * pairs * BLOCK * BLOCK * F,
        transcendentals=0,
        bytes_accessed=x.size * 2 + ltiles.size * 2 + init.size * 8,
    )
    return pl.pallas_call(
        _local_kernel,
        out_shape=jax.ShapeDtypeStruct(init.shape, jnp.float32),
        in_specs=[_smem()] * 6 + [_vmem()] * 3,
        out_specs=_vmem(),
        cost_estimate=cost,
        compiler_params=pltpu.CompilerParams(vmem_limit_bytes=VMEM_LIMIT),
    )(hs, ho, ns, no, lh, ln, x, ltiles, init)


SEND_GROUP = 8


def _send_kernel(picked_ref, spair_ref, sused_ref, rhome_ref, x_ref, rt_ref, send_ref):
    base = pl.program_id(0) * SEND_GROUP
    for j in range(SEND_GROUP):
        t = base + j
        send_ref[j, 0] = x_ref[picked_ref[t]]
        p = spair_ref[t]
        r = _dot_t(rt_ref[p], x_ref[rhome_ref[p]])
        r = jnp.where(sused_ref[t] > 0, r, 0.0)
        send_ref[j, 1] = r.astype(send_ref.dtype)


def build_send(picked, spair, sused, rhome, x, rtiles):
    slots = picked.shape[0]
    full3 = lambda i: (0, 0, 0)
    cost = pl.CostEstimate(
        flops=2 * slots * BLOCK * BLOCK * F,
        transcendentals=0,
        bytes_accessed=x.size * 2 + rtiles.size * 2 + slots * 2 * BLOCK * F * 2,
    )
    return pl.pallas_call(
        _send_kernel,
        grid=(slots // SEND_GROUP,),
        out_shape=jax.ShapeDtypeStruct((slots, 2, BLOCK, F), jnp.bfloat16),
        in_specs=[_smem()] * 4 + [
            pl.BlockSpec(x.shape, full3),
            pl.BlockSpec(rtiles.shape, full3),
        ],
        out_specs=pl.BlockSpec((SEND_GROUP, 2, BLOCK, F), lambda i: (i, 0, 0, 0)),
        cost_estimate=cost,
        compiler_params=pltpu.CompilerParams(vmem_limit_bytes=VMEM_LIMIT),
    )(picked, spair, sused, rhome, x, rtiles)


def _post_kernel(rs_ref, ro_ref, td_ref, ss_ref, so_ref, rt_ref, recv_ref, base_ref, out_ref):
    blocks = out_ref.shape[0]

    def per_block(k, c):
        acc = base_ref[k]

        def remote_term(i, a):
            p = ro_ref[i]
            return a + jnp.dot(rt_ref[p], recv_ref[td_ref[p], 0], preferred_element_type=jnp.float32)

        acc = lax.fori_loop(rs_ref[k], rs_ref[k + 1], remote_term, acc)

        def back_term(i, a):
            return a + recv_ref[so_ref[i], 1].astype(jnp.float32)

        acc = lax.fori_loop(ss_ref[k], ss_ref[k + 1], back_term, acc)
        out_ref[k] = acc
        return c

    lax.fori_loop(0, blocks, per_block, 0)


def post_sum(rs, ro, td, ss, so, rtiles, recv, base):
    pairs = rtiles.shape[0]
    cost = pl.CostEstimate(
        flops=2 * pairs * BLOCK * BLOCK * F,
        transcendentals=0,
        bytes_accessed=rtiles.size * 2 + recv.size * 2 + base.size * 8,
    )
    return pl.pallas_call(
        _post_kernel,
        out_shape=jax.ShapeDtypeStruct(base.shape, jnp.float32),
        in_specs=[_smem()] * 5 + [_vmem()] * 3,
        out_specs=_vmem(),
        cost_estimate=cost,
        input_output_aliases={7: 0},
        compiler_params=pltpu.CompilerParams(vmem_limit_bytes=VMEM_LIMIT),
    )(rs, ro, td, ss, so, rtiles, recv, base)


def body(
    features,
    local_home,
    local_near,
    local_tiles,
    remote_home,
    remote_far,
    remote_tiles,
    weight,
    cotangent,
):
    device_count = lax.axis_size(AXES)
    row_count = features.shape[0]
    own_blocks = row_count // BLOCK
    lhome = jnp.clip(local_home, 0, own_blocks - 1)
    lnear = jnp.clip(local_near, 0, own_blocks - 1)
    rhome = jnp.clip(remote_home, 0, own_blocks - 1)
    target_dev = jnp.clip(remote_far // BLK_DEV, 0, device_count - 1)
    wanted = remote_far % BLK_DEV
    request = jnp.full((device_count,), -1, jnp.int32).at[target_dev].set(wanted)
    asked = lax.all_to_all(request, AXES, split_axis=0, concat_axis=0, tiled=True)
    picked = jnp.clip(asked, 0, own_blocks - 1)
    back_dest = jnp.where(asked >= 0, picked, own_blocks)
    slot_pair = jnp.zeros((device_count,), jnp.int32).at[target_dev].set(
        jnp.arange(target_dev.shape[0], dtype=jnp.int32))
    slot_used = jnp.zeros((device_count,), jnp.int32).at[target_dev].set(1)
    h_order, h_starts = _lists(lhome, own_blocks)
    n_order, n_starts = _lists(lnear, own_blocks)
    r_order, r_starts = _lists(rhome, own_blocks)
    s_order, s_starts = _lists(back_dest, own_blocks)

    def apply_graph(blocks_in, init):
        send = build_send(picked, slot_pair, slot_used, rhome, blocks_in, remote_tiles)
        recv = lax.all_to_all(send, AXES, split_axis=0, concat_axis=0, tiled=True)
        part = local_sum(h_starts, h_order, n_starts, n_order, lhome, lnear, blocks_in, local_tiles, init)
        total = post_sum(r_starts, r_order, target_dev, s_starts, s_order, remote_tiles, recv, part)
        return total.reshape(row_count, F)

    zeros = jnp.zeros((own_blocks, BLOCK, F), jnp.float32)
    aggregate = apply_graph(features.reshape(own_blocks, BLOCK, F), zeros).astype(jnp.bfloat16)
    joined = jnp.concatenate([features, aggregate], axis=1)
    pre_act = jnp.dot(joined, weight, preferred_element_type=jnp.float32)
    sigmoid_z = jax.nn.sigmoid(pre_act)
    output = (pre_act * sigmoid_z).astype(jnp.bfloat16)
    grad_pre = (
        cotangent.astype(jnp.float32) * sigmoid_z * (1.0 + pre_act * (1.0 - sigmoid_z))
    ).astype(jnp.bfloat16)
    partial_grad = jnp.einsum("ra,rf->af", joined, grad_pre, preferred_element_type=jnp.float32)
    grad_scale = 1.0 / math.sqrt(row_count * device_count)
    grad_weight = lax.psum(partial_grad, AXES) * grad_scale
    grad_joined = jnp.einsum("rf,af->ra", grad_pre, weight, preferred_element_type=jnp.float32)
    grad_agg = grad_joined[:, F:].astype(jnp.bfloat16).reshape(own_blocks, BLOCK, F)
    init_b = grad_joined[:, :F].reshape(own_blocks, BLOCK, F)
    grad_features = apply_graph(grad_agg, init_b)
    return (output, grad_weight, grad_features)


def solution(mesh):
    in_specs = (
        P(AXES, None),
        P(AXES),
        P(AXES),
        P(AXES, None, None),
        P(AXES),
        P(AXES),
        P(AXES, None, None),
        P(),
        P(AXES, None),
    )
    out_specs = (P(AXES, None), P(), P(AXES, None))
    return jax.shard_map(body, mesh=mesh, in_specs=in_specs, out_specs=out_specs, check_vma=False)
```

time: 738 us -> 763 us (1.034)
  blocking collectives: 15.1 us -> 0 us
  between operations: 0.76 us -> 14.2 us
  other arithmetic: 10.3 us -> 22.7 us
  starting transfers between devices: 35.5 us -> 23.2 us
  waiting for transfers between devices: 549 us -> 561 us
  Pallas kernels: 112 us -> 121 us
    psum x0 -> x1, waiting for transfers between devices: none -> 327 us  [body(): grad_weight = lax.psum(partial_grad, AXES) * grad_scale]
    all_to_all x2, waiting for transfers between devices: 542 us -> 231 us  [apply_graph(): recv = lax.all_to_all(send, AXES, split_axis=0, concat_axis=0, tiled=True)]
    all_to_all x1 -> x0, blocking collectives: 15.1 us -> none  [body(): lax.all_to_all(partial_grad.reshape(device_count, chunk, F), AXES, split_...]
    sort x0 -> x4, other arithmetic: none -> 8.86 us  [_lists(): order = jnp.argsort(dest, stable=True).astype(jnp.int32)]
    pallas_call x4 -> x6, Pallas kernels: 112 us -> 121 us  [the longest x2 54.2 us: local_sum(): pl.pallas_call(_local_kernel, out_shape=jax.ShapeDtypeStruct(init.shape,...]
  transfers between devices with their start and end apart: 4 -> 4, of which waited for: 3 -> 3; matrix products, arithmetic and copies ran while one was open for 1% -> 3% of each run, Pallas kernels for 3% -> 7%
where the time goes in v2:
time: 763 us; the launch traced here: 759 us
  waiting for transfers between devices  561 us (74%)
  Pallas kernels  121 us (16%)
  starting transfers between devices  23.2 us (3%)
  other arithmetic  22.7 us (3%)
  between operations  14.2 us (2%)
  local copies, waits for them, and re-layouts  12.5 us (2%)
    psum x1, waiting for transfers between devices, body(): grad_weight = lax.psum(partial_grad, AXES) * grad_scale  327 us
    all_to_all x2, waiting for transfers between devices, apply_graph(): recv = lax.all_to_all(send, AXES, split_axis=0, concat_axis=0, tiled=True)  231 us
    pallas_call x2, Pallas kernels, local_sum(): pl.pallas_call(_local_kernel, out_shape=jax.ShapeDtypeStruct(init.shape,...  54.2 us
    pallas_call x2, Pallas kernels, post_sum(): pl.pallas_call(_post_kernel, out_shape=jax.ShapeDtypeStruct(base.shape, j...  40.4 us
    pallas_call x2, Pallas kernels, build_send(): pl.pallas_call(_send_kernel, grid=(slots // SEND_GROUP,), out_shape=jax.S...  26.2 us
  transfers between devices with their start and end apart: 4, of which 3 were waited for; matrix products, arithmetic and copies ran while one was open for 3% of the time, Pallas kernels for 7%

profile of v2, /device:TPU:41, one launch (start us, length us, event | category | flops | bytes accessed | tf_op | source)
XLA Modules:
  0.0 759.4 jit_solution(12828550764148857598)
XLA Ops:
  7.2 1.3 compare_select_fusion
  8.5 0.8 scatter_custom_fusion
  9.2 0.7 copy.33
  10.0 10.5 %all-to-all-start = ((s32[128,1,1]{2,1,0:T(1,128)}), s32[128,1,1]{2,1,0:T(1,128)S(1)}, u32[]{:S(2)}, u32[]{:S(2)}) async-start(s32[128,1,1]{2,1,0:T(1,128)} %copy.33), calls=%async_computation | async-start | bytes 131072 | tf_op jit(solution)/shard_map/all_to_all | solution.py:172
  20.5 1.2 broadcast_clamp_fusion.2.rhome_ref
  21.7 1.3 scatter_custom_fusion.1.spair_ref
  22.9 1.3 scatter_custom_fusion.2.sused_ref
  24.3 3.6 all-to-all-done
  27.9 2.9 clamp_reduce_fusion.picked_ref
  30.8 13.1 %shard_map.112 = bf16[128,2,128,256]{3,2,1,0:T(8,128)(2,1)} custom-call(s32[128]{0:T(128)} %clamp_reduce_fusion.picked_ref, s32[128]{0:T(128)} %scatter_custom_fusion.1.spair_ref, s32[128]{0:T(128)} %scatter_custom_fusion.2.sused_ref, s32[64]{0:T(128)} %broadcast_clamp_fusion.2.rhome_ref, bf16[16,128,256]{2,1,0:T(8,128)(2,1)} %bitcast.21, ...), custom_call_target="tpu_custom_call" | custom-call | flops 1073741824 | bytes 19922944 | tf_op jit(solution)/shard_map/pallas_call | solution.py:98
  43.9 7.7 %all-to-all-start.1 = ((bf16[128,2,128,256]{3,2,1,0:T(8,128)(2,1)}), bf16[128,2,128,256]{3,2,1,0:T(8,128)(2,1)}, u32[]{:S(2)}, u32[]{:S(2)}) async-start(bf16[128,2,128,256]{3,2,1,0:T(8,128)(2,1)} %shard_map.112), calls=%async_computation.1 | async-start | bytes 33554432 | tf_op jit(solution)/shard_map/all_to_all | solution.py:185
  51.6 2.1 sort.62
  53.8 2.1 sort.64
  55.9 0.1 convert_reduce_fusion.1
  56.0 0.1 copy.35
  56.1 0.1 reduce.4
  56.3 2.0 sort.65
  58.3 0.1 convert_reduce_fusion
  58.4 0.1 copy.36
  58.6 0.1 reduce.5
  58.7 0.1 convert_reduce_fusion.3
  58.8 0.1 copy.32
  58.9 0.1 reduce
  59.0 0.7 pad_add_fusion
  59.7 1.5 broadcast_in_dim.13.init_ref
  61.3 27.1 %shard_map.113.base_ref = f32[16,128,256]{2,1,0:T(8,128)} custom-call(s32[17]{0:T(128)} %get-tuple-element.17.hs_ref, s32[64]{0:T(128)} %get-tuple-element.9.ho_ref, s32[17]{0:T(128)} %get-tuple-element.16.ns_ref, s32[64]{0:T(128)} %get-tuple-element.10.no_ref, s32[64]{0:T(128)} %copy-done.6, s32[64]{0:T(128)} %copy-done.7, bf16[16,128,256]{2,1,0:T(8,128)(2,1)} %bitcast.22, ...), custom_call_target="tpu_custom_call" | custom-call | flops 1073741824 | bytes 7340032 | tf_op jit(solution)/shard_map/pallas_call | solution.py:66
  88.4 2.4 compare_reduce_fusion
  90.8 2.6 sort.63
  93.4 0.1 convert_reduce_fusion.2
  93.5 0.1 copy.34
  93.6 0.1 reduce.3
  93.7 0.7 pad_add_fusion.2
  94.4 230.7 %all-to-all-done.1.recv_ref = bf16[128,2,128,256]{3,2,1,0:T(8,128)(2,1)} async-done(((bf16[128,2,128,256]{3,2,1,0:T(8,128)(2,1)}), bf16[128,2,128,256]{3,2,1,0:T(8,128)(2,1)}, u32[]{:S(2)}, u32[]{:S(2)}) %all-to-all-start.1) | async-done | bytes 16777248 | tf_op jit(solution)/shard_map/all_to_all | solution.py:185
  325.1 20.2 %shard_map.114 = f32[16,128,256]{2,1,0:T(8,128)} custom-call(s32[17]{0:T(128)} %get-tuple-element.19.rs_ref, s32[64]{0:T(128)} %get-tuple-element.7.ro_ref, s32[64]{0:T(128)} %get-tuple-element.12.td_ref, s32[17]{0:T(128)} %get-tuple-element.18.ss_ref, s32[128]{0:T(128)} %get-tuple-element.8.so_ref, ...), custom_call_target="tpu_custom_call", output_to_operand_aliasing={{}: (7, {})} | custom-call | flops 536870912 | bytes 23068672 | tf_op jit(solution)/shard_map/pallas_call | solution.py:141
  345.3 1.9 convert_element_type.32
  347.2 0.3 copy-done.8
  347.5 2.3 multiply_convert_fusion
  349.7 0.7 fusion.12
  350.5 2.0 copy-done.2
  352.5 1.1 slice.12
  353.7 13.1 %shard_map.115 = bf16[128,2,128,256]{3,2,1,0:T(8,128)(2,1)} custom-call(s32[128]{0:T(128)} %clamp_reduce_fusion.picked_ref, s32[128]{0:T(128)} %scatter_custom_fusion.1.spair_ref, s32[128]{0:T(128)} %scatter_custom_fusion.2.sused_ref, s32[64]{0:T(128)} %broadcast_clamp_fusion.2.rhome_ref, bf16[16,128,256]{2,1,0:T(8,128)(2,1)} %bitcast.17, ...), custom_call_target="tpu_custom_call" | custom-call | flops 1073741824 | bytes 19922944 | tf_op jit(solution)/shard_map/pallas_call | solution.py:98
  366.8 5.0 all-to-all-start.2
  371.8 1.5 fusion
  373.3 3.0 slice.10
  376.4 27.1 %shard_map.116.base_ref = f32[16,128,256]{2,1,0:T(8,128)} custom-call(s32[17]{0:T(128)} %get-tuple-element.17.hs_ref, s32[64]{0:T(128)} %get-tuple-element.9.ho_ref, s32[17]{0:T(128)} %get-tuple-element.16.ns_ref, s32[64]{0:T(128)} %get-tuple-element.10.no_ref, s32[64]{0:T(128)} %copy-done.6, s32[64]{0:T(128)} %copy-done.7, bf16[16,128,256]{2,1,0:T(8,128)(2,1)} %bitcast.18, ...), custom_call_target="tpu_custom_call" | custom-call | flops 1073741824 | bytes 7340032 | tf_op jit(solution)/shard_map/pallas_call | solution.py:66
  403.5 327.0 %all-reduce.2.cloned.1.call-done = f32[512,256]{1,0:T(8,128)} async-done(((f32[512,256]{1,0:T(8,128)}), f32[512,256]{1,0:T(8,128)}) %all-reduce.2.cloned.1.call-update) | async-done | bytes 524304 | tf_op jit(solution)/shard_map/psum | solution.py:201
  730.5 1.9 broadcast_multiply_fusion
  732.4 20.2 %shard_map.117 = f32[16,128,256]{2,1,0:T(8,128)} custom-call(s32[17]{0:T(128)} %get-tuple-element.19.rs_ref, s32[64]{0:T(128)} %get-tuple-element.7.ro_ref, s32[64]{0:T(128)} %get-tuple-element.12.td_ref, s32[17]{0:T(128)} %get-tuple-element.18.ss_ref, s32[128]{0:T(128)} %get-tuple-element.8.so_ref, ...), custom_call_target="tpu_custom_call", output_to_operand_aliasing={{}: (7, {})} | custom-call | flops 536870912 | bytes 23068672 | tf_op jit(solution)/shard_map/pallas_call | solution.py:141
  (36 shorter events, 0.3 us)
Async XLA Ops:
  7.2 340.0 %copy-start = (bf16[512,256]{1,0:T(8,128)(2,1)S(1)}, bf16[512,256]{1,0:T(8,128)(2,1)}, u32[]{:S(2)}) copy-start(bf16[512,256]{1,0:T(8,128)(2,1)} %param.16) | copy-start | bytes 786436
  10.0 17.9 %all-to-all-start = ((s32[128,1,1]{2,1,0:T(1,128)}), s32[128,1,1]{2,1,0:T(1,128)S(1)}, u32[]{:S(2)}, u32[]{:S(2)}) async-start(s32[128,1,1]{2,1,0:T(1,128)} %copy.33), calls=%async_computation | async-start | bytes 131072 | tf_op jit(solution)/shard_map/all_to_all | solution.py:172
  43.9 7.7 %copy-start.5 = (s32[64]{0:T(128)S(1)}, s32[64]{0:T(128)}, u32[]{:S(2)}) copy-start(s32[64]{0:T(128)} %broadcast_clamp_fusion.2.rhome_ref) | copy-start | bytes 772
  43.9 9.9 %copy-start.9 = (s32[64]{0:T(128)S(1)}, s32[64]{0:T(128)}, u32[]{:S(2)}) copy-start(s32[64]{0:T(128)} %param.10) | copy-start | bytes 772
  43.9 12.3 %copy-start.10 = (s32[64]{0:T(128)S(1)}, s32[64]{0:T(128)}, u32[]{:S(2)}) copy-start(s32[64]{0:T(128)} %param.11) | copy-start | bytes 772
  43.9 281.2 %all-to-all-start.1 = ((bf16[128,2,128,256]{3,2,1,0:T(8,128)(2,1)}), bf16[128,2,128,256]{3,2,1,0:T(8,128)(2,1)}, u32[]{:S(2)}, u32[]{:S(2)}) async-start(bf16[128,2,128,256]{3,2,1,0:T(8,128)(2,1)} %shard_map.112), calls=%async_computation.1 | async-start | bytes 33554432 | tf_op jit(solution)/shard_map/all_to_all | solution.py:185
  53.8 7.5 copy-start.6
  56.3 5.0 copy-start.7
  61.3 29.5 %copy-start.4 = (s32[128]{0:T(128)S(1)}, s32[128]{0:T(128)}, u32[]{:S(2)}) copy-start(s32[128]{0:T(128)} %clamp_reduce_fusion.picked_ref) | copy-start | bytes 1540
  345.3 1.9 copy-start.3
  345.3 2.2 copy-start.8
  350.5 2.0 copy-start.2
  366.8 365.6 %all-to-all-start.2 = ((bf16[128,2,128,256]{3,2,1,0:T(8,128)(2,1)}), bf16[128,2,128,256]{3,2,1,0:T(8,128)(2,1)}, u32[]{:S(2)}, u32[]{:S(2)}) async-start(bf16[128,2,128,256]{3,2,1,0:T(8,128)(2,1)} %shard_map.115), calls=%async_computation.2 | async-start | bytes 33554432 | tf_op jit(solution)/shard_map/all_to_all | solution.py:185
  371.7 358.8 %all-reduce.2.cloned.1.call-start = ((), (), s32[]{:S(2)}) async-start(), calls=%async_computation.3 | async-start | bytes 1048576 | tf_op jit(solution)/shard_map/psum | solution.py:201
  732.4 20.2 %copy-start.1 = (bf16[512,256]{1,0:T(8,128)(2,1)S(1)}, bf16[512,256]{1,0:T(8,128)(2,1)}, u32[]{:S(2)}) copy-start(bf16[512,256]{1,0:T(8,128)(2,1)} %param.16) | copy-start | bytes 786436
Sparse Core Ops, SparseCore 0:
  377.9 352.5 all-reduce.1

commit v3 on v2

--- a/solution.py
+++ b/solution.py
@@ -76,37 +76,45 @@
 SEND_GROUP = 8
 
 
-def _send_kernel(picked_ref, spair_ref, sused_ref, rhome_ref, x_ref, rt_ref, send_ref):
+def _send_kernel(picked_ref, spair_ref, sused_ref, rhome_ref, x_ref, rt_ref, *rest):
+    send_ref = rest[-1]
+    extra_ref = rest[0] if len(rest) == 2 else None
     base = pl.program_id(0) * SEND_GROUP
     for j in range(SEND_GROUP):
         t = base + j
-        send_ref[j, 0] = x_ref[picked_ref[t]]
+        send_ref[j, pl.ds(0, BLOCK)] = x_ref[picked_ref[t]]
         p = spair_ref[t]
         r = _dot_t(rt_ref[p], x_ref[rhome_ref[p]])
         r = jnp.where(sused_ref[t] > 0, r, 0.0)
-        send_ref[j, 1] = r.astype(send_ref.dtype)
-
-
-def build_send(picked, spair, sused, rhome, x, rtiles):
+        send_ref[j, pl.ds(BLOCK, BLOCK)] = r.astype(send_ref.dtype)
+        if extra_ref is not None:
+            send_ref[j, pl.ds(2 * BLOCK, extra_ref.shape[1])] = extra_ref[j]
+
+
+def build_send(picked, spair, sused, rhome, x, rtiles, extra=None):
     slots = picked.shape[0]
     full3 = lambda i: (0, 0, 0)
+    extra_rows = 0 if extra is None else extra.shape[1]
+    rows = 2 * BLOCK + extra_rows
     cost = pl.CostEstimate(
         flops=2 * slots * BLOCK * BLOCK * F,
         transcendentals=0,
-        bytes_accessed=x.size * 2 + rtiles.size * 2 + slots * 2 * BLOCK * F * 2,
-    )
+        bytes_accessed=x.size * 2 + rtiles.size * 2 + slots * rows * F * 2,
+    )
+    in_specs = [_smem()] * 4 + [pl.BlockSpec(x.shape, full3), pl.BlockSpec(rtiles.shape, full3)]
+    args = [picked, spair, sused, rhome, x, rtiles]
+    if extra is not None:
+        in_specs.append(pl.BlockSpec((SEND_GROUP, extra_rows, F), lambda i: (i, 0, 0)))
+        args.append(extra)
     return pl.pallas_call(
         _send_kernel,
         grid=(slots // SEND_GROUP,),
-        out_shape=jax.ShapeDtypeStruct((slots, 2, BLOCK, F), jnp.bfloat16),
-        in_specs=[_smem()] * 4 + [
-            pl.BlockSpec(x.shape, full3),
-            pl.BlockSpec(rtiles.shape, full3),
-        ],
-        out_specs=pl.BlockSpec((SEND_GROUP, 2, BLOCK, F), lambda i: (i, 0, 0, 0)),
+        out_shape=jax.ShapeDtypeStruct((slots, rows, F), jnp.bfloat16),
+        in_specs=in_specs,
+        out_specs=pl.BlockSpec((SEND_GROUP, rows, F), lambda i: (i, 0, 0)),
         cost_estimate=cost,
         compiler_params=pltpu.CompilerParams(vmem_limit_bytes=VMEM_LIMIT),
-    )(picked, spair, sused, rhome, x, rtiles)
+    )(*args)
 
 
 def _post_kernel(rs_ref, ro_ref, td_ref, ss_ref, so_ref, rt_ref, recv_ref, base_ref, out_ref):
@@ -117,12 +125,12 @@
 
         def remote_term(i, a):
             p = ro_ref[i]
-            return a + jnp.dot(rt_ref[p], recv_ref[td_ref[p], 0], preferred_element_type=jnp.float32)
+            return a + jnp.dot(rt_ref[p], recv_ref[td_ref[p], pl.ds(0, BLOCK)], preferred_element_type=jnp.float32)
 
         acc = lax.fori_loop(rs_ref[k], rs_ref[k + 1], remote_term, acc)
 
         def back_term(i, a):
-            return a + recv_ref[so_ref[i], 1].astype(jnp.float32)
+            return a + recv_ref[so_ref[i], pl.ds(BLOCK, BLOCK)].astype(jnp.float32)
 
         acc = lax.fori_loop(ss_ref[k], ss_ref[k + 1], back_term, acc)
         out_ref[k] = acc
@@ -180,15 +188,15 @@
     r_order, r_starts = _lists(rhome, own_blocks)
     s_order, s_starts = _lists(back_dest, own_blocks)
 
-    def apply_graph(blocks_in, init):
-        send = build_send(picked, slot_pair, slot_used, rhome, blocks_in, remote_tiles)
+    def apply_graph(blocks_in, init, extra=None):
+        send = build_send(picked, slot_pair, slot_used, rhome, blocks_in, remote_tiles, extra)
         recv = lax.all_to_all(send, AXES, split_axis=0, concat_axis=0, tiled=True)
         part = local_sum(h_starts, h_order, n_starts, n_order, lhome, lnear, blocks_in, local_tiles, init)
         total = post_sum(r_starts, r_order, target_dev, s_starts, s_order, remote_tiles, recv, part)
-        return total.reshape(row_count, F)
+        return total.reshape(row_count, F), recv
 
     zeros = jnp.zeros((own_blocks, BLOCK, F), jnp.float32)
-    aggregate = apply_graph(features.reshape(own_blocks, BLOCK, F), zeros).astype(jnp.bfloat16)
+    aggregate = apply_graph(features.reshape(own_blocks, BLOCK, F), zeros)[0].astype(jnp.bfloat16)
     joined = jnp.concatenate([features, aggregate], axis=1)
     pre_act = jnp.dot(joined, weight, preferred_element_type=jnp.float32)
     sigmoid_z = jax.nn.sigmoid(pre_act)
@@ -197,12 +205,20 @@
         cotangent.astype(jnp.float32) * sigmoid_z * (1.0 + pre_act * (1.0 - sigmoid_z))
     ).astype(jnp.bfloat16)
     partial_grad = jnp.einsum("ra,rf->af", joined, grad_pre, preferred_element_type=jnp.float32)
-    grad_scale = 1.0 / math.sqrt(row_count * device_count)
-    grad_weight = lax.psum(partial_grad, AXES) * grad_scale
+    rows = partial_grad.shape[0]
+    chunk = rows // device_count
+    pieces = partial_grad.reshape(device_count, chunk, F)
+    pieces_hi = pieces.astype(jnp.bfloat16)
+    pieces_lo = (pieces - pieces_hi.astype(jnp.float32)).astype(jnp.bfloat16)
+    extra = jnp.concatenate([pieces_hi, pieces_lo], axis=1)
     grad_joined = jnp.einsum("rf,af->ra", grad_pre, weight, preferred_element_type=jnp.float32)
     grad_agg = grad_joined[:, F:].astype(jnp.bfloat16).reshape(own_blocks, BLOCK, F)
     init_b = grad_joined[:, :F].reshape(own_blocks, BLOCK, F)
-    grad_features = apply_graph(grad_agg, init_b)
+    grad_features, recv_b = apply_graph(grad_agg, init_b, extra)
+    got = recv_b[:, 2 * BLOCK:, :].astype(jnp.float32)
+    mine = jnp.sum(got[:, :chunk] + got[:, chunk:], axis=0)
+    grad_scale = 1.0 / math.sqrt(row_count * device_count)
+    grad_weight = lax.all_gather(mine, AXES, axis=0, tiled=True) * grad_scale
     return (output, grad_weight, grad_features)
 
 

time: 763 us -> 980 us (1.28); the launches traced: 759 us -> 963 us
  blocking collectives: 0 us -> 296 us
  waiting for transfers between devices: 561 us -> 479 us
  between operations: 14.2 us -> 0.83 us
    psum x1 -> x0, waiting for transfers between devices: 327 us -> none  [body(): grad_weight = lax.psum(partial_grad, AXES) * grad_scale]
    all_gather x0 -> x1, blocking collectives: none -> 296 us  [body(): grad_weight = lax.all_gather(mine, AXES, axis=0, tiled=True) * grad_scale]
    all_to_all x2, waiting for transfers between devices: 231 us -> 475 us  [apply_graph(): recv = lax.all_to_all(send, AXES, split_axis=0, concat_axis=0, tiled=True)]
  transfers between devices with their start and end apart: 4 -> 3, of which waited for: 3 -> 3; matrix products, arithmetic and copies ran while one was open for 3% -> 2% of each run, Pallas kernels for 7% -> 6%
where the time goes in v3:
time: 980 us; the launch traced here: 963 us
  waiting for transfers between devices  479 us (49%)
  blocking collectives  296 us (30%)
  Pallas kernels  121 us (12%)
  other arithmetic  23.5 us (2%)
  starting transfers between devices  23.1 us (2%)
  local copies, waits for them, and re-layouts  13.2 us (1%)
    all_to_all x2, waiting for transfers between devices, apply_graph(): recv = lax.all_to_all(send, AXES, split_axis=0, concat_axis=0, tiled=True)  475 us
    all_gather x1, blocking collectives, body(): grad_weight = lax.all_gather(mine, AXES, axis=0, tiled=True) * grad_scale  296 us
    pallas_call x2, Pallas kernels, local_sum(): pl.pallas_call(_local_kernel, out_shape=jax.ShapeDtypeStruct(init.shape,...  54.2 us
    pallas_call x2, Pallas kernels, post_sum(): pl.pallas_call(_post_kernel, out_shape=jax.ShapeDtypeStruct(base.shape, j...  40.1 us
    pallas_call x2, Pallas kernels, build_send(): pl.pallas_call(_send_kernel, grid=(slots // SEND_GROUP,), out_shape=jax.S...  26.9 us
  transfers between devices with their start and end apart: 3, of which 3 were waited for; matrix products, arithmetic and copies ran while one was open for 2% of the time, Pallas kernels for 6%

profile of v3, /device:TPU:41, one launch (start us, length us, event | category | flops | bytes accessed | tf_op | source)
XLA Modules:
  0.0 962.8 jit_solution(5568455406977382032)
XLA Ops:
  0.6 1.2 compare_select_fusion
  1.8 0.8 scatter_custom_fusion
  2.6 0.7 copy.33
  3.4 10.5 %all-to-all-start = ((s32[128,1,1]{2,1,0:T(1,128)}), s32[128,1,1]{2,1,0:T(1,128)S(1)}, u32[]{:S(2)}, u32[]{:S(2)}) async-start(s32[128,1,1]{2,1,0:T(1,128)} %copy.33), calls=%async_computation | async-start | bytes 131072 | tf_op jit(solution)/shard_map/all_to_all | solution.py:180
  13.8 1.2 broadcast_clamp_fusion.2.rhome_ref
  15.1 1.3 scatter_custom_fusion.1.spair_ref
  16.4 1.3 scatter_custom_fusion.2.sused_ref
  17.7 3.6 all-to-all-done
  21.3 2.9 clamp_reduce_fusion.picked_ref
  24.2 13.1 %shard_map.112 = bf16[128,256,256]{2,1,0:T(8,128)(2,1)} custom-call(s32[128]{0:T(128)} %clamp_reduce_fusion.picked_ref, s32[128]{0:T(128)} %scatter_custom_fusion.1.spair_ref, s32[128]{0:T(128)} %scatter_custom_fusion.2.sused_ref, s32[64]{0:T(128)} %broadcast_clamp_fusion.2.rhome_ref, bf16[16,128,256]{2,1,0:T(8,128)(2,1)} %bitcast.22, ...), custom_call_target="tpu_custom_call" | custom-call | flops 1073741824 | bytes 19922944 | tf_op jit(solution)/shard_map/pallas_call | solution.py:109
  37.4 7.7 all-to-all-start.1
  45.1 2.1 sort.62
  47.2 2.1 sort.64
  49.3 0.1 convert_reduce_fusion.1
  49.6 0.1 reduce.4
  49.7 2.1 sort.65
  51.8 0.1 convert_reduce_fusion
  52.1 0.1 reduce.5
  52.2 0.1 convert_reduce_fusion.3
  52.4 0.1 reduce
  52.5 0.7 pad_add_fusion
  53.2 1.5 broadcast_in_dim.13.init_ref
  54.7 27.1 %shard_map.113.base_ref = f32[16,128,256]{2,1,0:T(8,128)} custom-call(s32[17]{0:T(128)} %get-tuple-element.19.hs_ref, s32[64]{0:T(128)} %get-tuple-element.9.ho_ref, s32[17]{0:T(128)} %get-tuple-element.18.ns_ref, s32[64]{0:T(128)} %get-tuple-element.10.no_ref, s32[64]{0:T(128)} %copy-done.5, s32[64]{0:T(128)} %copy-done.6, bf16[16,128,256]{2,1,0:T(8,128)(2,1)} %bitcast.23, ...), custom_call_target="tpu_custom_call" | custom-call | flops 1073741824 | bytes 7340032 | tf_op jit(solution)/shard_map/pallas_call | solution.py:66
  81.8 2.4 compare_reduce_fusion
  84.2 2.6 sort.63
  87.1 0.1 reduce.3
  87.2 0.6 pad_add_fusion.2
  87.8 230.7 %all-to-all-done.1.recv_ref = bf16[128,256,256]{2,1,0:T(8,128)(2,1)} async-done(((bf16[128,256,256]{2,1,0:T(8,128)(2,1)}), bf16[128,256,256]{2,1,0:T(8,128)(2,1)}, u32[]{:S(2)}, u32[]{:S(2)}) %all-to-all-start.1) | async-done | bytes 16777248 | tf_op jit(solution)/shard_map/all_to_all | solution.py:193
  318.6 20.0 %shard_map.114 = f32[16,128,256]{2,1,0:T(8,128)} custom-call(s32[17]{0:T(128)} %get-tuple-element.21.rs_ref, s32[64]{0:T(128)} %get-tuple-element.7.ro_ref, s32[64]{0:T(128)} %get-tuple-element.14.td_ref, s32[17]{0:T(128)} %get-tuple-element.20.ss_ref, s32[128]{0:T(128)} %get-tuple-element.8.so_ref, ...), custom_call_target="tpu_custom_call", output_to_operand_aliasing={{}: (7, {})} | custom-call | flops 536870912 | bytes 23068672 | tf_op jit(solution)/shard_map/pallas_call | solution.py:149
  338.5 1.9 convert_element_type.44
  340.4 0.3 copy-done.7
  340.7 2.3 multiply_convert_fusion
  343.0 0.7 fusion
  343.7 2.8 fusion.13
  346.5 0.1 reshape.157
  346.7 0.1 subtract_convert_fusion
  346.8 2.7 slice.32
  349.5 1.1 pad_maximum_fusion.3.rest_0_
  350.6 13.8 %shard_map.115 = bf16[128,264,256]{2,1,0:T(8,128)(2,1)} custom-call(s32[128]{0:T(128)} %clamp_reduce_fusion.picked_ref, s32[128]{0:T(128)} %scatter_custom_fusion.1.spair_ref, s32[128]{0:T(128)} %scatter_custom_fusion.2.sused_ref, s32[64]{0:T(128)} %broadcast_clamp_fusion.2.rhome_ref, bf16[16,128,256]{2,1,0:T(8,128)(2,1)} %bitcast.18, ...), custom_call_target="tpu_custom_call" | custom-call | flops 1073741824 | bytes 20447232 | tf_op jit(solution)/shard_map/pallas_call | solution.py:109
  364.4 4.9 all-to-all-start.2
  369.3 3.0 slice.25
  372.3 27.1 %shard_map.116.base_ref = f32[16,128,256]{2,1,0:T(8,128)} custom-call(s32[17]{0:T(128)} %get-tuple-element.19.hs_ref, s32[64]{0:T(128)} %get-tuple-element.9.ho_ref, s32[17]{0:T(128)} %get-tuple-element.18.ns_ref, s32[64]{0:T(128)} %get-tuple-element.10.no_ref, s32[64]{0:T(128)} %copy-done.5, s32[64]{0:T(128)} %copy-done.6, bf16[16,128,256]{2,1,0:T(8,128)(2,1)} %bitcast.19, ...), custom_call_target="tpu_custom_call" | custom-call | flops 1073741824 | bytes 7340032 | tf_op jit(solution)/shard_map/pallas_call | solution.py:66
  399.4 244.7 %all-to-all-done.2.recv_ref = bf16[128,264,256]{2,1,0:T(8,128)(2,1)} async-done(((bf16[128,264,256]{2,1,0:T(8,128)(2,1)}), bf16[128,264,256]{2,1,0:T(8,128)(2,1)}, u32[]{:S(2)}, u32[]{:S(2)}) %all-to-all-start.2) | async-done | bytes 17301536 | tf_op jit(solution)/shard_map/all_to_all | solution.py:193
  644.1 1.1 slice_convert_fusion.1
  645.3 0.2 fusion.2
  645.5 296.1 %all-gather = f32[128,4,256]{2,1,0:T(4,128)S(1)} all-gather(f32[1,4,256]{2,1,0:T(4,128)S(1)} %bitcast.26), channel_id=1, replica_groups=mesh['group'=2,'member'=64] {'group','member'}, dimensions={0}, use_global_device_ids=true | all-gather | bytes 528384 | tf_op jit(solution)/shard_map/all_gather | solution.py:221
  941.6 1.0 reshape.190
  942.6 20.2 %shard_map.117 = f32[16,128,256]{2,1,0:T(8,128)} custom-call(s32[17]{0:T(128)} %get-tuple-element.21.rs_ref, s32[64]{0:T(128)} %get-tuple-element.7.ro_ref, s32[64]{0:T(128)} %get-tuple-element.14.td_ref, s32[17]{0:T(128)} %get-tuple-element.20.ss_ref, s32[128]{0:T(128)} %get-tuple-element.8.so_ref, ...), custom_call_target="tpu_custom_call", output_to_operand_aliasing={{}: (7, {})} | custom-call | flops 536870912 | bytes 23592960 | tf_op jit(solution)/shard_map/pallas_call | solution.py:149
  (38 shorter events, 0.8 us)
Async XLA Ops:
  0.6 339.8 %copy-start = (bf16[512,256]{1,0:T(8,128)(2,1)S(1)}, bf16[512,256]{1,0:T(8,128)(2,1)}, u32[]{:S(2)}) copy-start(bf16[512,256]{1,0:T(8,128)(2,1)} %param.16) | copy-start | bytes 786436
  3.4 17.9 %all-to-all-start = ((s32[128,1,1]{2,1,0:T(1,128)}), s32[128,1,1]{2,1,0:T(1,128)S(1)}, u32[]{:S(2)}, u32[]{:S(2)}) async-start(s32[128,1,1]{2,1,0:T(1,128)} %copy.33), calls=%async_computation | async-start | bytes 131072 | tf_op jit(solution)/shard_map/all_to_all | solution.py:180
  37.4 7.7 copy-start.4
  37.4 9.8 %copy-start.8 = (s32[64]{0:T(128)S(1)}, s32[64]{0:T(128)}, u32[]{:S(2)}) copy-start(s32[64]{0:T(128)} %param.10) | copy-start | bytes 772
  37.4 12.3 %copy-start.9 = (s32[64]{0:T(128)S(1)}, s32[64]{0:T(128)}, u32[]{:S(2)}) copy-start(s32[64]{0:T(128)} %param.11) | copy-start | bytes 772
  37.4 281.2 %all-to-all-start.1 = ((bf16[128,256,256]{2,1,0:T(8,128)(2,1)}), bf16[128,256,256]{2,1,0:T(8,128)(2,1)}, u32[]{:S(2)}, u32[]{:S(2)}) async-start(bf16[128,256,256]{2,1,0:T(8,128)(2,1)} %shard_map.112), calls=%async_computation.1 | async-start | bytes 33554432 | tf_op jit(solution)/shard_map/all_to_all | solution.py:193
  47.2 7.5 copy-start.5
  49.7 5.1 copy-start.6
  54.7 29.5 %copy-start.3 = (s32[128]{0:T(128)S(1)}, s32[128]{0:T(128)}, u32[]{:S(2)}) copy-start(s32[128]{0:T(128)} %clamp_reduce_fusion.picked_ref) | copy-start | bytes 1540
  338.5 1.9 copy-start.2
  338.5 2.2 copy-start.7
  364.4 279.7 %all-to-all-start.2 = ((bf16[128,264,256]{2,1,0:T(8,128)(2,1)}), bf16[128,264,256]{2,1,0:T(8,128)(2,1)}, u32[]{:S(2)}, u32[]{:S(2)}) async-start(bf16[128,264,256]{2,1,0:T(8,128)(2,1)} %shard_map.115), calls=%async_computation.2 | async-start | bytes 34603008 | tf_op jit(solution)/shard_map/all_to_all | solution.py:193
  942.6 20.2 %copy-start.1 = (bf16[512,256]{1,0:T(8,128)(2,1)S(1)}, bf16[512,256]{1,0:T(8,128)(2,1)}, u32[]{:S(2)}) copy-start(bf16[512,256]{1,0:T(8,128)(2,1)} %param.16) | copy-start | bytes 786436

commit v4 on v3

--- a/solution.py
+++ b/solution.py
@@ -208,8 +208,9 @@
     rows = partial_grad.shape[0]
     chunk = rows // device_count
     pieces = partial_grad.reshape(device_count, chunk, F)
-    pieces_hi = pieces.astype(jnp.bfloat16)
-    pieces_lo = (pieces - pieces_hi.astype(jnp.float32)).astype(jnp.bfloat16)
+    hi_f32 = lax.reduce_precision(pieces, exponent_bits=8, mantissa_bits=7)
+    pieces_hi = hi_f32.astype(jnp.bfloat16)
+    pieces_lo = (pieces - hi_f32).astype(jnp.bfloat16)
     extra = jnp.concatenate([pieces_hi, pieces_lo], axis=1)
     grad_joined = jnp.einsum("rf,af->ra", grad_pre, weight, preferred_element_type=jnp.float32)
     grad_agg = grad_joined[:, F:].astype(jnp.bfloat16).reshape(own_blocks, BLOCK, F)
@@ -217,8 +218,11 @@
     grad_features, recv_b = apply_graph(grad_agg, init_b, extra)
     got = recv_b[:, 2 * BLOCK:, :].astype(jnp.float32)
     mine = jnp.sum(got[:, :chunk] + got[:, chunk:], axis=0)
+    mine, grad_features = lax.optimization_barrier((mine, grad_features))
     grad_scale = 1.0 / math.sqrt(row_count * device_count)
-    grad_weight = lax.all_gather(mine, AXES, axis=0, tiled=True) * grad_scale
+    spread_out = jnp.broadcast_to(mine[None], (device_count, chunk, F))
+    gathered = lax.all_to_all(spread_out, AXES, split_axis=0, concat_axis=0, tiled=True)
+    grad_weight = gathered.reshape(rows, F) * grad_scale
     return (output, grad_weight, grad_features)
 
 

time: 980 us -> 699 us (0.71)
  blocking collectives: 296 us -> 19.8 us
    all_gather x1 -> x0, blocking collectives: 296 us -> none  [body(): grad_weight = lax.all_gather(mine, AXES, axis=0, tiled=True) * grad_scale]
    all_to_all x0 -> x1, blocking collectives: none -> 19.8 us  [body(): lax.all_to_all(spread_out, AXES, split_axis=0, concat_axis=0, tiled=True)]
  transfers between devices with their start and end apart: 3 -> 3, of which waited for: 3 -> 3; matrix products, arithmetic and copies ran while one was open for 2% -> 3% of each run, Pallas kernels for 6% -> 8%
where the time goes in v4:
time: 699 us; the launch traced here: 687 us
  waiting for transfers between devices  479 us (69%)
  Pallas kernels  122 us (17%)
  other arithmetic  23.5 us (3%)
  starting transfers between devices  23.1 us (3%)
  blocking collectives  19.8 us (3%)
  local copies, waits for them, and re-layouts  13.3 us (2%)
    all_to_all x2, waiting for transfers between devices, apply_graph(): recv = lax.all_to_all(send, AXES, split_axis=0, concat_axis=0, tiled=True)  475 us
    pallas_call x2, Pallas kernels, local_sum(): pl.pallas_call(_local_kernel, out_shape=jax.ShapeDtypeStruct(init.shape,...  54.3 us
    pallas_call x2, Pallas kernels, post_sum(): pl.pallas_call(_post_kernel, out_shape=jax.ShapeDtypeStruct(base.shape, j...  40.4 us
    pallas_call x2, Pallas kernels, build_send(): pl.pallas_call(_send_kernel, grid=(slots // SEND_GROUP,), out_shape=jax.S...  26.9 us
    all_to_all x1, blocking collectives, body(): lax.all_to_all(spread_out, AXES, split_axis=0, concat_axis=0, tiled=True)  19.8 us
  transfers between devices with their start and end apart: 3, of which 3 were waited for; matrix products, arithmetic and copies ran while one was open for 3% of the time, Pallas kernels for 8%

profile of v4, /device:TPU:41, one launch (start us, length us, event | category | flops | bytes accessed | tf_op | source)
XLA Modules:
  0.0 686.9 jit_solution(11759296151206985989)
XLA Ops:
  0.6 1.2 compare_select_fusion
  1.8 0.8 scatter_custom_fusion
  2.6 0.7 copy.33
  3.4 10.5 %all-to-all-start = ((s32[128,1,1]{2,1,0:T(1,128)}), s32[128,1,1]{2,1,0:T(1,128)S(1)}, u32[]{:S(2)}, u32[]{:S(2)}) async-start(s32[128,1,1]{2,1,0:T(1,128)} %copy.33), calls=%async_computation | async-start | bytes 131072 | tf_op jit(solution)/shard_map/all_to_all | solution.py:180
  13.8 1.2 broadcast_clamp_fusion.2.rhome_ref
  15.1 1.3 scatter_custom_fusion.1.spair_ref
  16.4 1.3 scatter_custom_fusion.2.sused_ref
  17.7 3.6 all-to-all-done
  21.3 2.9 clamp_reduce_fusion.picked_ref
  24.2 13.1 %shard_map.112 = bf16[128,256,256]{2,1,0:T(8,128)(2,1)} custom-call(s32[128]{0:T(128)} %clamp_reduce_fusion.picked_ref, s32[128]{0:T(128)} %scatter_custom_fusion.1.spair_ref, s32[128]{0:T(128)} %scatter_custom_fusion.2.sused_ref, s32[64]{0:T(128)} %broadcast_clamp_fusion.2.rhome_ref, bf16[16,128,256]{2,1,0:T(8,128)(2,1)} %bitcast.21, ...), custom_call_target="tpu_custom_call" | custom-call | flops 1073741824 | bytes 19922944 | tf_op jit(solution)/shard_map/pallas_call | solution.py:109
  37.4 7.7 %all-to-all-start.1 = ((bf16[128,256,256]{2,1,0:T(8,128)(2,1)}), bf16[128,256,256]{2,1,0:T(8,128)(2,1)}, u32[]{:S(2)}, u32[]{:S(2)}) async-start(bf16[128,256,256]{2,1,0:T(8,128)(2,1)} %shard_map.112), calls=%async_computation.1 | async-start | bytes 33554432 | tf_op jit(solution)/shard_map/all_to_all | solution.py:193
  45.1 2.1 sort.62
  47.2 2.1 sort.64
  49.3 0.1 convert_reduce_fusion.1
  49.6 0.1 reduce.4
  49.7 2.1 sort.65
  51.8 0.1 convert_reduce_fusion
  52.1 0.1 reduce.5
  52.2 0.1 convert_reduce_fusion.3
  52.4 0.1 reduce
  52.5 0.7 pad_add_fusion
  53.2 1.5 broadcast_in_dim.15.init_ref
  54.7 27.1 %shard_map.113.base_ref = f32[16,128,256]{2,1,0:T(8,128)} custom-call(s32[17]{0:T(128)} %get-tuple-element.23.hs_ref, s32[64]{0:T(128)} %get-tuple-element.11.ho_ref, s32[17]{0:T(128)} %get-tuple-element.22.ns_ref, s32[64]{0:T(128)} %get-tuple-element.12.no_ref, s32[64]{0:T(128)} %copy-done.5, s32[64]{0:T(128)} %copy-done.6, bf16[16,128,256]{2,1,0:T(8,128)(2,1)} %bitcast.22, ...), custom_call_target="tpu_custom_call" | custom-call | flops 1073741824 | bytes 7340032 | tf_op jit(solution)/shard_map/pallas_call | solution.py:66
  81.9 2.4 compare_reduce_fusion
  84.3 2.6 sort.63
  87.1 0.1 reduce.3
  87.2 0.6 pad_add_fusion.2
  87.9 230.7 %all-to-all-done.1.recv_ref = bf16[128,256,256]{2,1,0:T(8,128)(2,1)} async-done(((bf16[128,256,256]{2,1,0:T(8,128)(2,1)}), bf16[128,256,256]{2,1,0:T(8,128)(2,1)}, u32[]{:S(2)}, u32[]{:S(2)}) %all-to-all-start.1) | async-done | bytes 16777248 | tf_op jit(solution)/shard_map/all_to_all | solution.py:193
  318.6 20.1 %shard_map.114 = f32[16,128,256]{2,1,0:T(8,128)} custom-call(s32[17]{0:T(128)} %get-tuple-element.25.rs_ref, s32[64]{0:T(128)} %get-tuple-element.9.ro_ref, s32[64]{0:T(128)} %get-tuple-element.16.td_ref, s32[17]{0:T(128)} %get-tuple-element.24.ss_ref, s32[128]{0:T(128)} %get-tuple-element.10.so_ref, ...), custom_call_target="tpu_custom_call", output_to_operand_aliasing={{}: (7, {})} | custom-call | flops 536870912 | bytes 23068672 | tf_op jit(solution)/shard_map/pallas_call | solution.py:149
  338.7 1.9 convert_element_type.41
  340.6 0.3 copy-done.7
  340.8 2.3 multiply_convert_fusion
  343.1 0.7 fusion
  343.9 2.8 fusion.14
  346.7 0.1 reshape.161
  346.9 0.2 reduce-precision_convert_fusion
  347.0 2.7 slice.32
  349.7 1.1 pad_maximum_fusion.3.rest_0_
  350.8 13.8 %shard_map.115 = bf16[128,264,256]{2,1,0:T(8,128)(2,1)} custom-call(s32[128]{0:T(128)} %clamp_reduce_fusion.picked_ref, s32[128]{0:T(128)} %scatter_custom_fusion.1.spair_ref, s32[128]{0:T(128)} %scatter_custom_fusion.2.sused_ref, s32[64]{0:T(128)} %broadcast_clamp_fusion.2.rhome_ref, bf16[16,128,256]{2,1,0:T(8,128)(2,1)} %bitcast.17, ...), custom_call_target="tpu_custom_call" | custom-call | flops 1073741824 | bytes 20447232 | tf_op jit(solution)/shard_map/pallas_call | solution.py:109
  364.6 4.9 all-to-all-start.2
  369.5 3.0 slice.25
  372.5 27.1 %shard_map.116.base_ref = f32[16,128,256]{2,1,0:T(8,128)} custom-call(s32[17]{0:T(128)} %get-tuple-element.23.hs_ref, s32[64]{0:T(128)} %get-tuple-element.11.ho_ref, s32[17]{0:T(128)} %get-tuple-element.22.ns_ref, s32[64]{0:T(128)} %get-tuple-element.12.no_ref, s32[64]{0:T(128)} %copy-done.5, s32[64]{0:T(128)} %copy-done.6, bf16[16,128,256]{2,1,0:T(8,128)(2,1)} %bitcast.18, ...), custom_call_target="tpu_custom_call" | custom-call | flops 1073741824 | bytes 7340032 | tf_op jit(solution)/shard_map/pallas_call | solution.py:66
  399.7 244.6 %all-to-all-done.2.recv_ref = bf16[128,264,256]{2,1,0:T(8,128)(2,1)} async-done(((bf16[128,264,256]{2,1,0:T(8,128)(2,1)}), bf16[128,264,256]{2,1,0:T(8,128)(2,1)}, u32[]{:S(2)}, u32[]{:S(2)}) %all-to-all-start.2) | async-done | bytes 17301536 | tf_op jit(solution)/shard_map/all_to_all | solution.py:193
  644.3 1.1 slice_convert_fusion.1
  645.4 0.2 fusion.3
  645.6 20.3 %shard_map.117 = f32[16,128,256]{2,1,0:T(8,128)} custom-call(s32[17]{0:T(128)} %get-tuple-element.25.rs_ref, s32[64]{0:T(128)} %get-tuple-element.9.ro_ref, s32[64]{0:T(128)} %get-tuple-element.16.td_ref, s32[17]{0:T(128)} %get-tuple-element.24.ss_ref, s32[128]{0:T(128)} %get-tuple-element.10.so_ref, ...), custom_call_target="tpu_custom_call", output_to_operand_aliasing={{}: (7, {})} | custom-call | flops 536870912 | bytes 23592960 | tf_op jit(solution)/shard_map/pallas_call | solution.py:149
  666.0 19.8 %all_to_all.24 = f32[128,4,256]{2,1,0:T(4,128)S(1)} all-to-all(f32[128,4,256]{2,1,0:T(4,128)S(1)} %broadcast_in_dim.16), channel_id=1, replica_groups=mesh['group'=2,'member'=64] {'group','member'}, dimensions={0} | all-to-all | bytes 1048576 | tf_op jit(solution)/shard_map/all_to_all | solution.py:224
  685.9 1.0 mul.27
  (39 shorter events, 0.9 us)
Async XLA Ops:
  0.6 339.9 %copy-start = (bf16[512,256]{1,0:T(8,128)(2,1)S(1)}, bf16[512,256]{1,0:T(8,128)(2,1)}, u32[]{:S(2)}) copy-start(bf16[512,256]{1,0:T(8,128)(2,1)} %param.16) | copy-start | bytes 786436
  3.4 17.9 %all-to-all-start = ((s32[128,1,1]{2,1,0:T(1,128)}), s32[128,1,1]{2,1,0:T(1,128)S(1)}, u32[]{:S(2)}, u32[]{:S(2)}) async-start(s32[128,1,1]{2,1,0:T(1,128)} %copy.33), calls=%async_computation | async-start | bytes 131072 | tf_op jit(solution)/shard_map/all_to_all | solution.py:180
  37.4 7.7 %copy-start.4 = (s32[64]{0:T(128)S(1)}, s32[64]{0:T(128)}, u32[]{:S(2)}) copy-start(s32[64]{0:T(128)} %broadcast_clamp_fusion.2.rhome_ref) | copy-start | bytes 772
  37.4 9.8 %copy-start.8 = (s32[64]{0:T(128)S(1)}, s32[64]{0:T(128)}, u32[]{:S(2)}) copy-start(s32[64]{0:T(128)} %param.10) | copy-start | bytes 772
  37.4 12.3 %copy-start.9 = (s32[64]{0:T(128)S(1)}, s32[64]{0:T(128)}, u32[]{:S(2)}) copy-start(s32[64]{0:T(128)} %param.11) | copy-start | bytes 772
  37.4 281.2 %all-to-all-start.1 = ((bf16[128,256,256]{2,1,0:T(8,128)(2,1)}), bf16[128,256,256]{2,1,0:T(8,128)(2,1)}, u32[]{:S(2)}, u32[]{:S(2)}) async-start(bf16[128,256,256]{2,1,0:T(8,128)(2,1)} %shard_map.112), calls=%async_computation.1 | async-start | bytes 33554432 | tf_op jit(solution)/shard_map/all_to_all | solution.py:193
  47.2 7.5 %copy-start.5 = (s32[64]{0:T(128)}, s32[64]{0:T(128)S(1)}, u32[]{:S(2)}) copy-start(s32[64]{0:T(128)S(1)} %broadcast_clamp_fusion.1.lh_ref) | copy-start | bytes 772
  49.7 5.1 copy-start.6
  54.7 29.5 %copy-start.3 = (s32[128]{0:T(128)S(1)}, s32[128]{0:T(128)}, u32[]{:S(2)}) copy-start(s32[128]{0:T(128)} %clamp_reduce_fusion.picked_ref) | copy-start | bytes 1540
  338.7 1.9 copy-start.2
  338.7 2.2 copy-start.7
  364.6 279.7 %all-to-all-start.2 = ((bf16[128,264,256]{2,1,0:T(8,128)(2,1)}), bf16[128,264,256]{2,1,0:T(8,128)(2,1)}, u32[]{:S(2)}, u32[]{:S(2)}) async-start(bf16[128,264,256]{2,1,0:T(8,128)(2,1)} %shard_map.115), calls=%async_computation.2 | async-start | bytes 34603008 | tf_op jit(solution)/shard_map/all_to_all | solution.py:193
  645.6 41.2 %copy-start.1 = (bf16[512,256]{1,0:T(8,128)(2,1)S(1)}, bf16[512,256]{1,0:T(8,128)(2,1)}, u32[]{:S(2)}) copy-start(bf16[512,256]{1,0:T(8,128)(2,1)} %param.16) | copy-start | bytes 786436

commit v5 on v4

--- a/solution.py
+++ b/solution.py
@@ -11,6 +11,7 @@
 BLOCK = 128
 BLK_DEV = 16
 AXES = ("group", "member")
+SLOT_AXES = ("member", "group")
 VMEM_LIMIT = 56 * 1024 * 1024
 
 
@@ -33,23 +34,43 @@
     return order, starts
 
 
+def _pair_loop(lo, hi, term, acc):
+    count = hi - lo
+    iters = (count + 1) // 2
+
+    def step(i, a):
+        i0 = lo + 2 * i
+        i1 = i0 + 1
+        return a + term(i0, jnp.minimum(i1, hi - 1), i1 < hi)
+
+    return lax.fori_loop(0, iters, step, acc)
+
+
 def _local_kernel(hs_ref, ho_ref, ns_ref, no_ref, lh_ref, ln_ref, x_ref, lt_ref, init_ref, out_ref):
     blocks = out_ref.shape[0]
 
     def per_block(k, c):
         acc = init_ref[k]
 
-        def home_term(i, a):
-            p = ho_ref[i]
-            return a + jnp.dot(lt_ref[p], x_ref[ln_ref[p]], preferred_element_type=jnp.float32)
-
-        acc = lax.fori_loop(hs_ref[k], hs_ref[k + 1], home_term, acc)
-
-        def near_term(i, a):
-            p = no_ref[i]
-            return a + _dot_t(lt_ref[p], x_ref[lh_ref[p]])
-
-        acc = lax.fori_loop(ns_ref[k], ns_ref[k + 1], near_term, acc)
+        def home_term(i0, i1, ok):
+            p0 = ho_ref[i0]
+            p1 = ho_ref[i1]
+            lhs = jnp.concatenate([lt_ref[p0], lt_ref[p1]], axis=1)
+            v1 = jnp.where(ok, x_ref[ln_ref[p1]], jnp.zeros((BLOCK, F), x_ref.dtype))
+            rhs = jnp.concatenate([x_ref[ln_ref[p0]], v1], axis=0)
+            return jnp.dot(lhs, rhs, preferred_element_type=jnp.float32)
+
+        acc = _pair_loop(hs_ref[k], hs_ref[k + 1], home_term, acc)
+
+        def near_term(i0, i1, ok):
+            p0 = no_ref[i0]
+            p1 = no_ref[i1]
+            lhs = jnp.concatenate([lt_ref[p0], lt_ref[p1]], axis=0)
+            v1 = jnp.where(ok, x_ref[lh_ref[p1]], jnp.zeros((BLOCK, F), x_ref.dtype))
+            rhs = jnp.concatenate([x_ref[lh_ref[p0]], v1], axis=0)
+            return _dot_t(lhs, rhs)
+
+        acc = _pair_loop(ns_ref[k], ns_ref[k + 1], near_term, acc)
         out_ref[k] = acc
         return c
 
@@ -123,11 +144,15 @@
     def per_block(k, c):
         acc = base_ref[k]
 
-        def remote_term(i, a):
-            p = ro_ref[i]
-            return a + jnp.dot(rt_ref[p], recv_ref[td_ref[p], pl.ds(0, BLOCK)], preferred_element_type=jnp.float32)
-
-        acc = lax.fori_loop(rs_ref[k], rs_ref[k + 1], remote_term, acc)
+        def remote_term(i0, i1, ok):
+            p0 = ro_ref[i0]
+            p1 = ro_ref[i1]
+            lhs = jnp.concatenate([rt_ref[p0], rt_ref[p1]], axis=1)
+            v1 = jnp.where(ok, recv_ref[td_ref[p1], pl.ds(0, BLOCK)], jnp.zeros((BLOCK, F), recv_ref.dtype))
+            rhs = jnp.concatenate([recv_ref[td_ref[p0], pl.ds(0, BLOCK)], v1], axis=0)
+            return jnp.dot(lhs, rhs, preferred_element_type=jnp.float32)
+
+        acc = _pair_loop(rs_ref[k], rs_ref[k + 1], remote_term, acc)
 
         def back_term(i, a):
             return a + recv_ref[so_ref[i], pl.ds(BLOCK, BLOCK)].astype(jnp.float32)
@@ -178,11 +203,18 @@
     wanted = remote_far % BLK_DEV
     request = jnp.full((device_count,), -1, jnp.int32).at[target_dev].set(wanted)
     asked = lax.all_to_all(request, AXES, split_axis=0, concat_axis=0, tiled=True)
-    picked = jnp.clip(asked, 0, own_blocks - 1)
-    back_dest = jnp.where(asked >= 0, picked, own_blocks)
-    slot_pair = jnp.zeros((device_count,), jnp.int32).at[target_dev].set(
+    picked_dev = jnp.clip(asked, 0, own_blocks - 1)
+    back_dev = jnp.where(asked >= 0, picked_dev, own_blocks)
+    groups = lax.axis_size("group")
+    members = lax.axis_size("member")
+    slot_ids = jnp.arange(device_count, dtype=jnp.int32)
+    dev_of_slot = (slot_ids % groups) * members + slot_ids // groups
+    target_slot = (target_dev % members) * groups + target_dev // members
+    picked = picked_dev[dev_of_slot]
+    back_dest = back_dev[dev_of_slot]
+    slot_pair = jnp.zeros((device_count,), jnp.int32).at[target_slot].set(
         jnp.arange(target_dev.shape[0], dtype=jnp.int32))
-    slot_used = jnp.zeros((device_count,), jnp.int32).at[target_dev].set(1)
+    slot_used = jnp.zeros((device_count,), jnp.int32).at[target_slot].set(1)
     h_order, h_starts = _lists(lhome, own_blocks)
     n_order, n_starts = _lists(lnear, own_blocks)
     r_order, r_starts = _lists(rhome, own_blocks)
@@ -190,9 +222,9 @@
 
     def apply_graph(blocks_in, init, extra=None):
         send = build_send(picked, slot_pair, slot_used, rhome, blocks_in, remote_tiles, extra)
-        recv = lax.all_to_all(send, AXES, split_axis=0, concat_axis=0, tiled=True)
+        recv = lax.all_to_all(send, SLOT_AXES, split_axis=0, concat_axis=0, tiled=True)
         part = local_sum(h_starts, h_order, n_starts, n_order, lhome, lnear, blocks_in, local_tiles, init)
-        total = post_sum(r_starts, r_order, target_dev, s_starts, s_order, remote_tiles, recv, part)
+        total = post_sum(r_starts, r_order, target_slot, s_starts, s_order, remote_tiles, recv, part)
         return total.reshape(row_count, F), recv
 
     zeros = jnp.zeros((own_blocks, BLOCK, F), jnp.float32)
@@ -207,7 +239,7 @@
     partial_grad = jnp.einsum("ra,rf->af", joined, grad_pre, preferred_element_type=jnp.float32)
     rows = partial_grad.shape[0]
     chunk = rows // device_count
-    pieces = partial_grad.reshape(device_count, chunk, F)
+    pieces = partial_grad.reshape(device_count, chunk, F)[dev_of_slot]
     hi_f32 = lax.reduce_precision(pieces, exponent_bits=8, mantissa_bits=7)
     pieces_hi = hi_f32.astype(jnp.bfloat16)
     pieces_lo = (pieces - hi_f32).astype(jnp.bfloat16)

time: 699 us -> 625 us (0.89)
  waiting for transfers between devices: 479 us -> 408 us
  Pallas kernels: 122 us -> 96 us
  blocking collectives: 19.8 us -> 34.7 us
  starting transfers between devices: 23.1 us -> 33.8 us
    all_to_all x2, waiting for transfers between devices: 475 us -> 404 us  [apply_graph(): lax.all_to_all(send, SLOT_AXES, split_axis=0, concat_axis=0, tiled=True)]
    pallas_call x2, Pallas kernels: 54.3 us -> 35.7 us  [local_sum(): pl.pallas_call(_local_kernel, out_shape=jax.ShapeDtypeStruct(init.shape,...]
    all_to_all x1, blocking collectives: 19.8 us -> 34.7 us  [body(): lax.all_to_all(spread_out, AXES, split_axis=0, concat_axis=0, tiled=True)]
    all_to_all x2, starting transfers between devices: 12.6 us -> 23.3 us  [apply_graph(): lax.all_to_all(send, SLOT_AXES, split_axis=0, concat_axis=0, tiled=True)]
    pallas_call x2, Pallas kernels: 40.4 us -> 33.3 us  [post_sum(): pl.pallas_call(_post_kernel, out_shape=jax.ShapeDtypeStruct(base.shape, j...]
  transfers between devices with their start and end apart: 3 -> 3, of which waited for: 3 -> 3; matrix products, arithmetic and copies ran while one was open for 3% -> 4% of each run, Pallas kernels for 8% -> 6%
where the time goes in v5:
time: 625 us; the launch traced here: 619 us
  waiting for transfers between devices  408 us (65%)
  Pallas kernels  96 us (15%)
  blocking collectives  34.7 us (6%)
  starting transfers between devices  33.8 us (5%)
  other arithmetic  23 us (4%)
  local copies, waits for them, and re-layouts  17.2 us (3%)
    all_to_all x2, waiting for transfers between devices, apply_graph(): lax.all_to_all(send, SLOT_AXES, split_axis=0, concat_axis=0, tiled=True)  404 us
    pallas_call x2, Pallas kernels, local_sum(): pl.pallas_call(_local_kernel, out_shape=jax.ShapeDtypeStruct(init.shape,...  35.7 us
    all_to_all x1, blocking collectives, body(): lax.all_to_all(spread_out, AXES, split_axis=0, concat_axis=0, tiled=True)  34.7 us
    pallas_call x2, Pallas kernels, post_sum(): pl.pallas_call(_post_kernel, out_shape=jax.ShapeDtypeStruct(base.shape, j...  33.3 us
    pallas_call x2, Pallas kernels, build_send(): pl.pallas_call(_send_kernel, grid=(slots // SEND_GROUP,), out_shape=jax.S...  26.9 us
    all_to_all x2, starting transfers between devices, apply_graph(): lax.all_to_all(send, SLOT_AXES, split_axis=0, concat_axis=0, tiled=True)  23.3 us
  transfers between devices with their start and end apart: 3, of which 3 were waited for; matrix products, arithmetic and copies ran while one was open for 4% of the time, Pallas kernels for 6%

profile of v5, /device:TPU:41, one launch (start us, length us, event | category | flops | bytes accessed | tf_op | source)
XLA Modules:
  0.0 619.0 jit_solution(1222126575106527395)
XLA Ops:
  0.6 1.2 compare_select_fusion
  1.9 0.8 scatter_custom_fusion
  2.6 0.7 copy.33
  3.4 10.5 %all-to-all-start = ((s32[128,1,1]{2,1,0:T(1,128)}), s32[128,1,1]{2,1,0:T(1,128)S(1)}, u32[]{:S(2)}, u32[]{:S(2)}) async-start(s32[128,1,1]{2,1,0:T(1,128)} %copy.33), calls=%async_computation | async-start | bytes 131072 | tf_op jit(solution)/shard_map/all_to_all | solution.py:205
  13.9 1.2 broadcast_clamp_fusion.2.rhome_ref
  15.1 1.3 scatter_custom_fusion.1.spair_ref
  16.5 1.3 scatter_custom_fusion.2.sused_ref
  17.8 3.5 all-to-all-done
  21.3 2.4 clamp_reduce_fusion
  23.7 1.8 gather_fusion.1
  25.4 13.1 %shard_map.112 = bf16[128,256,256]{2,1,0:T(8,128)(2,1)} custom-call(s32[128]{0:T(128)} %gather_fusion.1, s32[128]{0:T(128)} %scatter_custom_fusion.1.spair_ref, s32[128]{0:T(128)} %scatter_custom_fusion.2.sused_ref, s32[64]{0:T(128)} %broadcast_clamp_fusion.2.rhome_ref, bf16[16,128,256]{2,1,0:T(8,128)(2,1)} %bitcast.23, bf16[64,128,128]{2,1,0:T(8,128)(2,1)} %rt_ref.7), custom_call_target="tpu_custom_call" | custom-call | flops 1073741824 | bytes 19922944 | tf_op jit(solution)/shard_map/pallas_call | solution.py:130
  38.6 7.7 %all-to-all-start.1 = ((bf16[128,256,256]{2,1,0:T(8,128)(2,1)}), bf16[128,256,256]{2,1,0:T(8,128)(2,1)}, u32[]{:S(2)}, u32[]{:S(2)}) async-start(bf16[128,256,256]{2,1,0:T(8,128)(2,1)} %shard_map.112), calls=%async_computation.1 | async-start | bytes 33554432 | tf_op jit(solution)/shard_map/all_to_all | solution.py:225
  46.3 2.1 sort.62
  48.4 2.1 sort.64
  50.8 0.1 reduce.4
  50.9 2.1 sort.65
  53.3 0.1 reduce.5
  53.6 0.1 reduce
  53.7 0.7 pad_add_fusion
  54.4 1.5 broadcast_in_dim.18.init_ref
  56.0 17.9 %shard_map.113.base_ref = f32[16,128,256]{2,1,0:T(8,128)} custom-call(s32[17]{0:T(128)} %get-tuple-element.24.hs_ref, s32[64]{0:T(128)} %get-tuple-element.11.ho_ref, s32[17]{0:T(128)} %get-tuple-element.23.ns_ref, s32[64]{0:T(128)} %get-tuple-element.12.no_ref, s32[64]{0:T(128)} %copy-done.4, s32[64]{0:T(128)} %copy-done.5, bf16[16,128,256]{2,1,0:T(8,128)(2,1)} %bitcast.24, ...), custom_call_target="tpu_custom_call" | custom-call | flops 1073741824 | bytes 7340032 | tf_op jit(solution)/shard_map/pallas_call | solution.py:87
  73.8 2.4 compare_reduce_fusion
  76.2 1.2 gather_fusion
  77.4 2.6 sort.63
  80.3 0.1 reduce.3
  80.4 0.6 pad_add_fusion.2
  81.0 194.2 %all-to-all-done.1.recv_ref = bf16[128,256,256]{2,1,0:T(8,128)(2,1)} async-done(((bf16[128,256,256]{2,1,0:T(8,128)(2,1)}), bf16[128,256,256]{2,1,0:T(8,128)(2,1)}, u32[]{:S(2)}, u32[]{:S(2)}) %all-to-all-start.1) | async-done | bytes 16777248 | tf_op jit(solution)/shard_map/all_to_all | solution.py:225
  275.2 16.5 %shard_map.114 = f32[16,128,256]{2,1,0:T(8,128)} custom-call(s32[17]{0:T(128)} %get-tuple-element.26.rs_ref, s32[64]{0:T(128)} %get-tuple-element.9.ro_ref, s32[64]{0:T(128)} %get-tuple-element.16.td_ref, s32[17]{0:T(128)} %get-tuple-element.25.ss_ref, s32[128]{0:T(128)} %get-tuple-element.10.so_ref, ...), custom_call_target="tpu_custom_call", output_to_operand_aliasing={{}: (7, {})} | custom-call | flops 536870912 | bytes 23068672 | tf_op jit(solution)/shard_map/pallas_call | solution.py:174
  291.8 1.9 convert_element_type.41
  293.7 0.3 copy-done.6
  294.0 2.3 multiply_convert_fusion
  296.2 0.7 fusion
  297.0 2.8 fusion.20
  299.8 0.1 reshape.216
  300.0 0.9 gather_fusion.2
  300.9 0.2 reduce-precision_convert_fusion
  301.0 2.7 slice.38
  303.7 1.1 pad_maximum_fusion.3.rest_0_
  304.8 13.8 %shard_map.115 = bf16[128,264,256]{2,1,0:T(8,128)(2,1)} custom-call(s32[128]{0:T(128)} %gather_fusion.1, s32[128]{0:T(128)} %scatter_custom_fusion.1.spair_ref, s32[128]{0:T(128)} %scatter_custom_fusion.2.sused_ref, s32[64]{0:T(128)} %broadcast_clamp_fusion.2.rhome_ref, bf16[16,128,256]{2,1,0:T(8,128)(2,1)} %bitcast.19, bf16[64,128,128]{2,1,0:T(8,128)(2,1)} %rt_ref.7, ...), custom_call_target="tpu_custom_call" | custom-call | flops 1073741824 | bytes 20447232 | tf_op jit(solution)/shard_map/pallas_call | solution.py:130
  318.6 15.6 %all-to-all-start.2 = ((bf16[128,264,256]{2,1,0:T(8,128)(2,1)}), bf16[128,264,256]{2,1,0:T(8,128)(2,1)}, u32[]{:S(2)}, u32[]{:S(2)}) async-start(bf16[128,264,256]{2,1,0:T(8,128)(2,1)} %shard_map.115), calls=%async_computation.2 | async-start | bytes 34603008 | tf_op jit(solution)/shard_map/all_to_all | solution.py:225
  334.2 3.0 slice.31
  337.2 17.9 %shard_map.116.base_ref = f32[16,128,256]{2,1,0:T(8,128)} custom-call(s32[17]{0:T(128)} %get-tuple-element.24.hs_ref, s32[64]{0:T(128)} %get-tuple-element.11.ho_ref, s32[17]{0:T(128)} %get-tuple-element.23.ns_ref, s32[64]{0:T(128)} %get-tuple-element.12.no_ref, s32[64]{0:T(128)} %copy-done.4, s32[64]{0:T(128)} %copy-done.5, bf16[16,128,256]{2,1,0:T(8,128)(2,1)} %bitcast.20, ...), custom_call_target="tpu_custom_call" | custom-call | flops 1073741824 | bytes 7340032 | tf_op jit(solution)/shard_map/pallas_call | solution.py:87
  355.1 209.9 %all-to-all-done.2.recv_ref = bf16[128,264,256]{2,1,0:T(8,128)(2,1)} async-done(((bf16[128,264,256]{2,1,0:T(8,128)(2,1)}), bf16[128,264,256]{2,1,0:T(8,128)(2,1)}, u32[]{:S(2)}, u32[]{:S(2)}) %all-to-all-start.2) | async-done | bytes 17301536 | tf_op jit(solution)/shard_map/all_to_all | solution.py:225
  565.0 1.1 slice_convert_fusion.1
  566.1 0.2 fusion.3
  566.4 16.7 %shard_map.117 = f32[16,128,256]{2,1,0:T(8,128)} custom-call(s32[17]{0:T(128)} %get-tuple-element.26.rs_ref, s32[64]{0:T(128)} %get-tuple-element.9.ro_ref, s32[64]{0:T(128)} %get-tuple-element.16.td_ref, s32[17]{0:T(128)} %get-tuple-element.25.ss_ref, s32[128]{0:T(128)} %get-tuple-element.10.so_ref, ...), custom_call_target="tpu_custom_call", output_to_operand_aliasing={{}: (7, {})} | custom-call | flops 536870912 | bytes 23592960 | tf_op jit(solution)/shard_map/pallas_call | solution.py:174
  583.2 34.7 %all_to_all.24 = f32[128,4,256]{2,1,0:T(4,128)S(1)} all-to-all(f32[128,4,256]{2,1,0:T(4,128)S(1)} %broadcast_in_dim.19), channel_id=1, replica_groups=mesh['group'=2,'member'=64] {'group','member'}, dimensions={0} | all-to-all | bytes 1048576 | tf_op jit(solution)/shard_map/all_to_all | solution.py:256
  618.0 1.0 mul.54
  (43 shorter events, 1.2 us)
Async XLA Ops:
  0.6 293.0 %copy-start = (bf16[512,256]{1,0:T(8,128)(2,1)S(1)}, bf16[512,256]{1,0:T(8,128)(2,1)}, u32[]{:S(2)}) copy-start(bf16[512,256]{1,0:T(8,128)(2,1)} %param.16) | copy-start | bytes 786436
  3.4 17.9 %all-to-all-start = ((s32[128,1,1]{2,1,0:T(1,128)}), s32[128,1,1]{2,1,0:T(1,128)S(1)}, u32[]{:S(2)}, u32[]{:S(2)}) async-start(s32[128,1,1]{2,1,0:T(1,128)} %copy.33), calls=%async_computation | async-start | bytes 131072 | tf_op jit(solution)/shard_map/all_to_all | solution.py:205
  38.6 7.7 %copy-start.3 = (s32[64]{0:T(128)S(1)}, s32[64]{0:T(128)}, u32[]{:S(2)}) copy-start(s32[64]{0:T(128)} %broadcast_clamp_fusion.2.rhome_ref) | copy-start | bytes 772
  38.6 9.8 %copy-start.7 = (s32[64]{0:T(128)S(1)}, s32[64]{0:T(128)}, u32[]{:S(2)}) copy-start(s32[64]{0:T(128)} %param.10) | copy-start | bytes 772
  38.6 12.3 %copy-start.8 = (s32[64]{0:T(128)S(1)}, s32[64]{0:T(128)}, u32[]{:S(2)}) copy-start(s32[64]{0:T(128)} %param.11) | copy-start | bytes 772
  38.6 236.7 %all-to-all-start.1 = ((bf16[128,256,256]{2,1,0:T(8,128)(2,1)}), bf16[128,256,256]{2,1,0:T(8,128)(2,1)}, u32[]{:S(2)}, u32[]{:S(2)}) async-start(bf16[128,256,256]{2,1,0:T(8,128)(2,1)} %shard_map.112), calls=%async_computation.1 | async-start | bytes 33554432 | tf_op jit(solution)/shard_map/all_to_all | solution.py:225
  48.4 7.5 %copy-start.4 = (s32[64]{0:T(128)}, s32[64]{0:T(128)S(1)}, u32[]{:S(2)}) copy-start(s32[64]{0:T(128)S(1)} %broadcast_clamp_fusion.1.lh_ref) | copy-start | bytes 772
  50.9 5.1 copy-start.5
  291.8 1.9 copy-start.2
  291.8 2.2 copy-start.6
  318.6 246.4 %all-to-all-start.2 = ((bf16[128,264,256]{2,1,0:T(8,128)(2,1)}), bf16[128,264,256]{2,1,0:T(8,128)(2,1)}, u32[]{:S(2)}, u32[]{:S(2)}) async-start(bf16[128,264,256]{2,1,0:T(8,128)(2,1)} %shard_map.115), calls=%async_computation.2 | async-start | bytes 34603008 | tf_op jit(solution)/shard_map/all_to_all | solution.py:225
  566.4 52.6 %copy-start.1 = (bf16[512,256]{1,0:T(8,128)(2,1)S(1)}, bf16[512,256]{1,0:T(8,128)(2,1)}, u32[]{:S(2)}) copy-start(bf16[512,256]{1,0:T(8,128)(2,1)} %param.16) | copy-start | bytes 786436

commit v6 on v5

--- a/solution.py
+++ b/solution.py
@@ -46,7 +46,7 @@
     return lax.fori_loop(0, iters, step, acc)
 
 
-def _local_kernel(hs_ref, ho_ref, ns_ref, no_ref, lh_ref, ln_ref, x_ref, lt_ref, init_ref, out_ref):
+def _local_kernel(hs_ref, ho_ref, ns_ref, no_ref, lh_ref, ln_ref, x_ref, lt_ref, ltt_ref, init_ref, out_ref):
     blocks = out_ref.shape[0]
 
     def per_block(k, c):
@@ -65,10 +65,10 @@
         def near_term(i0, i1, ok):
             p0 = no_ref[i0]
             p1 = no_ref[i1]
-            lhs = jnp.concatenate([lt_ref[p0], lt_ref[p1]], axis=0)
+            lhs = jnp.concatenate([ltt_ref[p0], ltt_ref[p1]], axis=1)
             v1 = jnp.where(ok, x_ref[lh_ref[p1]], jnp.zeros((BLOCK, F), x_ref.dtype))
             rhs = jnp.concatenate([x_ref[lh_ref[p0]], v1], axis=0)
-            return _dot_t(lhs, rhs)
+            return jnp.dot(lhs, rhs, preferred_element_type=jnp.float32)
 
         acc = _pair_loop(ns_ref[k], ns_ref[k + 1], near_term, acc)
         out_ref[k] = acc
@@ -77,7 +77,7 @@
     lax.fori_loop(0, blocks, per_block, 0)
 
 
-def local_sum(hs, ho, ns, no, lh, ln, x, ltiles, init):
+def local_sum(hs, ho, ns, no, lh, ln, x, ltiles, lttiles, init):
     pairs = ltiles.shape[0]
     cost = pl.CostEstimate(
         flops=2 * 2 * pairs * BLOCK * BLOCK * F,
@@ -87,25 +87,26 @@
     return pl.pallas_call(
         _local_kernel,
         out_shape=jax.ShapeDtypeStruct(init.shape, jnp.float32),
-        in_specs=[_smem()] * 6 + [_vmem()] * 3,
+        in_specs=[_smem()] * 6 + [_vmem()] * 4,
         out_specs=_vmem(),
         cost_estimate=cost,
         compiler_params=pltpu.CompilerParams(vmem_limit_bytes=VMEM_LIMIT),
-    )(hs, ho, ns, no, lh, ln, x, ltiles, init)
-
-
-SEND_GROUP = 8
+    )(hs, ho, ns, no, lh, ln, x, ltiles, lttiles, init)
+
+
+SEND_GROUP = 16
 
 
 def _send_kernel(picked_ref, spair_ref, sused_ref, rhome_ref, x_ref, rt_ref, *rest):
     send_ref = rest[-1]
     extra_ref = rest[0] if len(rest) == 2 else None
-    base = pl.program_id(0) * SEND_GROUP
-    for j in range(SEND_GROUP):
+    group = send_ref.shape[0]
+    base = pl.program_id(0) * group
+    for j in range(group):
         t = base + j
         send_ref[j, pl.ds(0, BLOCK)] = x_ref[picked_ref[t]]
         p = spair_ref[t]
-        r = _dot_t(rt_ref[p], x_ref[rhome_ref[p]])
+        r = jnp.dot(rt_ref[p], x_ref[rhome_ref[p]], preferred_element_type=jnp.float32)
         r = jnp.where(sused_ref[t] > 0, r, 0.0)
         send_ref[j, pl.ds(BLOCK, BLOCK)] = r.astype(send_ref.dtype)
         if extra_ref is not None:
@@ -114,6 +115,7 @@
 
 def build_send(picked, spair, sused, rhome, x, rtiles, extra=None):
     slots = picked.shape[0]
+    group = math.gcd(SEND_GROUP, slots)
     full3 = lambda i: (0, 0, 0)
     extra_rows = 0 if extra is None else extra.shape[1]
     rows = 2 * BLOCK + extra_rows
@@ -125,14 +127,14 @@
     in_specs = [_smem()] * 4 + [pl.BlockSpec(x.shape, full3), pl.BlockSpec(rtiles.shape, full3)]
     args = [picked, spair, sused, rhome, x, rtiles]
     if extra is not None:
-        in_specs.append(pl.BlockSpec((SEND_GROUP, extra_rows, F), lambda i: (i, 0, 0)))
+        in_specs.append(pl.BlockSpec((group, extra_rows, F), lambda i: (i, 0, 0)))
         args.append(extra)
     return pl.pallas_call(
         _send_kernel,
-        grid=(slots // SEND_GROUP,),
+        grid=(slots // group,),
         out_shape=jax.ShapeDtypeStruct((slots, rows, F), jnp.bfloat16),
         in_specs=in_specs,
-        out_specs=pl.BlockSpec((SEND_GROUP, rows, F), lambda i: (i, 0, 0)),
+        out_specs=pl.BlockSpec((group, rows, F), lambda i: (i, 0, 0)),
         cost_estimate=cost,
         compiler_params=pltpu.CompilerParams(vmem_limit_bytes=VMEM_LIMIT),
     )(*args)
@@ -220,10 +222,14 @@
     r_order, r_starts = _lists(rhome, own_blocks)
     s_order, s_starts = _lists(back_dest, own_blocks)
 
+    remote_tiles_t = jnp.swapaxes(remote_tiles, 1, 2)
+    local_tiles_t = jnp.swapaxes(local_tiles, 1, 2)
+
     def apply_graph(blocks_in, init, extra=None):
-        send = build_send(picked, slot_pair, slot_used, rhome, blocks_in, remote_tiles, extra)
+        send = build_send(picked, slot_pair, slot_used, rhome, blocks_in, remote_tiles_t, extra)
         recv = lax.all_to_all(send, SLOT_AXES, split_axis=0, concat_axis=0, tiled=True)
-        part = local_sum(h_starts, h_order, n_starts, n_order, lhome, lnear, blocks_in, local_tiles, init)
+        part = local_sum(h_starts, h_order, n_starts, n_order, lhome, lnear, blocks_in, local_tiles,
+                         local_tiles_t, init)
         total = post_sum(r_starts, r_order, target_slot, s_starts, s_order, remote_tiles, recv, part)
         return total.reshape(row_count, F), recv
 

time: 625 us -> 640 us (1.024)
  starting transfers between devices: 33.8 us -> 55.6 us
  Pallas kernels: 96 us -> 87.1 us
  local copies, waits for them, and re-layouts: 17.2 us -> 24.3 us
    all_to_all x2, starting transfers between devices: 23.3 us -> 45.2 us  [apply_graph(): lax.all_to_all(send, SLOT_AXES, split_axis=0, concat_axis=0, tiled=True)]
    pallas_call x2, Pallas kernels: 26.9 us -> 19.9 us  [build_send(): pl.pallas_call(_send_kernel, grid=(slots // group,), out_shape=jax.ShapeD...]
    unnamed x18 -> x22, local copies, waits for them, and re-layouts: 0.31 us -> 7.3 us
  transfers between devices with their start and end apart: 3 -> 3, of which waited for: 3 -> 2; matrix products, arithmetic and copies ran while one was open for 4% -> 5% of each run, Pallas kernels for 6% -> 5%
where the time goes in v6:
time: 640 us; the launch traced here: 636 us
  waiting for transfers between devices  404 us (63%)
  Pallas kernels  87.1 us (14%)
  starting transfers between devices  55.6 us (9%)
  blocking collectives  35.3 us (6%)
  local copies, waits for them, and re-layouts  24.3 us (4%)
  other arithmetic  22.9 us (4%)
    all_to_all x2, waiting for transfers between devices, apply_graph(): lax.all_to_all(send, SLOT_AXES, split_axis=0, concat_axis=0, tiled=True)  404 us
    all_to_all x2, starting transfers between devices, apply_graph(): lax.all_to_all(send, SLOT_AXES, split_axis=0, concat_axis=0, tiled=True)  45.2 us
    all_to_all x1, blocking collectives, body(): lax.all_to_all(spread_out, AXES, split_axis=0, concat_axis=0, tiled=True)  35.3 us
    pallas_call x2, Pallas kernels, local_sum(): pl.pallas_call(_local_kernel, out_shape=jax.ShapeDtypeStruct(init.shape,...  33.9 us
    pallas_call x2, Pallas kernels, post_sum(): pl.pallas_call(_post_kernel, out_shape=jax.ShapeDtypeStruct(base.shape, j...  33.2 us
    pallas_call x2, Pallas kernels, build_send(): pl.pallas_call(_send_kernel, grid=(slots // group,), out_shape=jax.ShapeD...  19.9 us
  transfers between devices with their start and end apart: 3, of which 2 were waited for; matrix products, arithmetic and copies ran while one was open for 5% of the time, Pallas kernels for 5%

profile of v6, /device:TPU:41, one launch (start us, length us, event | category | flops | bytes accessed | tf_op | source)
XLA Modules:
  0.0 635.9 jit_solution(10704424432104647912)
XLA Ops:
  0.6 1.3 compare_select_fusion
  1.9 0.8 scatter_custom_fusion
  2.7 0.7 copy.41
  3.5 10.5 %all-to-all-start = ((s32[128,1,1]{2,1,0:T(1,128)}), s32[128,1,1]{2,1,0:T(1,128)S(1)}, u32[]{:S(2)}, u32[]{:S(2)}) async-start(s32[128,1,1]{2,1,0:T(1,128)} %copy.41), calls=%async_computation | async-start | bytes 131072 | tf_op jit(solution)/shard_map/all_to_all | solution.py:207
  14.0 1.2 broadcast_clamp_fusion.2.rhome_ref
  15.2 1.3 scatter_custom_fusion.1.spair_ref
  16.5 1.3 scatter_custom_fusion.2.sused_ref
  17.9 4.1 copy.43
  21.9 2.4 clamp_reduce_fusion
  24.3 1.7 gather_fusion.1
  26.0 9.7 %shard_map.112 = bf16[128,256,256]{2,1,0:T(8,128)(2,1)} custom-call(s32[128]{0:T(128)} %gather_fusion.1, s32[128]{0:T(128)} %scatter_custom_fusion.1.spair_ref, s32[128]{0:T(128)} %scatter_custom_fusion.2.sused_ref, s32[64]{0:T(128)} %broadcast_clamp_fusion.2.rhome_ref, bf16[16,128,256]{2,1,0:T(8,128)(2,1)} %bitcast.29, bf16[64,128,128]{2,1,0:T(8,128)(2,1)} %bitcast.21), custom_call_target="tpu_custom_call" | custom-call | flops 1073741824 | bytes 19922944 | tf_op jit(solution)/shard_map/pallas_call | solution.py:132
  35.7 10.2 %all-to-all-start.1 = ((bf16[128,256,256]{2,1,0:T(8,128)(2,1)}), bf16[128,256,256]{2,1,0:T(8,128)(2,1)}, u32[]{:S(2)}, u32[]{:S(2)}) async-start(bf16[128,256,256]{2,1,0:T(8,128)(2,1)} %shard_map.112), calls=%async_computation.1 | async-start | bytes 33554432 | tf_op jit(solution)/shard_map/all_to_all | solution.py:230
  46.0 2.1 sort.62
  48.1 2.0 sort.64
  50.4 0.1 reduce.4
  50.5 2.1 sort.65
  52.9 0.1 reduce.5
  53.2 0.1 reduce
  53.4 2.9 copy.46
  56.3 0.7 pad_add_fusion
  56.9 1.6 broadcast_in_dim.18.init_ref
  58.5 17.0 %shard_map.113.base_ref = f32[16,128,256]{2,1,0:T(8,128)} custom-call(s32[17]{0:T(128)} %get-tuple-element.24.hs_ref, s32[64]{0:T(128)} %get-tuple-element.11.ho_ref, s32[17]{0:T(128)} %get-tuple-element.23.ns_ref, s32[64]{0:T(128)} %get-tuple-element.12.no_ref, s32[64]{0:T(128)} %copy-done.5, s32[64]{0:T(128)} %copy-done.6, bf16[16,128,256]{2,1,0:T(8,128)(2,1)} %bitcast.30, ...), custom_call_target="tpu_custom_call" | custom-call | flops 1073741824 | bytes 7340032 | tf_op jit(solution)/shard_map/pallas_call | solution.py:87
  75.5 2.4 compare_reduce_fusion
  77.9 1.2 gather_fusion
  79.1 2.6 sort.63
  82.0 0.7 pad_add_fusion.2
  82.7 193.2 %all-to-all-done.1.recv_ref = bf16[128,256,256]{2,1,0:T(8,128)(2,1)} async-done(((bf16[128,256,256]{2,1,0:T(8,128)(2,1)}), bf16[128,256,256]{2,1,0:T(8,128)(2,1)}, u32[]{:S(2)}, u32[]{:S(2)}) %all-to-all-start.1) | async-done | bytes 16777248 | tf_op jit(solution)/shard_map/all_to_all | solution.py:230
  275.9 16.5 %shard_map.114 = f32[16,128,256]{2,1,0:T(8,128)} custom-call(s32[17]{0:T(128)} %get-tuple-element.26.rs_ref, s32[64]{0:T(128)} %get-tuple-element.9.ro_ref, s32[64]{0:T(128)} %get-tuple-element.16.td_ref, s32[17]{0:T(128)} %get-tuple-element.25.ss_ref, s32[128]{0:T(128)} %get-tuple-element.10.so_ref, ...), custom_call_target="tpu_custom_call", output_to_operand_aliasing={{}: (7, {})} | custom-call | flops 536870912 | bytes 23068672 | tf_op jit(solution)/shard_map/pallas_call | solution.py:176
  292.4 1.9 convert_element_type.41
  294.3 0.3 copy-done.7
  294.6 2.3 multiply_convert_fusion
  296.9 0.7 fusion
  297.6 2.8 fusion.20
  300.5 0.1 reshape.216
  300.6 0.9 gather_fusion.2
  301.5 0.2 reduce-precision_convert_fusion
  301.7 2.7 slice.38
  304.4 1.1 pad_maximum_fusion.3.rest_0_
  305.4 10.2 %shard_map.115 = bf16[128,264,256]{2,1,0:T(8,128)(2,1)} custom-call(s32[128]{0:T(128)} %gather_fusion.1, s32[128]{0:T(128)} %scatter_custom_fusion.1.spair_ref, s32[128]{0:T(128)} %scatter_custom_fusion.2.sused_ref, s32[64]{0:T(128)} %broadcast_clamp_fusion.2.rhome_ref, bf16[16,128,256]{2,1,0:T(8,128)(2,1)} %bitcast.25, bf16[64,128,128]{2,1,0:T(8,128)(2,1)} %bitcast.22, ...), custom_call_target="tpu_custom_call" | custom-call | flops 1073741824 | bytes 20447232 | tf_op jit(solution)/shard_map/pallas_call | solution.py:132
  315.7 34.9 %all-to-all-start.2 = ((bf16[128,264,256]{2,1,0:T(8,128)(2,1)}), bf16[128,264,256]{2,1,0:T(8,128)(2,1)}, u32[]{:S(2)}, u32[]{:S(2)}) async-start(bf16[128,264,256]{2,1,0:T(8,128)(2,1)} %shard_map.115), calls=%async_computation.2 | async-start | bytes 34603008 | tf_op jit(solution)/shard_map/all_to_all | solution.py:230
  350.6 3.1 slice.31
  353.7 17.0 %shard_map.116.base_ref = f32[16,128,256]{2,1,0:T(8,128)} custom-call(s32[17]{0:T(128)} %get-tuple-element.24.hs_ref, s32[64]{0:T(128)} %get-tuple-element.11.ho_ref, s32[17]{0:T(128)} %get-tuple-element.23.ns_ref, s32[64]{0:T(128)} %get-tuple-element.12.no_ref, s32[64]{0:T(128)} %copy-done.5, s32[64]{0:T(128)} %copy-done.6, bf16[16,128,256]{2,1,0:T(8,128)(2,1)} %bitcast.26, ...), custom_call_target="tpu_custom_call" | custom-call | flops 1073741824 | bytes 7340032 | tf_op jit(solution)/shard_map/pallas_call | solution.py:87
  370.7 210.7 %all-to-all-done.2.recv_ref = bf16[128,264,256]{2,1,0:T(8,128)(2,1)} async-done(((bf16[128,264,256]{2,1,0:T(8,128)(2,1)}), bf16[128,264,256]{2,1,0:T(8,128)(2,1)}, u32[]{:S(2)}, u32[]{:S(2)}) %all-to-all-start.2) | async-done | bytes 17301536 | tf_op jit(solution)/shard_map/all_to_all | solution.py:230
  581.4 1.1 slice_convert_fusion.1
  582.5 0.2 fusion.3
  582.7 16.7 %shard_map.117 = f32[16,128,256]{2,1,0:T(8,128)} custom-call(s32[17]{0:T(128)} %get-tuple-element.26.rs_ref, s32[64]{0:T(128)} %get-tuple-element.9.ro_ref, s32[64]{0:T(128)} %get-tuple-element.16.td_ref, s32[17]{0:T(128)} %get-tuple-element.25.ss_ref, s32[128]{0:T(128)} %get-tuple-element.10.so_ref, ...), custom_call_target="tpu_custom_call", output_to_operand_aliasing={{}: (7, {})} | custom-call | flops 536870912 | bytes 23592960 | tf_op jit(solution)/shard_map/pallas_call | solution.py:176
  599.5 35.3 %all_to_all.24 = f32[128,4,256]{2,1,0:T(4,128)S(1)} all-to-all(f32[128,4,256]{2,1,0:T(4,128)S(1)} %broadcast_in_dim.19), channel_id=1, replica_groups=mesh['group'=2,'member'=64] {'group','member'}, dimensions={0} | all-to-all | bytes 1048576 | tf_op jit(solution)/shard_map/all_to_all | solution.py:262
  634.9 1.0 mul.54
  (47 shorter events, 1.3 us)
Async XLA Ops:
  0.6 293.7 %copy-start = (bf16[512,256]{1,0:T(8,128)(2,1)S(1)}, bf16[512,256]{1,0:T(8,128)(2,1)}, u32[]{:S(2)}) copy-start(bf16[512,256]{1,0:T(8,128)(2,1)} %param.16) | copy-start | bytes 786436
  3.5 18.4 %all-to-all-start = ((s32[128,1,1]{2,1,0:T(1,128)}), s32[128,1,1]{2,1,0:T(1,128)S(1)}, u32[]{:S(2)}, u32[]{:S(2)}) async-start(s32[128,1,1]{2,1,0:T(1,128)} %copy.41), calls=%async_computation | async-start | bytes 131072 | tf_op jit(solution)/shard_map/all_to_all | solution.py:207
  35.7 10.3 %copy-start.4 = (s32[64]{0:T(128)S(1)}, s32[64]{0:T(128)}, u32[]{:S(2)}) copy-start(s32[64]{0:T(128)} %broadcast_clamp_fusion.2.rhome_ref) | copy-start | bytes 772
  35.7 12.4 %copy-start.8 = (s32[64]{0:T(128)S(1)}, s32[64]{0:T(128)}, u32[]{:S(2)}) copy-start(s32[64]{0:T(128)} %param.10) | copy-start | bytes 772
  35.7 14.8 %copy-start.9 = (s32[64]{0:T(128)S(1)}, s32[64]{0:T(128)}, u32[]{:S(2)}) copy-start(s32[64]{0:T(128)} %param.11) | copy-start | bytes 772
  35.7 17.6 %copy-start.2 = (bf16[64,128,128]{2,1,0:T(8,128)(2,1)S(1)}, bf16[64,128,128]{2,1,0:T(8,128)(2,1)}, u32[]{:S(2)}) copy-start(bf16[64,128,128]{2,1,0:T(8,128)(2,1)} %lt_ref.3) | copy-start | bytes 6291460
  35.7 240.2 %all-to-all-start.1 = ((bf16[128,256,256]{2,1,0:T(8,128)(2,1)}), bf16[128,256,256]{2,1,0:T(8,128)(2,1)}, u32[]{:S(2)}, u32[]{:S(2)}) async-start(bf16[128,256,256]{2,1,0:T(8,128)(2,1)} %shard_map.112), calls=%async_computation.1 | async-start | bytes 33554432 | tf_op jit(solution)/shard_map/all_to_all | solution.py:230
  48.1 8.2 %copy-start.5 = (s32[64]{0:T(128)}, s32[64]{0:T(128)S(1)}, u32[]{:S(2)}) copy-start(s32[64]{0:T(128)S(1)} %broadcast_clamp_fusion.1.lh_ref) | copy-start | bytes 772
  50.5 5.8 copy-start.6
  292.4 1.9 copy-start.3
  292.4 2.2 copy-start.7
  315.7 265.7 %all-to-all-start.2 = ((bf16[128,264,256]{2,1,0:T(8,128)(2,1)}), bf16[128,264,256]{2,1,0:T(8,128)(2,1)}, u32[]{:S(2)}, u32[]{:S(2)}) async-start(bf16[128,264,256]{2,1,0:T(8,128)(2,1)} %shard_map.115), calls=%async_computation.2 | async-start | bytes 34603008 | tf_op jit(solution)/shard_map/all_to_all | solution.py:230
  582.7 53.2 %copy-start.1 = (bf16[512,256]{1,0:T(8,128)(2,1)S(1)}, bf16[512,256]{1,0:T(8,128)(2,1)}, u32[]{:S(2)}) copy-start(bf16[512,256]{1,0:T(8,128)(2,1)} %param.16) | copy-start | bytes 786436

commit v7 on v5

--- a/solution.py
+++ b/solution.py
@@ -99,7 +99,7 @@
 
 def _send_kernel(picked_ref, spair_ref, sused_ref, rhome_ref, x_ref, rt_ref, *rest):
     send_ref = rest[-1]
-    extra_ref = rest[0] if len(rest) == 2 else None
+    extra_ref = rest[0] if len(rest) == 2 and rest[0].shape[0] == send_ref.shape[0] else None
     base = pl.program_id(0) * SEND_GROUP
     for j in range(SEND_GROUP):
         t = base + j
@@ -112,7 +112,7 @@
             send_ref[j, pl.ds(2 * BLOCK, extra_ref.shape[1])] = extra_ref[j]
 
 
-def build_send(picked, spair, sused, rhome, x, rtiles, extra=None):
+def build_send(picked, spair, sused, rhome, x, rtiles, extra=None, after=None):
     slots = picked.shape[0]
     full3 = lambda i: (0, 0, 0)
     extra_rows = 0 if extra is None else extra.shape[1]
@@ -127,6 +127,9 @@
     if extra is not None:
         in_specs.append(pl.BlockSpec((SEND_GROUP, extra_rows, F), lambda i: (i, 0, 0)))
         args.append(extra)
+    if after is not None:
+        in_specs.append(pl.BlockSpec(memory_space=pl.ANY))
+        args.append(after)
     return pl.pallas_call(
         _send_kernel,
         grid=(slots // SEND_GROUP,),
@@ -220,15 +223,16 @@
     r_order, r_starts = _lists(rhome, own_blocks)
     s_order, s_starts = _lists(back_dest, own_blocks)
 
-    def apply_graph(blocks_in, init, extra=None):
-        send = build_send(picked, slot_pair, slot_used, rhome, blocks_in, remote_tiles, extra)
+    def apply_graph(blocks_in, init, extra=None, local_first=False):
+        part = local_sum(h_starts, h_order, n_starts, n_order, lhome, lnear, blocks_in, local_tiles, init)
+        send = build_send(picked, slot_pair, slot_used, rhome, blocks_in, remote_tiles, extra,
+                          part if local_first else None)
         recv = lax.all_to_all(send, SLOT_AXES, split_axis=0, concat_axis=0, tiled=True)
-        part = local_sum(h_starts, h_order, n_starts, n_order, lhome, lnear, blocks_in, local_tiles, init)
         total = post_sum(r_starts, r_order, target_slot, s_starts, s_order, remote_tiles, recv, part)
         return total.reshape(row_count, F), recv
 
     zeros = jnp.zeros((own_blocks, BLOCK, F), jnp.float32)
-    aggregate = apply_graph(features.reshape(own_blocks, BLOCK, F), zeros)[0].astype(jnp.bfloat16)
+    aggregate = apply_graph(features.reshape(own_blocks, BLOCK, F), zeros, local_first=True)[0].astype(jnp.bfloat16)
     joined = jnp.concatenate([features, aggregate], axis=1)
     pre_act = jnp.dot(joined, weight, preferred_element_type=jnp.float32)
     sigmoid_z = jax.nn.sigmoid(pre_act)

time: 625 us -> 669 us (1.070)
  starting transfers between devices: 33.8 us -> 56 us
  waiting for transfers between devices: 408 us -> 430 us
    all_to_all x2, waiting for transfers between devices: 404 us -> 430 us  [apply_graph(): lax.all_to_all(send, SLOT_AXES, split_axis=0, concat_axis=0, tiled=True)]
    all_to_all x2, starting transfers between devices: 23.3 us -> 45.6 us  [apply_graph(): lax.all_to_all(send, SLOT_AXES, split_axis=0, concat_axis=0, tiled=True)]
  transfers between devices with their start and end apart: 3 -> 3, of which waited for: 3 -> 2; matrix products, arithmetic and copies ran while one was open for 4% -> 4% of each run, Pallas kernels for 6% -> 5%
where the time goes in v7:
time: 669 us; the launch traced here: 664 us
  waiting for transfers between devices  430 us (64%)
  Pallas kernels  95 us (14%)
  starting transfers between devices  56 us (8%)
  blocking collectives  35.1 us (5%)
  other arithmetic  24.2 us (4%)
  local copies, waits for them, and re-layouts  17.1 us (3%)
    all_to_all x2, waiting for transfers between devices, apply_graph(): lax.all_to_all(send, SLOT_AXES, split_axis=0, concat_axis=0, tiled=True)  430 us
    all_to_all x2, starting transfers between devices, apply_graph(): lax.all_to_all(send, SLOT_AXES, split_axis=0, concat_axis=0, tiled=True)  45.6 us
    pallas_call x2, Pallas kernels, local_sum(): pl.pallas_call(_local_kernel, out_shape=jax.ShapeDtypeStruct(init.shape,...  35.8 us
    all_to_all x1, blocking collectives, body(): lax.all_to_all(spread_out, AXES, split_axis=0, concat_axis=0, tiled=True)  35.1 us
    pallas_call x2, Pallas kernels, post_sum(): pl.pallas_call(_post_kernel, out_shape=jax.ShapeDtypeStruct(base.shape, j...  32.2 us
    pallas_call x2, Pallas kernels, build_send(): pl.pallas_call(_send_kernel, grid=(slots // SEND_GROUP,), out_shape=jax.S...  26.9 us
  transfers between devices with their start and end apart: 3, of which 2 were waited for; matrix products, arithmetic and copies ran while one was open for 4% of the time, Pallas kernels for 5%

profile of v7, /device:TPU:41, one launch (start us, length us, event | category | flops | bytes accessed | tf_op | source)
XLA Modules:
  0.0 664.3 jit_solution(18193419697004217556)
XLA Ops:
  0.6 1.2 compare_select_fusion
  1.9 0.8 scatter_custom_fusion
  2.6 0.7 copy.33
  3.4 10.5 %all-to-all-start = ((s32[128,1,1]{2,1,0:T(1,128)}), s32[128,1,1]{2,1,0:T(1,128)S(1)}, u32[]{:S(2)}, u32[]{:S(2)}) async-start(s32[128,1,1]{2,1,0:T(1,128)} %copy.33), calls=%async_computation | async-start | bytes 131072 | tf_op jit(solution)/shard_map/all_to_all | solution.py:208
  13.9 0.7 broadcast_clamp_fusion.1.lh_ref
  14.5 0.7 broadcast_clamp_fusion.ln_ref
  15.2 1.2 broadcast_clamp_fusion.2.rhome_ref
  16.7 2.1 sort.64
  18.8 2.1 sort.65
  21.0 0.1 reduce.4
  21.3 0.1 reduce.5
  21.4 0.7 pad_add_fusion
  22.0 1.5 broadcast_in_dim.18.init_ref
  23.6 17.9 %shard_map.112.rest_0_.base_ref = f32[16,128,256]{2,1,0:T(8,128)} custom-call(s32[17]{0:T(128)} %get-tuple-element.24.hs_ref, s32[64]{0:T(128)} %get-tuple-element.11.ho_ref, s32[17]{0:T(128)} %get-tuple-element.23.ns_ref, s32[64]{0:T(128)} %get-tuple-element.12.no_ref, s32[64]{0:T(128)} %copy-done.3, s32[64]{0:T(128)} %copy-done.4, ...), custom_call_target="tpu_custom_call" | custom-call | flops 1073741824 | bytes 7340032 | tf_op jit(solution)/shard_map/pallas_call | solution.py:87
  41.5 1.3 scatter_custom_fusion.1.spair_ref
  42.8 1.3 scatter_custom_fusion.2.sused_ref
  44.1 2.4 clamp_reduce_fusion
  46.5 1.7 gather_fusion.1
  48.2 13.1 %shard_map.113 = bf16[128,256,256]{2,1,0:T(8,128)(2,1)} custom-call(s32[128]{0:T(128)} %gather_fusion.1, s32[128]{0:T(128)} %scatter_custom_fusion.1.spair_ref, s32[128]{0:T(128)} %scatter_custom_fusion.2.sused_ref, s32[64]{0:T(128)} %broadcast_clamp_fusion.2.rhome_ref, bf16[16,128,256]{2,1,0:T(8,128)(2,1)} %bitcast.24, bf16[64,128,128]{2,1,0:T(8,128)(2,1)} %rt_ref.7, ...), custom_call_target="tpu_custom_call" | custom-call | flops 1073741824 | bytes 19922944 | tf_op jit(solution)/shard_map/pallas_call | solution.py:133
  61.3 10.6 %all-to-all-start.1 = ((bf16[128,256,256]{2,1,0:T(8,128)(2,1)}), bf16[128,256,256]{2,1,0:T(8,128)(2,1)}, u32[]{:S(2)}, u32[]{:S(2)}) async-start(bf16[128,256,256]{2,1,0:T(8,128)(2,1)} %shard_map.113), calls=%async_computation.1 | async-start | bytes 33554432 | tf_op jit(solution)/shard_map/all_to_all | solution.py:230
  71.9 2.0 sort.62
  74.2 0.1 reduce
  74.3 2.4 compare_reduce_fusion
  76.7 1.2 gather_fusion
  77.9 2.5 sort.63
  80.8 0.7 pad_add_fusion.2
  81.5 220.3 %all-to-all-done.1.recv_ref = bf16[128,256,256]{2,1,0:T(8,128)(2,1)} async-done(((bf16[128,256,256]{2,1,0:T(8,128)(2,1)}), bf16[128,256,256]{2,1,0:T(8,128)(2,1)}, u32[]{:S(2)}, u32[]{:S(2)}) %all-to-all-start.1) | async-done | bytes 16777248 | tf_op jit(solution)/shard_map/all_to_all | solution.py:230
  301.8 16.0 %shard_map.114 = f32[16,128,256]{2,1,0:T(8,128)} custom-call(s32[17]{0:T(128)} %get-tuple-element.26.rs_ref, s32[64]{0:T(128)} %get-tuple-element.9.ro_ref, s32[64]{0:T(128)} %get-tuple-element.16.td_ref, s32[17]{0:T(128)} %get-tuple-element.25.ss_ref, s32[128]{0:T(128)} %get-tuple-element.10.so_ref, ...), custom_call_target="tpu_custom_call", output_to_operand_aliasing={{}: (7, {})} | custom-call | flops 536870912 | bytes 23068672 | tf_op jit(solution)/shard_map/pallas_call | solution.py:177
  317.8 1.9 convert_element_type.41
  319.7 0.3 copy-done.6
  320.0 2.3 multiply_convert_fusion
  322.3 0.7 fusion
  323.0 2.8 fusion.20
  325.9 0.1 reshape.216
  326.0 0.9 gather_fusion.2
  326.9 0.2 reduce-precision_convert_fusion
  327.1 2.7 slice.38
  329.7 1.1 pad_maximum_fusion.3.rest_0_
  330.8 13.8 %shard_map.115 = bf16[128,264,256]{2,1,0:T(8,128)(2,1)} custom-call(s32[128]{0:T(128)} %gather_fusion.1, s32[128]{0:T(128)} %scatter_custom_fusion.1.spair_ref, s32[128]{0:T(128)} %scatter_custom_fusion.2.sused_ref, s32[64]{0:T(128)} %broadcast_clamp_fusion.2.rhome_ref, bf16[16,128,256]{2,1,0:T(8,128)(2,1)} %bitcast.19, bf16[64,128,128]{2,1,0:T(8,128)(2,1)} %rt_ref.7, ...), custom_call_target="tpu_custom_call" | custom-call | flops 1073741824 | bytes 20447232 | tf_op jit(solution)/shard_map/pallas_call | solution.py:133
  344.6 35.0 %all-to-all-start.2 = ((bf16[128,264,256]{2,1,0:T(8,128)(2,1)}), bf16[128,264,256]{2,1,0:T(8,128)(2,1)}, u32[]{:S(2)}, u32[]{:S(2)}) async-start(bf16[128,264,256]{2,1,0:T(8,128)(2,1)} %shard_map.115), calls=%async_computation.2 | async-start | bytes 34603008 | tf_op jit(solution)/shard_map/all_to_all | solution.py:230
  379.7 3.0 slice.31
  382.7 17.9 %shard_map.116.base_ref = f32[16,128,256]{2,1,0:T(8,128)} custom-call(s32[17]{0:T(128)} %get-tuple-element.24.hs_ref, s32[64]{0:T(128)} %get-tuple-element.11.ho_ref, s32[17]{0:T(128)} %get-tuple-element.23.ns_ref, s32[64]{0:T(128)} %get-tuple-element.12.no_ref, s32[64]{0:T(128)} %copy-done.3, s32[64]{0:T(128)} %copy-done.4, bf16[16,128,256]{2,1,0:T(8,128)(2,1)} %bitcast.20, ...), custom_call_target="tpu_custom_call" | custom-call | flops 1073741824 | bytes 7340032 | tf_op jit(solution)/shard_map/pallas_call | solution.py:87
  400.6 209.9 %all-to-all-done.2.recv_ref = bf16[128,264,256]{2,1,0:T(8,128)(2,1)} async-done(((bf16[128,264,256]{2,1,0:T(8,128)(2,1)}), bf16[128,264,256]{2,1,0:T(8,128)(2,1)}, u32[]{:S(2)}, u32[]{:S(2)}) %all-to-all-start.2) | async-done | bytes 17301536 | tf_op jit(solution)/shard_map/all_to_all | solution.py:230
  610.5 1.1 slice_convert_fusion.1
  611.6 0.2 fusion.3
  611.8 16.2 %shard_map.117 = f32[16,128,256]{2,1,0:T(8,128)} custom-call(s32[17]{0:T(128)} %get-tuple-element.26.rs_ref, s32[64]{0:T(128)} %get-tuple-element.9.ro_ref, s32[64]{0:T(128)} %get-tuple-element.16.td_ref, s32[17]{0:T(128)} %get-tuple-element.25.ss_ref, s32[128]{0:T(128)} %get-tuple-element.10.so_ref, ...), custom_call_target="tpu_custom_call", output_to_operand_aliasing={{}: (7, {})} | custom-call | flops 536870912 | bytes 23592960 | tf_op jit(solution)/shard_map/pallas_call | solution.py:177
  628.1 35.1 %all_to_all.24 = f32[128,4,256]{2,1,0:T(4,128)S(1)} all-to-all(f32[128,4,256]{2,1,0:T(4,128)S(1)} %broadcast_in_dim.19), channel_id=1, replica_groups=mesh['group'=2,'member'=64] {'group','member'}, dimensions={0} | all-to-all | bytes 1048576 | tf_op jit(solution)/shard_map/all_to_all | solution.py:260
  663.3 1.0 mul.54
  (39 shorter events, 1.3 us)
Async XLA Ops:
  0.6 319.1 %copy-start = (bf16[512,256]{1,0:T(8,128)(2,1)S(1)}, bf16[512,256]{1,0:T(8,128)(2,1)}, u32[]{:S(2)}) copy-start(bf16[512,256]{1,0:T(8,128)(2,1)} %param.16) | copy-start | bytes 786436
  3.4 40.8 %all-to-all-start = ((s32[128,1,1]{2,1,0:T(1,128)}), s32[128,1,1]{2,1,0:T(1,128)S(1)}, u32[]{:S(2)}, u32[]{:S(2)}) async-start(s32[128,1,1]{2,1,0:T(1,128)} %copy.33), calls=%async_computation | async-start | bytes 131072 | tf_op jit(solution)/shard_map/all_to_all | solution.py:208
  14.5 9.0 %copy-start.3 = (s32[64]{0:T(128)}, s32[64]{0:T(128)S(1)}, u32[]{:S(2)}) copy-start(s32[64]{0:T(128)S(1)} %broadcast_clamp_fusion.1.lh_ref) | copy-start | bytes 772
  15.2 8.4 %copy-start.4 = (s32[64]{0:T(128)}, s32[64]{0:T(128)S(1)}, u32[]{:S(2)}) copy-start(s32[64]{0:T(128)S(1)} %broadcast_clamp_fusion.ln_ref) | copy-start | bytes 772
  61.3 10.6 %copy-start.5 = (s32[64]{0:T(128)S(1)}, s32[64]{0:T(128)}, u32[]{:S(2)}) copy-start(s32[64]{0:T(128)} %broadcast_clamp_fusion.2.rhome_ref) | copy-start | bytes 772
  61.3 240.5 %all-to-all-start.1 = ((bf16[128,256,256]{2,1,0:T(8,128)(2,1)}), bf16[128,256,256]{2,1,0:T(8,128)(2,1)}, u32[]{:S(2)}, u32[]{:S(2)}) async-start(bf16[128,256,256]{2,1,0:T(8,128)(2,1)} %shard_map.113), calls=%async_computation.1 | async-start | bytes 33554432 | tf_op jit(solution)/shard_map/all_to_all | solution.py:230
  317.8 1.9 copy-start.2
  317.8 2.2 copy-start.6
  344.6 265.8 %all-to-all-start.2 = ((bf16[128,264,256]{2,1,0:T(8,128)(2,1)}), bf16[128,264,256]{2,1,0:T(8,128)(2,1)}, u32[]{:S(2)}, u32[]{:S(2)}) async-start(bf16[128,264,256]{2,1,0:T(8,128)(2,1)} %shard_map.115), calls=%async_computation.2 | async-start | bytes 34603008 | tf_op jit(solution)/shard_map/all_to_all | solution.py:230
  611.8 52.5 %copy-start.1 = (bf16[512,256]{1,0:T(8,128)(2,1)S(1)}, bf16[512,256]{1,0:T(8,128)(2,1)}, u32[]{:S(2)}) copy-start(bf16[512,256]{1,0:T(8,128)(2,1)} %param.16) | copy-start | bytes 786436

commit v8 on v5

--- a/solution.py
+++ b/solution.py
@@ -94,14 +94,15 @@
     )(hs, ho, ns, no, lh, ln, x, ltiles, init)
 
 
-SEND_GROUP = 8
+SEND_GROUP = 16
 
 
 def _send_kernel(picked_ref, spair_ref, sused_ref, rhome_ref, x_ref, rt_ref, *rest):
     send_ref = rest[-1]
     extra_ref = rest[0] if len(rest) == 2 else None
-    base = pl.program_id(0) * SEND_GROUP
-    for j in range(SEND_GROUP):
+    group = send_ref.shape[0]
+    base = pl.program_id(0) * group
+    for j in range(group):
         t = base + j
         send_ref[j, pl.ds(0, BLOCK)] = x_ref[picked_ref[t]]
         p = spair_ref[t]
@@ -114,6 +115,7 @@
 
 def build_send(picked, spair, sused, rhome, x, rtiles, extra=None):
     slots = picked.shape[0]
+    group = math.gcd(SEND_GROUP, slots)
     full3 = lambda i: (0, 0, 0)
     extra_rows = 0 if extra is None else extra.shape[1]
     rows = 2 * BLOCK + extra_rows
@@ -125,14 +127,14 @@
     in_specs = [_smem()] * 4 + [pl.BlockSpec(x.shape, full3), pl.BlockSpec(rtiles.shape, full3)]
     args = [picked, spair, sused, rhome, x, rtiles]
     if extra is not None:
-        in_specs.append(pl.BlockSpec((SEND_GROUP, extra_rows, F), lambda i: (i, 0, 0)))
+        in_specs.append(pl.BlockSpec((group, extra_rows, F), lambda i: (i, 0, 0)))
         args.append(extra)
     return pl.pallas_call(
         _send_kernel,
-        grid=(slots // SEND_GROUP,),
+        grid=(slots // group,),
         out_shape=jax.ShapeDtypeStruct((slots, rows, F), jnp.bfloat16),
         in_specs=in_specs,
-        out_specs=pl.BlockSpec((SEND_GROUP, rows, F), lambda i: (i, 0, 0)),
+        out_specs=pl.BlockSpec((group, rows, F), lambda i: (i, 0, 0)),
         cost_estimate=cost,
         compiler_params=pltpu.CompilerParams(vmem_limit_bytes=VMEM_LIMIT),
     )(*args)

time: 625 us -> 616 us (0.986)
  Pallas kernels: 96 us -> 87.6 us
    pallas_call x2, Pallas kernels: 26.9 us -> 20.2 us  [build_send(): pl.pallas_call(_send_kernel, grid=(slots // group,), out_shape=jax.ShapeD...]
where the time goes in v8:
time: 616 us; the launch traced here: 612 us
  waiting for transfers between devices  409 us (66%)
  Pallas kernels  87.6 us (14%)
  blocking collectives  34.8 us (6%)
  starting transfers between devices  34.3 us (6%)
  other arithmetic  23 us (4%)
  local copies, waits for them, and re-layouts  17.2 us (3%)
    all_to_all x2, waiting for transfers between devices, apply_graph(): lax.all_to_all(send, SLOT_AXES, split_axis=0, concat_axis=0, tiled=True)  405 us
    all_to_all x1, blocking collectives, body(): lax.all_to_all(spread_out, AXES, split_axis=0, concat_axis=0, tiled=True)  34.8 us
    pallas_call x2, Pallas kernels, local_sum(): pl.pallas_call(_local_kernel, out_shape=jax.ShapeDtypeStruct(init.shape,...  34.6 us
    pallas_call x2, Pallas kernels, post_sum(): pl.pallas_call(_post_kernel, out_shape=jax.ShapeDtypeStruct(base.shape, j...  32.8 us
    all_to_all x2, starting transfers between devices, apply_graph(): lax.all_to_all(send, SLOT_AXES, split_axis=0, concat_axis=0, tiled=True)  23.8 us
    pallas_call x2, Pallas kernels, build_send(): pl.pallas_call(_send_kernel, grid=(slots // group,), out_shape=jax.ShapeD...  20.2 us
  transfers between devices with their start and end apart: 3, of which 3 were waited for; matrix products, arithmetic and copies ran while one was open for 4% of the time, Pallas kernels for 6%

profile of v8, /device:TPU:41, one launch (start us, length us, event | category | flops | bytes accessed | tf_op | source)
XLA Modules:
  0.0 612.4 jit_solution(15376943628161280799)
XLA Ops:
  0.6 1.2 compare_select_fusion
  1.9 0.8 scatter_custom_fusion
  2.6 0.7 copy.33
  3.4 10.5 %all-to-all-start = ((s32[128,1,1]{2,1,0:T(1,128)}), s32[128,1,1]{2,1,0:T(1,128)S(1)}, u32[]{:S(2)}, u32[]{:S(2)}) async-start(s32[128,1,1]{2,1,0:T(1,128)} %copy.33), calls=%async_computation | async-start | bytes 131072 | tf_op jit(solution)/shard_map/all_to_all | solution.py:207
  13.9 1.2 broadcast_clamp_fusion.2.rhome_ref
  15.1 1.3 scatter_custom_fusion.1.spair_ref
  16.5 1.3 scatter_custom_fusion.2.sused_ref
  17.8 3.5 all-to-all-done
  21.3 2.4 clamp_reduce_fusion
  23.7 1.8 gather_fusion.1
  25.4 9.9 %shard_map.112 = bf16[128,256,256]{2,1,0:T(8,128)(2,1)} custom-call(s32[128]{0:T(128)} %gather_fusion.1, s32[128]{0:T(128)} %scatter_custom_fusion.1.spair_ref, s32[128]{0:T(128)} %scatter_custom_fusion.2.sused_ref, s32[64]{0:T(128)} %broadcast_clamp_fusion.2.rhome_ref, bf16[16,128,256]{2,1,0:T(8,128)(2,1)} %bitcast.23, bf16[64,128,128]{2,1,0:T(8,128)(2,1)} %rt_ref.7), custom_call_target="tpu_custom_call" | custom-call | flops 1073741824 | bytes 19922944 | tf_op jit(solution)/shard_map/pallas_call | solution.py:132
  35.3 7.7 %all-to-all-start.1 = ((bf16[128,256,256]{2,1,0:T(8,128)(2,1)}), bf16[128,256,256]{2,1,0:T(8,128)(2,1)}, u32[]{:S(2)}, u32[]{:S(2)}) async-start(bf16[128,256,256]{2,1,0:T(8,128)(2,1)} %shard_map.112), calls=%async_computation.1 | async-start | bytes 33554432 | tf_op jit(solution)/shard_map/all_to_all | solution.py:227
  43.1 2.1 sort.62
  45.2 2.1 sort.64
  47.5 0.1 reduce.4
  47.7 2.1 sort.65
  50.0 0.1 reduce.5
  50.4 0.1 reduce
  50.5 0.7 pad_add_fusion
  51.2 1.5 broadcast_in_dim.18.init_ref
  52.7 17.3 %shard_map.113.base_ref = f32[16,128,256]{2,1,0:T(8,128)} custom-call(s32[17]{0:T(128)} %get-tuple-element.24.hs_ref, s32[64]{0:T(128)} %get-tuple-element.11.ho_ref, s32[17]{0:T(128)} %get-tuple-element.23.ns_ref, s32[64]{0:T(128)} %get-tuple-element.12.no_ref, s32[64]{0:T(128)} %copy-done.4, s32[64]{0:T(128)} %copy-done.5, bf16[16,128,256]{2,1,0:T(8,128)(2,1)} %bitcast.24, ...), custom_call_target="tpu_custom_call" | custom-call | flops 1073741824 | bytes 7340032 | tf_op jit(solution)/shard_map/pallas_call | solution.py:87
  70.0 2.4 compare_reduce_fusion
  72.4 1.2 gather_fusion
  73.6 2.6 sort.63
  76.5 0.1 reduce.3
  76.6 0.6 pad_add_fusion.2
  77.2 194.8 %all-to-all-done.1.recv_ref = bf16[128,256,256]{2,1,0:T(8,128)(2,1)} async-done(((bf16[128,256,256]{2,1,0:T(8,128)(2,1)}), bf16[128,256,256]{2,1,0:T(8,128)(2,1)}, u32[]{:S(2)}, u32[]{:S(2)}) %all-to-all-start.1) | async-done | bytes 16777248 | tf_op jit(solution)/shard_map/all_to_all | solution.py:227
  272.0 16.3 %shard_map.114 = f32[16,128,256]{2,1,0:T(8,128)} custom-call(s32[17]{0:T(128)} %get-tuple-element.26.rs_ref, s32[64]{0:T(128)} %get-tuple-element.9.ro_ref, s32[64]{0:T(128)} %get-tuple-element.16.td_ref, s32[17]{0:T(128)} %get-tuple-element.25.ss_ref, s32[128]{0:T(128)} %get-tuple-element.10.so_ref, ...), custom_call_target="tpu_custom_call", output_to_operand_aliasing={{}: (7, {})} | custom-call | flops 536870912 | bytes 23068672 | tf_op jit(solution)/shard_map/pallas_call | solution.py:176
  288.3 1.9 convert_element_type.41
  290.2 0.3 copy-done.6
  290.5 2.3 multiply_convert_fusion
  292.8 0.7 fusion
  293.5 2.8 fusion.20
  296.3 0.1 reshape.216
  296.5 0.9 gather_fusion.2
  297.4 0.2 reduce-precision_convert_fusion
  297.6 2.7 slice.38
  300.2 1.1 pad_maximum_fusion.3.rest_0_
  301.3 10.4 %shard_map.115 = bf16[128,264,256]{2,1,0:T(8,128)(2,1)} custom-call(s32[128]{0:T(128)} %gather_fusion.1, s32[128]{0:T(128)} %scatter_custom_fusion.1.spair_ref, s32[128]{0:T(128)} %scatter_custom_fusion.2.sused_ref, s32[64]{0:T(128)} %broadcast_clamp_fusion.2.rhome_ref, bf16[16,128,256]{2,1,0:T(8,128)(2,1)} %bitcast.19, bf16[64,128,128]{2,1,0:T(8,128)(2,1)} %rt_ref.7, ...), custom_call_target="tpu_custom_call" | custom-call | flops 1073741824 | bytes 20447232 | tf_op jit(solution)/shard_map/pallas_call | solution.py:132
  311.6 16.1 %all-to-all-start.2 = ((bf16[128,264,256]{2,1,0:T(8,128)(2,1)}), bf16[128,264,256]{2,1,0:T(8,128)(2,1)}, u32[]{:S(2)}, u32[]{:S(2)}) async-start(bf16[128,264,256]{2,1,0:T(8,128)(2,1)} %shard_map.115), calls=%async_computation.2 | async-start | bytes 34603008 | tf_op jit(solution)/shard_map/all_to_all | solution.py:227
  327.7 3.0 slice.31
  330.8 17.3 %shard_map.116.base_ref = f32[16,128,256]{2,1,0:T(8,128)} custom-call(s32[17]{0:T(128)} %get-tuple-element.24.hs_ref, s32[64]{0:T(128)} %get-tuple-element.11.ho_ref, s32[17]{0:T(128)} %get-tuple-element.23.ns_ref, s32[64]{0:T(128)} %get-tuple-element.12.no_ref, s32[64]{0:T(128)} %copy-done.4, s32[64]{0:T(128)} %copy-done.5, bf16[16,128,256]{2,1,0:T(8,128)(2,1)} %bitcast.20, ...), custom_call_target="tpu_custom_call" | custom-call | flops 1073741824 | bytes 7340032 | tf_op jit(solution)/shard_map/pallas_call | solution.py:87
  348.1 210.5 %all-to-all-done.2.recv_ref = bf16[128,264,256]{2,1,0:T(8,128)(2,1)} async-done(((bf16[128,264,256]{2,1,0:T(8,128)(2,1)}), bf16[128,264,256]{2,1,0:T(8,128)(2,1)}, u32[]{:S(2)}, u32[]{:S(2)}) %all-to-all-start.2) | async-done | bytes 17301536 | tf_op jit(solution)/shard_map/all_to_all | solution.py:227
  558.5 1.1 slice_convert_fusion.1
  559.7 0.2 fusion.3
  559.9 16.5 %shard_map.117 = f32[16,128,256]{2,1,0:T(8,128)} custom-call(s32[17]{0:T(128)} %get-tuple-element.26.rs_ref, s32[64]{0:T(128)} %get-tuple-element.9.ro_ref, s32[64]{0:T(128)} %get-tuple-element.16.td_ref, s32[17]{0:T(128)} %get-tuple-element.25.ss_ref, s32[128]{0:T(128)} %get-tuple-element.10.so_ref, ...), custom_call_target="tpu_custom_call", output_to_operand_aliasing={{}: (7, {})} | custom-call | flops 536870912 | bytes 23592960 | tf_op jit(solution)/shard_map/pallas_call | solution.py:176
  576.5 34.8 %all_to_all.24 = f32[128,4,256]{2,1,0:T(4,128)S(1)} all-to-all(f32[128,4,256]{2,1,0:T(4,128)S(1)} %broadcast_in_dim.19), channel_id=1, replica_groups=mesh['group'=2,'member'=64] {'group','member'}, dimensions={0} | all-to-all | bytes 1048576 | tf_op jit(solution)/shard_map/all_to_all | solution.py:258
  611.4 1.0 mul.54
  (43 shorter events, 1.2 us)
Async XLA Ops:
  0.6 289.6 %copy-start = (bf16[512,256]{1,0:T(8,128)(2,1)S(1)}, bf16[512,256]{1,0:T(8,128)(2,1)}, u32[]{:S(2)}) copy-start(bf16[512,256]{1,0:T(8,128)(2,1)} %param.16) | copy-start | bytes 786436
  3.4 17.9 %all-to-all-start = ((s32[128,1,1]{2,1,0:T(1,128)}), s32[128,1,1]{2,1,0:T(1,128)S(1)}, u32[]{:S(2)}, u32[]{:S(2)}) async-start(s32[128,1,1]{2,1,0:T(1,128)} %copy.33), calls=%async_computation | async-start | bytes 131072 | tf_op jit(solution)/shard_map/all_to_all | solution.py:207
  35.3 7.7 %copy-start.3 = (s32[64]{0:T(128)S(1)}, s32[64]{0:T(128)}, u32[]{:S(2)}) copy-start(s32[64]{0:T(128)} %broadcast_clamp_fusion.2.rhome_ref) | copy-start | bytes 772
  35.3 9.9 %copy-start.7 = (s32[64]{0:T(128)S(1)}, s32[64]{0:T(128)}, u32[]{:S(2)}) copy-start(s32[64]{0:T(128)} %param.10) | copy-start | bytes 772
  35.3 12.3 %copy-start.8 = (s32[64]{0:T(128)S(1)}, s32[64]{0:T(128)}, u32[]{:S(2)}) copy-start(s32[64]{0:T(128)} %param.11) | copy-start | bytes 772
  35.3 236.7 %all-to-all-start.1 = ((bf16[128,256,256]{2,1,0:T(8,128)(2,1)}), bf16[128,256,256]{2,1,0:T(8,128)(2,1)}, u32[]{:S(2)}, u32[]{:S(2)}) async-start(bf16[128,256,256]{2,1,0:T(8,128)(2,1)} %shard_map.112), calls=%async_computation.1 | async-start | bytes 33554432 | tf_op jit(solution)/shard_map/all_to_all | solution.py:227
  45.2 7.5 %copy-start.4 = (s32[64]{0:T(128)}, s32[64]{0:T(128)S(1)}, u32[]{:S(2)}) copy-start(s32[64]{0:T(128)S(1)} %broadcast_clamp_fusion.1.lh_ref) | copy-start | bytes 772
  47.7 5.1 copy-start.5
  288.3 1.9 copy-start.2
  288.3 2.2 copy-start.6
  311.6 246.9 %all-to-all-start.2 = ((bf16[128,264,256]{2,1,0:T(8,128)(2,1)}), bf16[128,264,256]{2,1,0:T(8,128)(2,1)}, u32[]{:S(2)}, u32[]{:S(2)}) async-start(bf16[128,264,256]{2,1,0:T(8,128)(2,1)} %shard_map.115), calls=%async_computation.2 | async-start | bytes 34603008 | tf_op jit(solution)/shard_map/all_to_all | solution.py:227
  559.9 52.5 %copy-start.1 = (bf16[512,256]{1,0:T(8,128)(2,1)S(1)}, bf16[512,256]{1,0:T(8,128)(2,1)}, u32[]{:S(2)}) copy-start(bf16[512,256]{1,0:T(8,128)(2,1)} %param.16) | copy-start | bytes 786436

commit v9 on v8

--- a/solution.py
+++ b/solution.py
@@ -246,9 +246,10 @@
     pieces_hi = hi_f32.astype(jnp.bfloat16)
     pieces_lo = (pieces - hi_f32).astype(jnp.bfloat16)
     extra = jnp.concatenate([pieces_hi, pieces_lo], axis=1)
-    grad_joined = jnp.einsum("rf,af->ra", grad_pre, weight, preferred_element_type=jnp.float32)
-    grad_agg = grad_joined[:, F:].astype(jnp.bfloat16).reshape(own_blocks, BLOCK, F)
-    init_b = grad_joined[:, :F].reshape(own_blocks, BLOCK, F)
+    grad_self = jnp.einsum("rf,af->ra", grad_pre, weight[:F], preferred_element_type=jnp.float32)
+    grad_nbr = jnp.einsum("rf,af->ra", grad_pre, weight[F:], preferred_element_type=jnp.float32)
+    grad_agg = grad_nbr.astype(jnp.bfloat16).reshape(own_blocks, BLOCK, F)
+    init_b = grad_self.reshape(own_blocks, BLOCK, F)
     grad_features, recv_b = apply_graph(grad_agg, init_b, extra)
     got = recv_b[:, 2 * BLOCK:, :].astype(jnp.float32)
     mine = jnp.sum(got[:, :chunk] + got[:, chunk:], axis=0)

time: 616 us -> 613 us (level)
  no operation moved by 1% of the time
where the time goes in v9:
time: 613 us; the launch traced here: 609 us
  waiting for transfers between devices  410 us (67%)
  Pallas kernels  88 us (14%)
  blocking collectives  34.9 us (6%)
  starting transfers between devices  34.5 us (6%)
  other arithmetic  22.8 us (4%)
  local copies, waits for them, and re-layouts  11.5 us (2%)
  matrix products  6.31 us (1%)
    all_to_all x2, waiting for transfers between devices, apply_graph(): lax.all_to_all(send, SLOT_AXES, split_axis=0, concat_axis=0, tiled=True)  406 us
    pallas_call x2, Pallas kernels, local_sum(): pl.pallas_call(_local_kernel, out_shape=jax.ShapeDtypeStruct(init.shape,...  35.1 us
    all_to_all x1, blocking collectives, body(): lax.all_to_all(spread_out, AXES, split_axis=0, concat_axis=0, tiled=True)  34.9 us
    pallas_call x2, Pallas kernels, post_sum(): pl.pallas_call(_post_kernel, out_shape=jax.ShapeDtypeStruct(base.shape, j...  32.7 us
    all_to_all x2, starting transfers between devices, apply_graph(): lax.all_to_all(send, SLOT_AXES, split_axis=0, concat_axis=0, tiled=True)  24 us
    pallas_call x2, Pallas kernels, build_send(): pl.pallas_call(_send_kernel, grid=(slots // group,), out_shape=jax.ShapeD...  20.2 us
  transfers between devices with their start and end apart: 3, of which 3 were waited for; matrix products, arithmetic and copies ran while one was open for 4% of the time, Pallas kernels for 6%

profile of v9, /device:TPU:41, one launch (start us, length us, event | category | flops | bytes accessed | tf_op | source)
XLA Modules:
  0.0 608.6 jit_solution(8848795798162270011)
XLA Ops:
  0.6 1.2 compare_select_fusion
  1.8 0.8 scatter_custom_fusion
  2.6 0.7 copy.33
  3.4 10.5 %all-to-all-start = ((s32[128,1,1]{2,1,0:T(1,128)}), s32[128,1,1]{2,1,0:T(1,128)S(1)}, u32[]{:S(2)}, u32[]{:S(2)}) async-start(s32[128,1,1]{2,1,0:T(1,128)} %copy.33), calls=%async_computation | async-start | bytes 131072 | tf_op jit(solution)/shard_map/all_to_all | solution.py:207
  13.8 1.2 broadcast_clamp_fusion.2.rhome_ref
  15.0 1.3 scatter_custom_fusion.1.spair_ref
  16.3 1.3 scatter_custom_fusion.2.sused_ref
  17.6 3.7 all-to-all-done
  21.3 2.4 clamp_reduce_fusion
  23.6 1.8 gather_fusion.1
  25.5 9.9 %shard_map.112 = bf16[128,256,256]{2,1,0:T(8,128)(2,1)} custom-call(s32[128]{0:T(128)} %gather_fusion.1, s32[128]{0:T(128)} %scatter_custom_fusion.1.spair_ref, s32[128]{0:T(128)} %scatter_custom_fusion.2.sused_ref, s32[64]{0:T(128)} %broadcast_clamp_fusion.2.rhome_ref, bf16[16,128,256]{2,1,0:T(8,128)(2,1)} %bitcast.23, bf16[64,128,128]{2,1,0:T(8,128)(2,1)} %rt_ref.7), custom_call_target="tpu_custom_call" | custom-call | flops 1073741824 | bytes 19922944 | tf_op jit(solution)/shard_map/pallas_call | solution.py:132
  35.3 7.7 %all-to-all-start.1 = ((bf16[128,256,256]{2,1,0:T(8,128)(2,1)}), bf16[128,256,256]{2,1,0:T(8,128)(2,1)}, u32[]{:S(2)}, u32[]{:S(2)}) async-start(bf16[128,256,256]{2,1,0:T(8,128)(2,1)} %shard_map.112), calls=%async_computation.1 | async-start | bytes 33554432 | tf_op jit(solution)/shard_map/all_to_all | solution.py:227
  43.1 2.0 sort.62
  45.1 2.1 sort.64
  47.5 0.1 reduce.4
  47.6 2.1 sort.65
  50.0 0.1 reduce.5
  50.3 0.1 reduce
  50.5 0.7 pad_add_fusion
  51.1 1.5 broadcast_in_dim.18.init_ref
  52.7 17.5 %shard_map.113.base_ref = f32[16,128,256]{2,1,0:T(8,128)} custom-call(s32[17]{0:T(128)} %get-tuple-element.24.hs_ref, s32[64]{0:T(128)} %get-tuple-element.11.ho_ref, s32[17]{0:T(128)} %get-tuple-element.23.ns_ref, s32[64]{0:T(128)} %get-tuple-element.12.no_ref, s32[64]{0:T(128)} %copy-done.3, s32[64]{0:T(128)} %copy-done.4, bf16[16,128,256]{2,1,0:T(8,128)(2,1)} %bitcast.24, ...), custom_call_target="tpu_custom_call" | custom-call | flops 1073741824 | bytes 7340032 | tf_op jit(solution)/shard_map/pallas_call | solution.py:87
  70.2 2.4 compare_reduce_fusion
  72.5 1.2 gather_fusion
  73.8 2.6 sort.63
  76.6 0.1 reduce.3
  76.7 0.6 pad_add_fusion.2
  77.3 194.7 %all-to-all-done.1.recv_ref = bf16[128,256,256]{2,1,0:T(8,128)(2,1)} async-done(((bf16[128,256,256]{2,1,0:T(8,128)(2,1)}), bf16[128,256,256]{2,1,0:T(8,128)(2,1)}, u32[]{:S(2)}, u32[]{:S(2)}) %all-to-all-start.1) | async-done | bytes 16777248 | tf_op jit(solution)/shard_map/all_to_all | solution.py:227
  272.0 16.3 %shard_map.114 = f32[16,128,256]{2,1,0:T(8,128)} custom-call(s32[17]{0:T(128)} %get-tuple-element.26.rs_ref, s32[64]{0:T(128)} %get-tuple-element.9.ro_ref, s32[64]{0:T(128)} %get-tuple-element.16.td_ref, s32[17]{0:T(128)} %get-tuple-element.25.ss_ref, s32[128]{0:T(128)} %get-tuple-element.10.so_ref, ...), custom_call_target="tpu_custom_call", output_to_operand_aliasing={{}: (7, {})} | custom-call | flops 536870912 | bytes 23068672 | tf_op jit(solution)/shard_map/pallas_call | solution.py:176
  288.3 1.9 convert_element_type.43
  290.2 0.3 copy-done.5
  290.6 2.3 multiply_convert_fusion
  292.9 0.7 fusion
  293.6 1.5 convolution_convert_fusion
  295.1 0.1 reshape.216
  295.2 0.9 gather_fusion.2
  296.1 0.2 reduce-precision_convert_fusion
  296.3 1.1 pad_maximum_fusion.3.rest_0_
  297.4 10.4 %shard_map.115 = bf16[128,264,256]{2,1,0:T(8,128)(2,1)} custom-call(s32[128]{0:T(128)} %gather_fusion.1, s32[128]{0:T(128)} %scatter_custom_fusion.1.spair_ref, s32[128]{0:T(128)} %scatter_custom_fusion.2.sused_ref, s32[64]{0:T(128)} %broadcast_clamp_fusion.2.rhome_ref, bf16[16,128,256]{2,1,0:T(8,128)(2,1)} %bitcast.19, bf16[64,128,128]{2,1,0:T(8,128)(2,1)} %rt_ref.7, ...), custom_call_target="tpu_custom_call" | custom-call | flops 1073741824 | bytes 20447232 | tf_op jit(solution)/shard_map/pallas_call | solution.py:132
  307.7 16.3 %all-to-all-start.2 = ((bf16[128,264,256]{2,1,0:T(8,128)(2,1)}), bf16[128,264,256]{2,1,0:T(8,128)(2,1)}, u32[]{:S(2)}, u32[]{:S(2)}) async-start(bf16[128,264,256]{2,1,0:T(8,128)(2,1)} %shard_map.115), calls=%async_computation.2 | async-start | bytes 34603008 | tf_op jit(solution)/shard_map/all_to_all | solution.py:227
  324.0 1.8 fusion.4
  325.8 17.5 %shard_map.116.base_ref = f32[16,128,256]{2,1,0:T(8,128)} custom-call(s32[17]{0:T(128)} %get-tuple-element.24.hs_ref, s32[64]{0:T(128)} %get-tuple-element.11.ho_ref, s32[17]{0:T(128)} %get-tuple-element.23.ns_ref, s32[64]{0:T(128)} %get-tuple-element.12.no_ref, s32[64]{0:T(128)} %copy-done.3, s32[64]{0:T(128)} %copy-done.4, bf16[16,128,256]{2,1,0:T(8,128)(2,1)} %bitcast.20, ...), custom_call_target="tpu_custom_call" | custom-call | flops 1073741824 | bytes 7340032 | tf_op jit(solution)/shard_map/pallas_call | solution.py:87
  343.3 211.5 %all-to-all-done.2.recv_ref = bf16[128,264,256]{2,1,0:T(8,128)(2,1)} async-done(((bf16[128,264,256]{2,1,0:T(8,128)(2,1)}), bf16[128,264,256]{2,1,0:T(8,128)(2,1)}, u32[]{:S(2)}, u32[]{:S(2)}) %all-to-all-start.2) | async-done | bytes 17301536 | tf_op jit(solution)/shard_map/all_to_all | solution.py:227
  554.8 1.1 slice_convert_fusion
  556.0 0.2 fusion.3
  556.2 16.4 %shard_map.117 = f32[16,128,256]{2,1,0:T(8,128)} custom-call(s32[17]{0:T(128)} %get-tuple-element.26.rs_ref, s32[64]{0:T(128)} %get-tuple-element.9.ro_ref, s32[64]{0:T(128)} %get-tuple-element.16.td_ref, s32[17]{0:T(128)} %get-tuple-element.25.ss_ref, s32[128]{0:T(128)} %get-tuple-element.10.so_ref, ...), custom_call_target="tpu_custom_call", output_to_operand_aliasing={{}: (7, {})} | custom-call | flops 536870912 | bytes 23592960 | tf_op jit(solution)/shard_map/pallas_call | solution.py:176
  572.7 34.9 %all_to_all.24 = f32[128,4,256]{2,1,0:T(4,128)S(1)} all-to-all(f32[128,4,256]{2,1,0:T(4,128)S(1)} %broadcast_in_dim.19), channel_id=1, replica_groups=mesh['group'=2,'member'=64] {'group','member'}, dimensions={0} | all-to-all | bytes 1048576 | tf_op jit(solution)/shard_map/all_to_all | solution.py:259
  607.5 0.1 broadcast_multiply_fusion
  607.7 1.0 mul.54
  (40 shorter events, 1.1 us)
Async XLA Ops:
  3.4 17.9 %all-to-all-start = ((s32[128,1,1]{2,1,0:T(1,128)}), s32[128,1,1]{2,1,0:T(1,128)S(1)}, u32[]{:S(2)}, u32[]{:S(2)}) async-start(s32[128,1,1]{2,1,0:T(1,128)} %copy.33), calls=%async_computation | async-start | bytes 131072 | tf_op jit(solution)/shard_map/all_to_all | solution.py:207
  35.3 7.7 %copy-start.2 = (s32[64]{0:T(128)S(1)}, s32[64]{0:T(128)}, u32[]{:S(2)}) copy-start(s32[64]{0:T(128)} %broadcast_clamp_fusion.2.rhome_ref) | copy-start | bytes 772
  35.3 9.8 %copy-start.6 = (s32[64]{0:T(128)S(1)}, s32[64]{0:T(128)}, u32[]{:S(2)}) copy-start(s32[64]{0:T(128)} %param.10) | copy-start | bytes 772
  35.3 12.3 %copy-start.7 = (s32[64]{0:T(128)S(1)}, s32[64]{0:T(128)}, u32[]{:S(2)}) copy-start(s32[64]{0:T(128)} %param.11) | copy-start | bytes 772
  35.3 236.7 %all-to-all-start.1 = ((bf16[128,256,256]{2,1,0:T(8,128)(2,1)}), bf16[128,256,256]{2,1,0:T(8,128)(2,1)}, u32[]{:S(2)}, u32[]{:S(2)}) async-start(bf16[128,256,256]{2,1,0:T(8,128)(2,1)} %shard_map.112), calls=%async_computation.1 | async-start | bytes 33554432 | tf_op jit(solution)/shard_map/all_to_all | solution.py:227
  45.1 7.5 %copy-start.3 = (s32[64]{0:T(128)}, s32[64]{0:T(128)S(1)}, u32[]{:S(2)}) copy-start(s32[64]{0:T(128)S(1)} %broadcast_clamp_fusion.1.lh_ref) | copy-start | bytes 772
  47.6 5.0 copy-start.4
  288.3 1.9 copy-start
  288.3 1.9 copy-start.1
  288.3 2.2 copy-start.5
  307.7 247.1 %all-to-all-start.2 = ((bf16[128,264,256]{2,1,0:T(8,128)(2,1)}), bf16[128,264,256]{2,1,0:T(8,128)(2,1)}, u32[]{:S(2)}, u32[]{:S(2)}) async-start(bf16[128,264,256]{2,1,0:T(8,128)(2,1)} %shard_map.115), calls=%async_computation.2 | async-start | bytes 34603008 | tf_op jit(solution)/shard_map/all_to_all | solution.py:227

commit v10 on v9

--- a/solution.py
+++ b/solution.py
@@ -160,13 +160,13 @@
             return a + recv_ref[so_ref[i], pl.ds(BLOCK, BLOCK)].astype(jnp.float32)
 
         acc = lax.fori_loop(ss_ref[k], ss_ref[k + 1], back_term, acc)
-        out_ref[k] = acc
+        out_ref[k] = acc.astype(out_ref.dtype)
         return c
 
     lax.fori_loop(0, blocks, per_block, 0)
 
 
-def post_sum(rs, ro, td, ss, so, rtiles, recv, base):
+def post_sum(rs, ro, td, ss, so, rtiles, recv, base, out_dtype=jnp.float32):
     pairs = rtiles.shape[0]
     cost = pl.CostEstimate(
         flops=2 * pairs * BLOCK * BLOCK * F,
@@ -175,11 +175,11 @@
     )
     return pl.pallas_call(
         _post_kernel,
-        out_shape=jax.ShapeDtypeStruct(base.shape, jnp.float32),
+        out_shape=jax.ShapeDtypeStruct(base.shape, out_dtype),
         in_specs=[_smem()] * 5 + [_vmem()] * 3,
         out_specs=_vmem(),
         cost_estimate=cost,
-        input_output_aliases={7: 0},
+        input_output_aliases={7: 0} if out_dtype == base.dtype else {},
         compiler_params=pltpu.CompilerParams(vmem_limit_bytes=VMEM_LIMIT),
     )(rs, ro, td, ss, so, rtiles, recv, base)
 
@@ -222,15 +222,16 @@
     r_order, r_starts = _lists(rhome, own_blocks)
     s_order, s_starts = _lists(back_dest, own_blocks)
 
-    def apply_graph(blocks_in, init, extra=None):
+    def apply_graph(blocks_in, init, extra=None, out_dtype=jnp.float32):
         send = build_send(picked, slot_pair, slot_used, rhome, blocks_in, remote_tiles, extra)
         recv = lax.all_to_all(send, SLOT_AXES, split_axis=0, concat_axis=0, tiled=True)
         part = local_sum(h_starts, h_order, n_starts, n_order, lhome, lnear, blocks_in, local_tiles, init)
-        total = post_sum(r_starts, r_order, target_slot, s_starts, s_order, remote_tiles, recv, part)
+        total = post_sum(r_starts, r_order, target_slot, s_starts, s_order, remote_tiles, recv, part,
+                         out_dtype)
         return total.reshape(row_count, F), recv
 
     zeros = jnp.zeros((own_blocks, BLOCK, F), jnp.float32)
-    aggregate = apply_graph(features.reshape(own_blocks, BLOCK, F), zeros)[0].astype(jnp.bfloat16)
+    aggregate = apply_graph(features.reshape(own_blocks, BLOCK, F), zeros, out_dtype=jnp.bfloat16)[0]
     joined = jnp.concatenate([features, aggregate], axis=1)
     pre_act = jnp.dot(joined, weight, preferred_element_type=jnp.float32)
     sigmoid_z = jax.nn.sigmoid(pre_act)

time: 613 us -> 612 us (level)
  no operation moved by 1% of the time
where the time goes in v10:
time: 612 us; the launch traced here: 608 us
  waiting for transfers between devices  410 us (67%)
  Pallas kernels  88.8 us (15%)
  blocking collectives  35.1 us (6%)
  starting transfers between devices  34.3 us (6%)
  other arithmetic  20.9 us (3%)
  local copies, waits for them, and re-layouts  11.1 us (2%)
  matrix products  7.57 us (1%)
    all_to_all x2, waiting for transfers between devices, apply_graph(): lax.all_to_all(send, SLOT_AXES, split_axis=0, concat_axis=0, tiled=True)  406 us
    pallas_call x2, Pallas kernels, local_sum(): pl.pallas_call(_local_kernel, out_shape=jax.ShapeDtypeStruct(init.shape,...  35.4 us
    all_to_all x1, blocking collectives, body(): lax.all_to_all(spread_out, AXES, split_axis=0, concat_axis=0, tiled=True)  35.1 us
    pallas_call x2, Pallas kernels, post_sum(): pl.pallas_call(_post_kernel, out_shape=jax.ShapeDtypeStruct(base.shape, o...  33.2 us
    all_to_all x2, starting transfers between devices, apply_graph(): lax.all_to_all(send, SLOT_AXES, split_axis=0, concat_axis=0, tiled=True)  23.8 us
    pallas_call x2, Pallas kernels, build_send(): pl.pallas_call(_send_kernel, grid=(slots // group,), out_shape=jax.ShapeD...  20.2 us
  transfers between devices with their start and end apart: 3, of which 3 were waited for; matrix products, arithmetic and copies ran while one was open for 4% of the time, Pallas kernels for 6%

profile of v10, /device:TPU:41, one launch (start us, length us, event | category | flops | bytes accessed | tf_op | source)
XLA Modules:
  0.0 608.2 jit_solution(14722354763357065588)
XLA Ops:
  0.6 1.2 compare_select_fusion
  1.8 0.8 scatter_custom_fusion
  2.6 0.7 copy.32
  3.4 10.5 %all-to-all-start = ((s32[128,1,1]{2,1,0:T(1,128)}), s32[128,1,1]{2,1,0:T(1,128)S(1)}, u32[]{:S(2)}, u32[]{:S(2)}) async-start(s32[128,1,1]{2,1,0:T(1,128)} %copy.32), calls=%async_computation | async-start | bytes 131072 | tf_op jit(solution)/shard_map/all_to_all | solution.py:207
  13.8 1.2 broadcast_clamp_fusion.2.rhome_ref
  15.0 1.3 scatter_custom_fusion.1.spair_ref
  16.3 1.3 scatter_custom_fusion.2.sused_ref
  17.6 3.7 all-to-all-done
  21.3 2.4 clamp_reduce_fusion
  23.6 1.8 gather_fusion.1
  25.5 9.9 %shard_map.112 = bf16[128,256,256]{2,1,0:T(8,128)(2,1)} custom-call(s32[128]{0:T(128)} %gather_fusion.1, s32[128]{0:T(128)} %scatter_custom_fusion.1.spair_ref, s32[128]{0:T(128)} %scatter_custom_fusion.2.sused_ref, s32[64]{0:T(128)} %broadcast_clamp_fusion.2.rhome_ref, bf16[16,128,256]{2,1,0:T(8,128)(2,1)} %bitcast.23, bf16[64,128,128]{2,1,0:T(8,128)(2,1)} %rt_ref.7), custom_call_target="tpu_custom_call" | custom-call | flops 1073741824 | bytes 19922944 | tf_op jit(solution)/shard_map/pallas_call | solution.py:132
  35.3 7.7 %all-to-all-start.1 = ((bf16[128,256,256]{2,1,0:T(8,128)(2,1)}), bf16[128,256,256]{2,1,0:T(8,128)(2,1)}, u32[]{:S(2)}, u32[]{:S(2)}) async-start(bf16[128,256,256]{2,1,0:T(8,128)(2,1)} %shard_map.112), calls=%async_computation.1 | async-start | bytes 33554432 | tf_op jit(solution)/shard_map/all_to_all | solution.py:227
  43.1 2.0 sort.62
  45.1 2.1 sort.64
  47.2 0.1 convert_reduce_fusion.1
  47.5 0.1 reduce.4
  47.6 2.1 sort.65
  49.7 0.1 convert_reduce_fusion
  50.0 0.1 reduce.5
  50.3 0.1 reduce
  50.5 0.7 pad_add_fusion
  51.1 1.5 broadcast_in_dim.18.init_ref
  52.7 17.7 %shard_map.113.base_ref = f32[16,128,256]{2,1,0:T(8,128)} custom-call(s32[17]{0:T(128)} %get-tuple-element.24.hs_ref, s32[64]{0:T(128)} %get-tuple-element.11.ho_ref, s32[17]{0:T(128)} %get-tuple-element.23.ns_ref, s32[64]{0:T(128)} %get-tuple-element.12.no_ref, s32[64]{0:T(128)} %copy-done.4, s32[64]{0:T(128)} %copy-done.5, bf16[16,128,256]{2,1,0:T(8,128)(2,1)} %bitcast.24, ...), custom_call_target="tpu_custom_call" | custom-call | flops 1073741824 | bytes 7340032 | tf_op jit(solution)/shard_map/pallas_call | solution.py:87
  70.4 2.4 compare_reduce_fusion
  72.7 1.2 gather_fusion
  74.0 2.6 sort.63
  76.8 0.1 reduce.3
  76.9 0.6 pad_add_fusion.2
  77.5 194.5 %all-to-all-done.1.recv_ref = bf16[128,256,256]{2,1,0:T(8,128)(2,1)} async-done(((bf16[128,256,256]{2,1,0:T(8,128)(2,1)}), bf16[128,256,256]{2,1,0:T(8,128)(2,1)}, u32[]{:S(2)}, u32[]{:S(2)}) %all-to-all-start.1) | async-done | bytes 16777248 | tf_op jit(solution)/shard_map/all_to_all | solution.py:227
  272.0 16.4 %shard_map.114 = bf16[16,128,256]{2,1,0:T(8,128)(2,1)} custom-call(s32[17]{0:T(128)} %get-tuple-element.26.rs_ref, s32[64]{0:T(128)} %get-tuple-element.9.ro_ref, s32[64]{0:T(128)} %get-tuple-element.16.td_ref, s32[17]{0:T(128)} %get-tuple-element.25.ss_ref, s32[128]{0:T(128)} %get-tuple-element.10.so_ref, bf16[64,128,128]{2,1,0:T(8,128)(2,1)} %rt_ref.7, ...), custom_call_target="tpu_custom_call" | custom-call | flops 536870912 | bytes 23068672 | tf_op jit(solution)/shard_map/pallas_call | solution.py:176
  288.4 3.6 multiply_convert_fusion
  292.0 0.7 fusion
  292.7 1.5 convolution_convert_fusion
  294.2 0.1 reshape.218
  294.4 0.9 gather_fusion.2
  295.3 0.2 reduce-precision_convert_fusion
  295.4 1.1 pad_maximum_fusion.3.rest_0_
  296.5 10.4 %shard_map.115 = bf16[128,264,256]{2,1,0:T(8,128)(2,1)} custom-call(s32[128]{0:T(128)} %gather_fusion.1, s32[128]{0:T(128)} %scatter_custom_fusion.1.spair_ref, s32[128]{0:T(128)} %scatter_custom_fusion.2.sused_ref, s32[64]{0:T(128)} %broadcast_clamp_fusion.2.rhome_ref, bf16[16,128,256]{2,1,0:T(8,128)(2,1)} %bitcast.19, bf16[64,128,128]{2,1,0:T(8,128)(2,1)} %rt_ref.7, ...), custom_call_target="tpu_custom_call" | custom-call | flops 1073741824 | bytes 20447232 | tf_op jit(solution)/shard_map/pallas_call | solution.py:132
  306.9 16.1 %all-to-all-start.2 = ((bf16[128,264,256]{2,1,0:T(8,128)(2,1)}), bf16[128,264,256]{2,1,0:T(8,128)(2,1)}, u32[]{:S(2)}, u32[]{:S(2)}) async-start(bf16[128,264,256]{2,1,0:T(8,128)(2,1)} %shard_map.115), calls=%async_computation.2 | async-start | bytes 34603008 | tf_op jit(solution)/shard_map/all_to_all | solution.py:227
  323.0 1.8 fusion.4
  324.8 17.7 %shard_map.116.base_ref = f32[16,128,256]{2,1,0:T(8,128)} custom-call(s32[17]{0:T(128)} %get-tuple-element.24.hs_ref, s32[64]{0:T(128)} %get-tuple-element.11.ho_ref, s32[17]{0:T(128)} %get-tuple-element.23.ns_ref, s32[64]{0:T(128)} %get-tuple-element.12.no_ref, s32[64]{0:T(128)} %copy-done.4, s32[64]{0:T(128)} %copy-done.5, bf16[16,128,256]{2,1,0:T(8,128)(2,1)} %bitcast.20, ...), custom_call_target="tpu_custom_call" | custom-call | flops 1073741824 | bytes 7340032 | tf_op jit(solution)/shard_map/pallas_call | solution.py:87
  342.5 211.3 %all-to-all-done.2.recv_ref = bf16[128,264,256]{2,1,0:T(8,128)(2,1)} async-done(((bf16[128,264,256]{2,1,0:T(8,128)(2,1)}), bf16[128,264,256]{2,1,0:T(8,128)(2,1)}, u32[]{:S(2)}, u32[]{:S(2)}) %all-to-all-start.2) | async-done | bytes 17301536 | tf_op jit(solution)/shard_map/all_to_all | solution.py:227
  553.8 1.1 slice_convert_fusion
  554.9 0.2 fusion.3
  555.1 16.8 %shard_map.117 = f32[16,128,256]{2,1,0:T(8,128)} custom-call(s32[17]{0:T(128)} %get-tuple-element.26.rs_ref, s32[64]{0:T(128)} %get-tuple-element.9.ro_ref, s32[64]{0:T(128)} %get-tuple-element.16.td_ref, s32[17]{0:T(128)} %get-tuple-element.25.ss_ref, s32[128]{0:T(128)} %get-tuple-element.10.so_ref, ...), custom_call_target="tpu_custom_call", output_to_operand_aliasing={{}: (7, {})} | custom-call | flops 536870912 | bytes 23592960 | tf_op jit(solution)/shard_map/pallas_call | solution.py:176
  572.0 35.1 %all_to_all.24 = f32[128,4,256]{2,1,0:T(4,128)S(1)} all-to-all(f32[128,4,256]{2,1,0:T(4,128)S(1)} %broadcast_in_dim.19), channel_id=1, replica_groups=mesh['group'=2,'member'=64] {'group','member'}, dimensions={0} | all-to-all | bytes 1048576 | tf_op jit(solution)/shard_map/all_to_all | solution.py:260
  607.1 0.1 broadcast_multiply_fusion
  607.2 1.0 mul.54
  (41 shorter events, 0.9 us)
Async XLA Ops:
  3.4 17.9 %all-to-all-start = ((s32[128,1,1]{2,1,0:T(1,128)}), s32[128,1,1]{2,1,0:T(1,128)S(1)}, u32[]{:S(2)}, u32[]{:S(2)}) async-start(s32[128,1,1]{2,1,0:T(1,128)} %copy.32), calls=%async_computation | async-start | bytes 131072 | tf_op jit(solution)/shard_map/all_to_all | solution.py:207
  35.3 7.7 %copy-start.3 = (s32[64]{0:T(128)S(1)}, s32[64]{0:T(128)}, u32[]{:S(2)}) copy-start(s32[64]{0:T(128)} %broadcast_clamp_fusion.2.rhome_ref) | copy-start | bytes 772
  35.3 9.8 %copy-start.7 = (s32[64]{0:T(128)S(1)}, s32[64]{0:T(128)}, u32[]{:S(2)}) copy-start(s32[64]{0:T(128)} %param.10) | copy-start | bytes 772
  35.3 12.3 %copy-start.8 = (s32[64]{0:T(128)S(1)}, s32[64]{0:T(128)}, u32[]{:S(2)}) copy-start(s32[64]{0:T(128)} %param.11) | copy-start | bytes 772
  35.3 236.7 %all-to-all-start.1 = ((bf16[128,256,256]{2,1,0:T(8,128)(2,1)}), bf16[128,256,256]{2,1,0:T(8,128)(2,1)}, u32[]{:S(2)}, u32[]{:S(2)}) async-start(bf16[128,256,256]{2,1,0:T(8,128)(2,1)} %shard_map.112), calls=%async_computation.1 | async-start | bytes 33554432 | tf_op jit(solution)/shard_map/all_to_all | solution.py:227
  45.1 7.5 %copy-start.4 = (s32[64]{0:T(128)}, s32[64]{0:T(128)S(1)}, u32[]{:S(2)}) copy-start(s32[64]{0:T(128)S(1)} %broadcast_clamp_fusion.1.lh_ref) | copy-start | bytes 772
  47.6 5.0 copy-start.5
  272.0 16.4 %copy-start = (bf16[2048,256]{1,0:T(8,128)(2,1)S(1)}, bf16[2048,256]{1,0:T(8,128)(2,1)}, u32[]{:S(2)}) copy-start(bf16[2048,256]{1,0:T(8,128)(2,1)} %param.9) | copy-start | bytes 3145732
  272.0 16.4 %copy-start.2 = (bf16[512,256]{1,0:T(8,128)(2,1)S(1)}, bf16[512,256]{1,0:T(8,128)(2,1)}, u32[]{:S(2)}) copy-start(bf16[512,256]{1,0:T(8,128)(2,1)} %param.16) | copy-start | bytes 786436
  272.0 16.4 %copy-start.6 = (bf16[2048,256]{1,0:T(8,128)(2,1)S(1)}, bf16[2048,256]{1,0:T(8,128)(2,1)}, u32[]{:S(2)}) copy-start(bf16[2048,256]{1,0:T(8,128)(2,1)} %param.17) | copy-start | bytes 3145732
  288.4 3.6 copy-start.1
  306.9 246.9 %all-to-all-start.2 = ((bf16[128,264,256]{2,1,0:T(8,128)(2,1)}), bf16[128,264,256]{2,1,0:T(8,128)(2,1)}, u32[]{:S(2)}, u32[]{:S(2)}) async-start(bf16[128,264,256]{2,1,0:T(8,128)(2,1)} %shard_map.115), calls=%async_computation.2 | async-start | bytes 34603008 | tf_op jit(solution)/shard_map/all_to_all | solution.py:227

commit v11 on v10

--- a/solution.py
+++ b/solution.py
@@ -94,7 +94,7 @@
     )(hs, ho, ns, no, lh, ln, x, ltiles, init)
 
 
-SEND_GROUP = 16
+SEND_GROUP = 32
 
 
 def _send_kernel(picked_ref, spair_ref, sused_ref, rhome_ref, x_ref, rt_ref, *rest):

time: 612 us -> 608 us (level)
  no operation moved by 1% of the time
where the time goes in v11:
time: 608 us; the launch traced here: 604 us
  waiting for transfers between devices  409 us (67%)
  Pallas kernels  84.8 us (14%)
  blocking collectives  35.1 us (6%)
  starting transfers between devices  34.7 us (6%)
  other arithmetic  20.9 us (3%)
  local copies, waits for them, and re-layouts  11.1 us (2%)
  matrix products  7.58 us (1%)
    all_to_all x2, waiting for transfers between devices, apply_graph(): lax.all_to_all(send, SLOT_AXES, split_axis=0, concat_axis=0, tiled=True)  406 us
    pallas_call x2, Pallas kernels, local_sum(): pl.pallas_call(_local_kernel, out_shape=jax.ShapeDtypeStruct(init.shape,...  35.7 us
    all_to_all x1, blocking collectives, body(): lax.all_to_all(spread_out, AXES, split_axis=0, concat_axis=0, tiled=True)  35.1 us
    pallas_call x2, Pallas kernels, post_sum(): pl.pallas_call(_post_kernel, out_shape=jax.ShapeDtypeStruct(base.shape, o...  31.7 us
    all_to_all x2, starting transfers between devices, apply_graph(): lax.all_to_all(send, SLOT_AXES, split_axis=0, concat_axis=0, tiled=True)  24.2 us
    pallas_call x2, Pallas kernels, build_send(): pl.pallas_call(_send_kernel, grid=(slots // group,), out_shape=jax.ShapeD...  17.4 us
  transfers between devices with their start and end apart: 3, of which 3 were waited for; matrix products, arithmetic and copies ran while one was open for 4% of the time, Pallas kernels for 6%

profile of v11, /device:TPU:41, one launch (start us, length us, event | category | flops | bytes accessed | tf_op | source)
XLA Modules:
  0.0 604.3 jit_solution(3126552587226012070)
XLA Ops:
  0.6 1.2 compare_select_fusion
  1.8 0.8 scatter_custom_fusion
  2.6 0.7 copy.32
  3.4 10.5 %all-to-all-start = ((s32[128,1,1]{2,1,0:T(1,128)}), s32[128,1,1]{2,1,0:T(1,128)S(1)}, u32[]{:S(2)}, u32[]{:S(2)}) async-start(s32[128,1,1]{2,1,0:T(1,128)} %copy.32), calls=%async_computation | async-start | bytes 131072 | tf_op jit(solution)/shard_map/all_to_all | solution.py:207
  13.8 1.2 broadcast_clamp_fusion.2.rhome_ref
  15.0 1.3 scatter_custom_fusion.1.spair_ref
  16.3 1.3 scatter_custom_fusion.2.sused_ref
  17.6 3.7 all-to-all-done
  21.3 2.4 clamp_reduce_fusion
  23.6 1.8 gather_fusion.1
  25.5 8.6 %shard_map.112 = bf16[128,256,256]{2,1,0:T(8,128)(2,1)} custom-call(s32[128]{0:T(128)} %gather_fusion.1, s32[128]{0:T(128)} %scatter_custom_fusion.1.spair_ref, s32[128]{0:T(128)} %scatter_custom_fusion.2.sused_ref, s32[64]{0:T(128)} %broadcast_clamp_fusion.2.rhome_ref, bf16[16,128,256]{2,1,0:T(8,128)(2,1)} %bitcast.23, bf16[64,128,128]{2,1,0:T(8,128)(2,1)} %rt_ref.7), custom_call_target="tpu_custom_call" | custom-call | flops 1073741824 | bytes 19922944 | tf_op jit(solution)/shard_map/pallas_call | solution.py:132
  34.1 7.7 %all-to-all-start.1 = ((bf16[128,256,256]{2,1,0:T(8,128)(2,1)}), bf16[128,256,256]{2,1,0:T(8,128)(2,1)}, u32[]{:S(2)}, u32[]{:S(2)}) async-start(bf16[128,256,256]{2,1,0:T(8,128)(2,1)} %shard_map.112), calls=%async_computation.1 | async-start | bytes 33554432 | tf_op jit(solution)/shard_map/all_to_all | solution.py:227
  41.8 2.0 sort.62
  43.9 2.1 sort.64
  46.0 0.1 convert_reduce_fusion.1
  46.2 0.1 reduce.4
  46.4 2.1 sort.65
  48.5 0.1 convert_reduce_fusion
  48.7 0.1 reduce.5
  48.8 0.1 convert_reduce_fusion.3
  49.1 0.1 reduce
  49.2 0.7 pad_add_fusion
  49.8 1.5 broadcast_in_dim.18.init_ref
  51.4 17.8 %shard_map.113.base_ref = f32[16,128,256]{2,1,0:T(8,128)} custom-call(s32[17]{0:T(128)} %get-tuple-element.24.hs_ref, s32[64]{0:T(128)} %get-tuple-element.11.ho_ref, s32[17]{0:T(128)} %get-tuple-element.23.ns_ref, s32[64]{0:T(128)} %get-tuple-element.12.no_ref, s32[64]{0:T(128)} %copy-done.4, s32[64]{0:T(128)} %copy-done.5, bf16[16,128,256]{2,1,0:T(8,128)(2,1)} %bitcast.24, ...), custom_call_target="tpu_custom_call" | custom-call | flops 1073741824 | bytes 7340032 | tf_op jit(solution)/shard_map/pallas_call | solution.py:87
  69.2 2.4 compare_reduce_fusion
  71.6 1.2 gather_fusion
  72.8 2.6 sort.63
  75.6 0.1 reduce.3
  75.8 0.6 pad_add_fusion.2
  76.4 194.4 %all-to-all-done.1.recv_ref = bf16[128,256,256]{2,1,0:T(8,128)(2,1)} async-done(((bf16[128,256,256]{2,1,0:T(8,128)(2,1)}), bf16[128,256,256]{2,1,0:T(8,128)(2,1)}, u32[]{:S(2)}, u32[]{:S(2)}) %all-to-all-start.1) | async-done | bytes 16777248 | tf_op jit(solution)/shard_map/all_to_all | solution.py:227
  270.8 15.6 %shard_map.114 = bf16[16,128,256]{2,1,0:T(8,128)(2,1)} custom-call(s32[17]{0:T(128)} %get-tuple-element.26.rs_ref, s32[64]{0:T(128)} %get-tuple-element.9.ro_ref, s32[64]{0:T(128)} %get-tuple-element.16.td_ref, s32[17]{0:T(128)} %get-tuple-element.25.ss_ref, s32[128]{0:T(128)} %get-tuple-element.10.so_ref, bf16[64,128,128]{2,1,0:T(8,128)(2,1)} %rt_ref.7, ...), custom_call_target="tpu_custom_call" | custom-call | flops 536870912 | bytes 23068672 | tf_op jit(solution)/shard_map/pallas_call | solution.py:176
  286.4 3.6 multiply_convert_fusion
  290.0 0.7 fusion
  290.7 1.5 convolution_convert_fusion
  292.2 0.1 reshape.218
  292.4 0.9 gather_fusion.2
  293.2 0.2 reduce-precision_convert_fusion
  293.4 1.1 pad_maximum_fusion.3.rest_0_
  294.5 8.8 %shard_map.115 = bf16[128,264,256]{2,1,0:T(8,128)(2,1)} custom-call(s32[128]{0:T(128)} %gather_fusion.1, s32[128]{0:T(128)} %scatter_custom_fusion.1.spair_ref, s32[128]{0:T(128)} %scatter_custom_fusion.2.sused_ref, s32[64]{0:T(128)} %broadcast_clamp_fusion.2.rhome_ref, bf16[16,128,256]{2,1,0:T(8,128)(2,1)} %bitcast.19, bf16[64,128,128]{2,1,0:T(8,128)(2,1)} %rt_ref.7, ...), custom_call_target="tpu_custom_call" | custom-call | flops 1073741824 | bytes 20447232 | tf_op jit(solution)/shard_map/pallas_call | solution.py:132
  303.3 16.5 %all-to-all-start.2 = ((bf16[128,264,256]{2,1,0:T(8,128)(2,1)}), bf16[128,264,256]{2,1,0:T(8,128)(2,1)}, u32[]{:S(2)}, u32[]{:S(2)}) async-start(bf16[128,264,256]{2,1,0:T(8,128)(2,1)} %shard_map.115), calls=%async_computation.2 | async-start | bytes 34603008 | tf_op jit(solution)/shard_map/all_to_all | solution.py:227
  319.8 1.8 fusion.4
  321.6 17.8 %shard_map.116.base_ref = f32[16,128,256]{2,1,0:T(8,128)} custom-call(s32[17]{0:T(128)} %get-tuple-element.24.hs_ref, s32[64]{0:T(128)} %get-tuple-element.11.ho_ref, s32[17]{0:T(128)} %get-tuple-element.23.ns_ref, s32[64]{0:T(128)} %get-tuple-element.12.no_ref, s32[64]{0:T(128)} %copy-done.4, s32[64]{0:T(128)} %copy-done.5, bf16[16,128,256]{2,1,0:T(8,128)(2,1)} %bitcast.20, ...), custom_call_target="tpu_custom_call" | custom-call | flops 1073741824 | bytes 7340032 | tf_op jit(solution)/shard_map/pallas_call | solution.py:87
  339.5 211.2 %all-to-all-done.2.recv_ref = bf16[128,264,256]{2,1,0:T(8,128)(2,1)} async-done(((bf16[128,264,256]{2,1,0:T(8,128)(2,1)}), bf16[128,264,256]{2,1,0:T(8,128)(2,1)}, u32[]{:S(2)}, u32[]{:S(2)}) %all-to-all-start.2) | async-done | bytes 17301536 | tf_op jit(solution)/shard_map/all_to_all | solution.py:227
  550.6 1.1 slice_convert_fusion
  551.8 0.2 fusion.3
  552.0 16.1 %shard_map.117 = f32[16,128,256]{2,1,0:T(8,128)} custom-call(s32[17]{0:T(128)} %get-tuple-element.26.rs_ref, s32[64]{0:T(128)} %get-tuple-element.9.ro_ref, s32[64]{0:T(128)} %get-tuple-element.16.td_ref, s32[17]{0:T(128)} %get-tuple-element.25.ss_ref, s32[128]{0:T(128)} %get-tuple-element.10.so_ref, ...), custom_call_target="tpu_custom_call", output_to_operand_aliasing={{}: (7, {})} | custom-call | flops 536870912 | bytes 23592960 | tf_op jit(solution)/shard_map/pallas_call | solution.py:176
  568.1 35.1 %all_to_all.24 = f32[128,4,256]{2,1,0:T(4,128)S(1)} all-to-all(f32[128,4,256]{2,1,0:T(4,128)S(1)} %broadcast_in_dim.19), channel_id=1, replica_groups=mesh['group'=2,'member'=64] {'group','member'}, dimensions={0} | all-to-all | bytes 1048576 | tf_op jit(solution)/shard_map/all_to_all | solution.py:260
  603.4 1.0 mul.54
  (41 shorter events, 0.9 us)
Async XLA Ops:
  3.4 17.9 %all-to-all-start = ((s32[128,1,1]{2,1,0:T(1,128)}), s32[128,1,1]{2,1,0:T(1,128)S(1)}, u32[]{:S(2)}, u32[]{:S(2)}) async-start(s32[128,1,1]{2,1,0:T(1,128)} %copy.32), calls=%async_computation | async-start | bytes 131072 | tf_op jit(solution)/shard_map/all_to_all | solution.py:207
  34.0 7.7 %copy-start.3 = (s32[64]{0:T(128)S(1)}, s32[64]{0:T(128)}, u32[]{:S(2)}) copy-start(s32[64]{0:T(128)} %broadcast_clamp_fusion.2.rhome_ref) | copy-start | bytes 772
  34.0 9.8 %copy-start.7 = (s32[64]{0:T(128)S(1)}, s32[64]{0:T(128)}, u32[]{:S(2)}) copy-start(s32[64]{0:T(128)} %param.10) | copy-start | bytes 772
  34.0 12.3 %copy-start.8 = (s32[64]{0:T(128)S(1)}, s32[64]{0:T(128)}, u32[]{:S(2)}) copy-start(s32[64]{0:T(128)} %param.11) | copy-start | bytes 772
  34.1 236.7 %all-to-all-start.1 = ((bf16[128,256,256]{2,1,0:T(8,128)(2,1)}), bf16[128,256,256]{2,1,0:T(8,128)(2,1)}, u32[]{:S(2)}, u32[]{:S(2)}) async-start(bf16[128,256,256]{2,1,0:T(8,128)(2,1)} %shard_map.112), calls=%async_computation.1 | async-start | bytes 33554432 | tf_op jit(solution)/shard_map/all_to_all | solution.py:227
  43.8 7.5 %copy-start.4 = (s32[64]{0:T(128)}, s32[64]{0:T(128)S(1)}, u32[]{:S(2)}) copy-start(s32[64]{0:T(128)S(1)} %broadcast_clamp_fusion.1.lh_ref) | copy-start | bytes 772
  46.3 5.0 copy-start.5
  270.7 15.6 %copy-start = (bf16[2048,256]{1,0:T(8,128)(2,1)S(1)}, bf16[2048,256]{1,0:T(8,128)(2,1)}, u32[]{:S(2)}) copy-start(bf16[2048,256]{1,0:T(8,128)(2,1)} %param.9) | copy-start | bytes 3145732
  270.7 15.6 %copy-start.2 = (bf16[512,256]{1,0:T(8,128)(2,1)S(1)}, bf16[512,256]{1,0:T(8,128)(2,1)}, u32[]{:S(2)}) copy-start(bf16[512,256]{1,0:T(8,128)(2,1)} %param.16) | copy-start | bytes 786436
  270.7 15.6 %copy-start.6 = (bf16[2048,256]{1,0:T(8,128)(2,1)S(1)}, bf16[2048,256]{1,0:T(8,128)(2,1)}, u32[]{:S(2)}) copy-start(bf16[2048,256]{1,0:T(8,128)(2,1)} %param.17) | copy-start | bytes 3145732
  286.4 3.6 copy-start.1
  303.3 247.3 %all-to-all-start.2 = ((bf16[128,264,256]{2,1,0:T(8,128)(2,1)}), bf16[128,264,256]{2,1,0:T(8,128)(2,1)}, u32[]{:S(2)}, u32[]{:S(2)}) async-start(bf16[128,264,256]{2,1,0:T(8,128)(2,1)} %shard_map.115), calls=%async_computation.2 | async-start | bytes 34603008 | tf_op jit(solution)/shard_map/all_to_all | solution.py:227

commit v12 on v11

--- a/solution.py
+++ b/solution.py
@@ -94,7 +94,7 @@
     )(hs, ho, ns, no, lh, ln, x, ltiles, init)
 
 
-SEND_GROUP = 32
+SEND_GROUP = 64
 
 
 def _send_kernel(picked_ref, spair_ref, sused_ref, rhome_ref, x_ref, rt_ref, *rest):

time: 608 us -> 609 us (level)
  no operation moved by 1% of the time
where the time goes in v12:
time: 609 us; the launch traced here: 605 us
  waiting for transfers between devices  409 us (67%)
  Pallas kernels  86.3 us (14%)
  blocking collectives  35.5 us (6%)
  starting transfers between devices  34.3 us (6%)
  other arithmetic  20.9 us (3%)
  local copies, waits for them, and re-layouts  11.1 us (2%)
  matrix products  7.57 us (1%)
    all_to_all x2, waiting for transfers between devices, apply_graph(): lax.all_to_all(send, SLOT_AXES, split_axis=0, concat_axis=0, tiled=True)  405 us
    pallas_call x2, Pallas kernels, local_sum(): pl.pallas_call(_local_kernel, out_shape=jax.ShapeDtypeStruct(init.shape,...  36.1 us
    all_to_all x1, blocking collectives, body(): lax.all_to_all(spread_out, AXES, split_axis=0, concat_axis=0, tiled=True)  35.5 us
    pallas_call x2, Pallas kernels, post_sum(): pl.pallas_call(_post_kernel, out_shape=jax.ShapeDtypeStruct(base.shape, o...  32 us
    all_to_all x2, starting transfers between devices, apply_graph(): lax.all_to_all(send, SLOT_AXES, split_axis=0, concat_axis=0, tiled=True)  23.9 us
    pallas_call x2, Pallas kernels, build_send(): pl.pallas_call(_send_kernel, grid=(slots // group,), out_shape=jax.ShapeD...  18.2 us
  transfers between devices with their start and end apart: 3, of which 3 were waited for; matrix products, arithmetic and copies ran while one was open for 4% of the time, Pallas kernels for 6%

profile of v12, /device:TPU:41, one launch (start us, length us, event | category | flops | bytes accessed | tf_op | source)
XLA Modules:
  0.0 605.4 jit_solution(11260151216461454035)
XLA Ops:
  0.6 1.2 compare_select_fusion
  1.8 0.8 scatter_custom_fusion
  2.6 0.7 copy.32
  3.4 10.5 %all-to-all-start = ((s32[128,1,1]{2,1,0:T(1,128)}), s32[128,1,1]{2,1,0:T(1,128)S(1)}, u32[]{:S(2)}, u32[]{:S(2)}) async-start(s32[128,1,1]{2,1,0:T(1,128)} %copy.32), calls=%async_computation | async-start | bytes 131072 | tf_op jit(solution)/shard_map/all_to_all | solution.py:207
  13.8 1.2 broadcast_clamp_fusion.2.rhome_ref
  15.0 1.3 scatter_custom_fusion.1.spair_ref
  16.3 1.3 scatter_custom_fusion.2.sused_ref
  17.6 3.7 all-to-all-done
  21.3 2.4 clamp_reduce_fusion
  23.6 1.8 gather_fusion.1
  25.5 8.9 %shard_map.112 = bf16[128,256,256]{2,1,0:T(8,128)(2,1)} custom-call(s32[128]{0:T(128)} %gather_fusion.1, s32[128]{0:T(128)} %scatter_custom_fusion.1.spair_ref, s32[128]{0:T(128)} %scatter_custom_fusion.2.sused_ref, s32[64]{0:T(128)} %broadcast_clamp_fusion.2.rhome_ref, bf16[16,128,256]{2,1,0:T(8,128)(2,1)} %bitcast.23, bf16[64,128,128]{2,1,0:T(8,128)(2,1)} %rt_ref.7), custom_call_target="tpu_custom_call" | custom-call | flops 1073741824 | bytes 19922944 | tf_op jit(solution)/shard_map/pallas_call | solution.py:132
  34.4 7.7 %all-to-all-start.1 = ((bf16[128,256,256]{2,1,0:T(8,128)(2,1)}), bf16[128,256,256]{2,1,0:T(8,128)(2,1)}, u32[]{:S(2)}, u32[]{:S(2)}) async-start(bf16[128,256,256]{2,1,0:T(8,128)(2,1)} %shard_map.112), calls=%async_computation.1 | async-start | bytes 33554432 | tf_op jit(solution)/shard_map/all_to_all | solution.py:227
  42.1 2.0 sort.62
  44.2 2.1 sort.64
  46.3 0.1 convert_reduce_fusion.1
  46.6 0.1 reduce.4
  46.7 2.1 sort.65
  48.8 0.1 convert_reduce_fusion
  49.0 0.1 reduce.5
  49.2 0.1 convert_reduce_fusion.3
  49.4 0.1 reduce
  49.5 0.7 pad_add_fusion
  50.2 1.5 broadcast_in_dim.18.init_ref
  51.7 18.0 %shard_map.113.base_ref = f32[16,128,256]{2,1,0:T(8,128)} custom-call(s32[17]{0:T(128)} %get-tuple-element.24.hs_ref, s32[64]{0:T(128)} %get-tuple-element.11.ho_ref, s32[17]{0:T(128)} %get-tuple-element.23.ns_ref, s32[64]{0:T(128)} %get-tuple-element.12.no_ref, s32[64]{0:T(128)} %copy-done.4, s32[64]{0:T(128)} %copy-done.5, bf16[16,128,256]{2,1,0:T(8,128)(2,1)} %bitcast.24, ...), custom_call_target="tpu_custom_call" | custom-call | flops 1073741824 | bytes 7340032 | tf_op jit(solution)/shard_map/pallas_call | solution.py:87
  69.8 2.4 compare_reduce_fusion
  72.1 1.2 gather_fusion
  73.4 2.6 sort.63
  76.2 0.1 reduce.3
  76.3 0.6 pad_add_fusion.2
  76.9 194.2 %all-to-all-done.1.recv_ref = bf16[128,256,256]{2,1,0:T(8,128)(2,1)} async-done(((bf16[128,256,256]{2,1,0:T(8,128)(2,1)}), bf16[128,256,256]{2,1,0:T(8,128)(2,1)}, u32[]{:S(2)}, u32[]{:S(2)}) %all-to-all-start.1) | async-done | bytes 16777248 | tf_op jit(solution)/shard_map/all_to_all | solution.py:227
  271.1 15.8 %shard_map.114 = bf16[16,128,256]{2,1,0:T(8,128)(2,1)} custom-call(s32[17]{0:T(128)} %get-tuple-element.26.rs_ref, s32[64]{0:T(128)} %get-tuple-element.9.ro_ref, s32[64]{0:T(128)} %get-tuple-element.16.td_ref, s32[17]{0:T(128)} %get-tuple-element.25.ss_ref, s32[128]{0:T(128)} %get-tuple-element.10.so_ref, bf16[64,128,128]{2,1,0:T(8,128)(2,1)} %rt_ref.7, ...), custom_call_target="tpu_custom_call" | custom-call | flops 536870912 | bytes 23068672 | tf_op jit(solution)/shard_map/pallas_call | solution.py:176
  286.9 3.6 multiply_convert_fusion
  290.5 0.7 fusion
  291.2 1.5 convolution_convert_fusion
  292.7 0.1 reshape.218
  292.9 0.9 gather_fusion.2
  293.8 0.2 reduce-precision_convert_fusion
  293.9 1.1 pad_maximum_fusion.3.rest_0_
  295.0 9.2 %shard_map.115 = bf16[128,264,256]{2,1,0:T(8,128)(2,1)} custom-call(s32[128]{0:T(128)} %gather_fusion.1, s32[128]{0:T(128)} %scatter_custom_fusion.1.spair_ref, s32[128]{0:T(128)} %scatter_custom_fusion.2.sused_ref, s32[64]{0:T(128)} %broadcast_clamp_fusion.2.rhome_ref, bf16[16,128,256]{2,1,0:T(8,128)(2,1)} %bitcast.19, bf16[64,128,128]{2,1,0:T(8,128)(2,1)} %rt_ref.7, ...), custom_call_target="tpu_custom_call" | custom-call | flops 1073741824 | bytes 20447232 | tf_op jit(solution)/shard_map/pallas_call | solution.py:132
  304.2 16.2 %all-to-all-start.2 = ((bf16[128,264,256]{2,1,0:T(8,128)(2,1)}), bf16[128,264,256]{2,1,0:T(8,128)(2,1)}, u32[]{:S(2)}, u32[]{:S(2)}) async-start(bf16[128,264,256]{2,1,0:T(8,128)(2,1)} %shard_map.115), calls=%async_computation.2 | async-start | bytes 34603008 | tf_op jit(solution)/shard_map/all_to_all | solution.py:227
  320.4 1.8 fusion.4
  322.2 18.0 %shard_map.116.base_ref = f32[16,128,256]{2,1,0:T(8,128)} custom-call(s32[17]{0:T(128)} %get-tuple-element.24.hs_ref, s32[64]{0:T(128)} %get-tuple-element.11.ho_ref, s32[17]{0:T(128)} %get-tuple-element.23.ns_ref, s32[64]{0:T(128)} %get-tuple-element.12.no_ref, s32[64]{0:T(128)} %copy-done.4, s32[64]{0:T(128)} %copy-done.5, bf16[16,128,256]{2,1,0:T(8,128)(2,1)} %bitcast.20, ...), custom_call_target="tpu_custom_call" | custom-call | flops 1073741824 | bytes 7340032 | tf_op jit(solution)/shard_map/pallas_call | solution.py:87
  340.2 211.0 %all-to-all-done.2.recv_ref = bf16[128,264,256]{2,1,0:T(8,128)(2,1)} async-done(((bf16[128,264,256]{2,1,0:T(8,128)(2,1)}), bf16[128,264,256]{2,1,0:T(8,128)(2,1)}, u32[]{:S(2)}, u32[]{:S(2)}) %all-to-all-start.2) | async-done | bytes 17301536 | tf_op jit(solution)/shard_map/all_to_all | solution.py:227
  551.2 1.1 slice_convert_fusion
  552.3 0.2 fusion.3
  552.5 16.2 %shard_map.117 = f32[16,128,256]{2,1,0:T(8,128)} custom-call(s32[17]{0:T(128)} %get-tuple-element.26.rs_ref, s32[64]{0:T(128)} %get-tuple-element.9.ro_ref, s32[64]{0:T(128)} %get-tuple-element.16.td_ref, s32[17]{0:T(128)} %get-tuple-element.25.ss_ref, s32[128]{0:T(128)} %get-tuple-element.10.so_ref, ...), custom_call_target="tpu_custom_call", output_to_operand_aliasing={{}: (7, {})} | custom-call | flops 536870912 | bytes 23592960 | tf_op jit(solution)/shard_map/pallas_call | solution.py:176
  568.8 35.5 %all_to_all.24 = f32[128,4,256]{2,1,0:T(4,128)S(1)} all-to-all(f32[128,4,256]{2,1,0:T(4,128)S(1)} %broadcast_in_dim.19), channel_id=1, replica_groups=mesh['group'=2,'member'=64] {'group','member'}, dimensions={0} | all-to-all | bytes 1048576 | tf_op jit(solution)/shard_map/all_to_all | solution.py:260
  604.5 1.0 mul.54
  (41 shorter events, 0.9 us)
Async XLA Ops:
  3.4 17.9 %all-to-all-start = ((s32[128,1,1]{2,1,0:T(1,128)}), s32[128,1,1]{2,1,0:T(1,128)S(1)}, u32[]{:S(2)}, u32[]{:S(2)}) async-start(s32[128,1,1]{2,1,0:T(1,128)} %copy.32), calls=%async_computation | async-start | bytes 131072 | tf_op jit(solution)/shard_map/all_to_all | solution.py:207
  34.4 7.7 %copy-start.3 = (s32[64]{0:T(128)S(1)}, s32[64]{0:T(128)}, u32[]{:S(2)}) copy-start(s32[64]{0:T(128)} %broadcast_clamp_fusion.2.rhome_ref) | copy-start | bytes 772
  34.4 9.8 %copy-start.7 = (s32[64]{0:T(128)S(1)}, s32[64]{0:T(128)}, u32[]{:S(2)}) copy-start(s32[64]{0:T(128)} %param.10) | copy-start | bytes 772
  34.4 12.3 %copy-start.8 = (s32[64]{0:T(128)S(1)}, s32[64]{0:T(128)}, u32[]{:S(2)}) copy-start(s32[64]{0:T(128)} %param.11) | copy-start | bytes 772
  34.4 236.7 %all-to-all-start.1 = ((bf16[128,256,256]{2,1,0:T(8,128)(2,1)}), bf16[128,256,256]{2,1,0:T(8,128)(2,1)}, u32[]{:S(2)}, u32[]{:S(2)}) async-start(bf16[128,256,256]{2,1,0:T(8,128)(2,1)} %shard_map.112), calls=%async_computation.1 | async-start | bytes 33554432 | tf_op jit(solution)/shard_map/all_to_all | solution.py:227
  44.2 7.5 %copy-start.4 = (s32[64]{0:T(128)}, s32[64]{0:T(128)S(1)}, u32[]{:S(2)}) copy-start(s32[64]{0:T(128)S(1)} %broadcast_clamp_fusion.1.lh_ref) | copy-start | bytes 772
  46.7 5.0 copy-start.5
  271.1 15.8 %copy-start = (bf16[2048,256]{1,0:T(8,128)(2,1)S(1)}, bf16[2048,256]{1,0:T(8,128)(2,1)}, u32[]{:S(2)}) copy-start(bf16[2048,256]{1,0:T(8,128)(2,1)} %param.9) | copy-start | bytes 3145732
  271.1 15.8 %copy-start.2 = (bf16[512,256]{1,0:T(8,128)(2,1)S(1)}, bf16[512,256]{1,0:T(8,128)(2,1)}, u32[]{:S(2)}) copy-start(bf16[512,256]{1,0:T(8,128)(2,1)} %param.16) | copy-start | bytes 786436
  271.1 15.8 %copy-start.6 = (bf16[2048,256]{1,0:T(8,128)(2,1)S(1)}, bf16[2048,256]{1,0:T(8,128)(2,1)}, u32[]{:S(2)}) copy-start(bf16[2048,256]{1,0:T(8,128)(2,1)} %param.17) | copy-start | bytes 3145732
  286.9 3.6 copy-start.1
  304.2 247.0 %all-to-all-start.2 = ((bf16[128,264,256]{2,1,0:T(8,128)(2,1)}), bf16[128,264,256]{2,1,0:T(8,128)(2,1)}, u32[]{:S(2)}, u32[]{:S(2)}) async-start(bf16[128,264,256]{2,1,0:T(8,128)(2,1)} %shard_map.115), calls=%async_computation.2 | async-start | bytes 34603008 | tf_op jit(solution)/shard_map/all_to_all | solution.py:227
